TPU v7x, 32 devices: a whole 2x2x4 slice. The times are simulated.
32 devices in a mesh: group: 4 (over z), member: 8 (over y, x, core).
Axes of the slice: x: 2, y: 2, z: 4, core: 2. Of those that a mesh axis runs over, the one named last changes fastest.
Arguments:
- query_feat: bfloat16 [4096, 4096], P(('group', 'member'))
- code_feat: bfloat16 [4096, 4096], P(('group', 'member'))
- projection: bfloat16 [4096, 1024], replicated
- hard_ids: int32 [32, 16], P(('group', 'member')), may hold values from 0 to 63, as said below
- loss_weight: float32 [4096], P(('group', 'member')), may hold values from 1 to 4
Outputs:
- query_grad: bfloat16 [4096, 4096], P(('group', 'member'))
- code_grad: bfloat16 [4096, 4096], P(('group', 'member'))
- projection_grad: float32 [4096, 1024], P(('group', 'member'))
Inputs may be any that keep to these rules, and one draw needn't show every extreme that they name: `hard_ids`: entry (owner device g * 8 + m) * 2 + slot names code rows of that device. A row names 16 different blocks, none of its own group; at most 8 of them lie in one group, and exactly 8 in some group of every row.
All inputs are finite; a program needn't handle non-finite values.
Results may differ from a plain program's by a relative error of at most 0.02.
Values may be sent and summed in bfloat16 or wider, within the bound.
No kernel may reach another device: no remote copies, remote signals or barrier semaphores. Data moves between devices by JAX's collectives and lax.ppermute only.
A program may use at most 128 MiB of HBM per device.

v0:
```python
import jax
import jax.numpy as jnp
from jax import lax
from jax.sharding import PartitionSpec as P

CB = 64


inverse_temp = 120.0
epsilon = 1e-06


def embed(features, projection):
    values = jnp.dot(features, projection, preferred_element_type=jnp.float32)
    inverse = lax.rsqrt(jnp.sum(values * values, axis=1) + epsilon)
    unit_vec = values * inverse[:, None]
    return (unit_vec, inverse, unit_vec.astype(jnp.bfloat16))


def norm_back(upstream, unit_vec, inverse):
    inner_prod = jnp.sum(unit_vec * upstream, axis=1, keepdims=True)
    return (inverse[:, None] * (upstream - unit_vec * inner_prod)).astype(jnp.bfloat16)


def body(query_feat, code_feat, projection, hard_ids, loss_weight):
    groups = lax.axis_size("group")
    members = lax.axis_size("member")
    member_index = lax.axis_index("member")
    queries_dev = query_feat.shape[0]
    emb_width = projection.shape[1]
    count_hard = hard_ids.shape[1]
    slot_count = queries_dev // CB
    per_group = members * slot_count
    capacity = 2 * count_hard // groups
    q_unit, q_inv, q_emb = embed(query_feat, projection)
    c_unit, c_inv, c_emb = embed(code_feat, projection)
    group_codes = lax.all_gather(c_emb, "member", axis=0, tiled=True)
    code_blocks = group_codes.reshape(per_group, CB, emb_width)
    wanted = hard_ids[0]
    owner_group = wanted // per_group
    local_block = wanted % per_group
    request_order = jnp.arange(count_hard, dtype=jnp.int32)
    same_group = (owner_group[:, None] == owner_group[None, :]) & (
        request_order[None, :] < request_order[:, None]
    )
    slot_place = jnp.sum(same_group.astype(jnp.int32), axis=1)
    pick_group = (owner_group[:, None] == jnp.arange(groups, dtype=jnp.int32)[None, :]).astype(
        jnp.int32
    )
    pick_place = (slot_place[:, None] == jnp.arange(capacity, dtype=jnp.int32)[None, :]).astype(
        jnp.int32
    )
    request_table = (
        jnp.sum(
            pick_group[:, :, None] * (pick_place * (local_block + 1)[:, None])[:, None, :], axis=0
        )
        - 1
    )
    asked_blocks = lax.all_to_all(request_table, "group", split_axis=0, concat_axis=0, tiled=True)
    asked_valid = asked_blocks >= 0
    picked = (
        code_blocks[jnp.clip(asked_blocks, 0, per_group - 1)]
        * asked_valid.astype(jnp.bfloat16)[:, :, None, None]
    )
    group_scores = inverse_temp * jnp.einsum(
        "qe,ke->qk", q_emb, group_codes, preferred_element_type=jnp.float32
    )
    offsets = jnp.arange(queries_dev, dtype=jnp.int32)
    columns = jnp.arange(members * queries_dev, dtype=jnp.int32)
    positive = (columns[None, :] == (member_index * queries_dev + offsets)[:, None]).astype(
        jnp.float32
    )
    factor = loss_weight * inverse_temp
    fetched = lax.all_to_all(picked, "group", split_axis=0, concat_axis=0, tiled=True).reshape(
        groups * capacity * CB, emb_width
    )
    table_valid = jnp.broadcast_to(
        (request_table >= 0)[:, :, None], (groups, capacity, CB)
    ).reshape(-1)
    hard_scores = jnp.where(
        table_valid[None, :],
        inverse_temp * jnp.einsum("qe,ke->qk", q_emb, fetched, preferred_element_type=jnp.float32),
        -jnp.inf,
    )
    row_max = jnp.maximum(jnp.max(group_scores, axis=1), jnp.max(hard_scores, axis=1))
    row_sum = jnp.sum(jnp.exp(group_scores - row_max[:, None]), axis=1) + jnp.sum(
        jnp.exp(hard_scores - row_max[:, None]), axis=1
    )
    log_total = row_max + jnp.log(row_sum)
    grad_hard = (factor[:, None] * jnp.exp(hard_scores - log_total[:, None])).astype(jnp.bfloat16)
    hard_delta = jnp.einsum("qk,ke->qe", grad_hard, fetched, preferred_element_type=jnp.float32)
    outgoing = jnp.einsum("qk,qe->ke", grad_hard, q_emb, preferred_element_type=jnp.float32).astype(
        jnp.bfloat16
    )
    returned = lax.all_to_all(
        outgoing.reshape(groups, capacity, CB, emb_width),
        "group",
        split_axis=0,
        concat_axis=0,
        tiled=True,
    )
    grad_group = (factor[:, None] * (jnp.exp(group_scores - log_total[:, None]) - positive)).astype(
        jnp.bfloat16
    )
    query_delta = (
        jnp.einsum("qk,ke->qe", grad_group, group_codes, preferred_element_type=jnp.float32)
        + hard_delta
    )
    hit_table = (
        asked_blocks.reshape(-1)[:, None] == jnp.arange(per_group, dtype=jnp.int32)[None, :]
    ).astype(jnp.bfloat16)
    hard_sum = jnp.einsum(
        "rj,rx->jx",
        hit_table,
        returned.reshape(groups * capacity, CB * emb_width),
        preferred_element_type=jnp.float32,
    )
    code_terms = jnp.einsum(
        "qk,qe->ke", grad_group, q_emb, preferred_element_type=jnp.float32
    ) + hard_sum.reshape(members * queries_dev, emb_width)
    code_delta = lax.psum_scatter(
        code_terms.astype(jnp.bfloat16), "member", scatter_dimension=0, tiled=True
    ).astype(jnp.float32)
    dz_query = norm_back(query_delta, q_unit, q_inv)
    dz_code = norm_back(code_delta, c_unit, c_inv)
    query_grad = jnp.einsum(
        "qe,de->qd", dz_query, projection, preferred_element_type=jnp.float32
    ).astype(jnp.bfloat16)
    code_grad = jnp.einsum(
        "qe,de->qd", dz_code, projection, preferred_element_type=jnp.float32
    ).astype(jnp.bfloat16)
    projection_grad = lax.psum_scatter(
        jnp.einsum("qd,qe->de", query_feat, dz_query, preferred_element_type=jnp.float32)
        + jnp.einsum("qd,qe->de", code_feat, dz_code, preferred_element_type=jnp.float32),
        ("group", "member"),
        scatter_dimension=0,
        tiled=True,
    )
    return (query_grad, code_grad, projection_grad)


def solution(mesh):
    return jax.shard_map(
        body,
        mesh=mesh,
        in_specs=(
            P(("group", "member"), None),
            P(("group", "member"), None),
            P(),
            P(("group", "member"), None),
            P(("group", "member")),
        ),
        out_specs=(
            P(("group", "member"), None),
            P(("group", "member"), None),
            P(("group", "member"), None),
        ),
        check_vma=False,
    )
```

profile of v0, /device:TPU:3, one launch (start us, length us, event | category | flops | bytes accessed | tf_op | source)
XLA Modules:
  0.0 518.9 jit_solution(848729848182131653)
XLA Ops:
  7.2 5.1 multiply_reduce_fusion.1
  14.4 8.8 %all_to_all.16 = s32[4,1,8]{2,1,0:T(1,128)S(1)} all-to-all(s32[4,1,8]{2,1,0:T(1,128)S(1)} %bitcast.61), channel_id=1, replica_groups=mesh['group'=4,'member'=8] {'group'}, dimensions={0} | all-to-all | bytes 256 | tf_op jit(solution)/shard_map/all_to_all | solution.py:59
  24.5 19.0 %all-gather.2.cloned.1.call-done = bf16[1024,1024]{1,0:T(8,128)(2,1)} async-done(((bf16[128,1024]{1,0:T(8,128)(2,1)}), bf16[1024,1024]{1,0:T(8,128)(2,1)}) %all-gather.2.cloned.1.call-update) | async-done | bytes 2097168 | tf_op jit(solution)/shard_map/all_gather | solution.py:37
  43.5 4.3 gather_fusion
  47.9 4.5 broadcast_multiply_fusion
  52.4 4.9 all-to-all-start.1
  57.4 4.9 multiply_reduce_fusion.2
  64.8 85.4 %all-to-all-done.1 = bf16[4,8,64,1024]{3,2,1,0:T(8,128)(2,1)} async-done(((bf16[4,8,64,1024]{3,2,1,0:T(8,128)(2,1)}), bf16[4,8,64,1024]{3,2,1,0:T(8,128)(2,1)}, u32[]{:S(2)}, u32[]{:S(2)}) %all-to-all-start.1) | async-done | bytes 4194336 | tf_op jit(solution)/shard_map/all_to_all | solution.py:74
  150.2 3.8 fusion.14
  155.1 3.4 convolution_convert_fusion.2
  158.4 4.8 all-to-all-start.2
  163.6 92.4 %all-to-all-done.2 = bf16[4,8,64,1024]{3,2,1,0:T(8,128)(2,1)} async-done(((bf16[4,8,64,1024]{3,2,1,0:T(8,128)(2,1)}), bf16[4,8,64,1024]{3,2,1,0:T(8,128)(2,1)}, u32[]{:S(2)}, u32[]{:S(2)}) %all-to-all-start.2) | async-done | bytes 4194336 | tf_op jit(solution)/shard_map/all_to_all | solution.py:95
  256.0 4.5 copy.16
  260.5 2.8 fusion.4
  263.3 3.9 reshape.206
  267.3 4.6 add_convert_fusion
  273.5 3.6 multiply_reduce_fusion
  277.3 8.5 %fusion.15 = f32[1024,4096]{1,0:T(8,128)} fusion(bf16[128,1024]{1,0:T(8,128)(2,1)S(1)} %multiply_convert_fusion.1, bf16[128,4096]{1,0:T(8,128)(2,1)S(1)} %copy-done), kind=kOutput, calls=%fused_computation.66 | convolution fusion | flops 1073741824 | bytes 18087936 | tf_op jit(solution)/shard_map/qd,qe->de/dot_general | solution.py:133
  285.8 26.0 %reduce-scatter.3.cloned.1.call-done = bf16[128,1024]{1,0:T(8,128)(2,1)} async-done(((bf16[1024,1024]{1,0:T(8,128)(2,1)}), bf16[128,1024]{1,0:T(8,128)(2,1)}) %reduce-scatter.3.cloned.1.call-update) | async-done | bytes 262160 | tf_op jit(solution)/shard_map/reduce_scatter | solution.py:121
  314.2 13.9 %add_bitcast_fusion = f32[4096,1024]{0,1:T(8,128)} fusion(f32[1024,4096]{1,0:T(8,128)} %fusion.15, bf16[128,1024]{1,0:T(8,128)(2,1)S(1)} %fusion.3, bf16[128,4096]{1,0:T(8,128)(2,1)S(1)} %copy-done.9), kind=kOutput, calls=%fused_computation.1 | convolution fusion | flops 1077936128 | bytes 34865152 | tf_op jit(solution)/shard_map/qd,qe->de/dot_general | solution.py:134
  328.1 7.3 %convolution_convert_fusion.1 = bf16[128,4096]{1,0:T(8,128)(2,1)} fusion(bf16[128,1024]{1,0:T(8,128)(2,1)S(1)} %multiply_convert_fusion.1, bf16[4096,1024]{1,0:T(8,128)(2,1)} %param.7), kind=kOutput, calls=%fused_computation.3 | convolution fusion | flops 1074266112 | bytes 9699328 | tf_op jit(solution)/shard_map/qe,de->qd/dot_general | solution.py:126
  335.4 7.3 %convolution_convert_fusion = bf16[128,4096]{1,0:T(8,128)(2,1)} fusion(bf16[128,1024]{1,0:T(8,128)(2,1)S(1)} %fusion.3, bf16[4096,1024]{1,0:T(8,128)(2,1)} %param.7), kind=kOutput, calls=%fused_computation.2 | convolution fusion | flops 1074266112 | bytes 9699328 | tf_op jit(solution)/shard_map/qe,de->qd/dot_general | solution.py:129
  342.6 167.7 %reduce-scatter.5.cloned.1.call-done = f32[128,1024]{0,1:T(8,128)} async-done(((f32[4096,1024]{0,1:T(8,128)}), f32[128,1024]{0,1:T(8,128)}) %reduce-scatter.5.cloned.1.call-update) | async-done | bytes 524304 | tf_op jit(solution)/shard_map/reduce_scatter | solution.py:132
  510.3 2.0 copy.14
  (62 shorter events, 11.3 us)
Async XLA Ops:
  7.2 50.2 %copy-start = (bf16[128,4096]{1,0:T(8,128)(2,1)S(1)}, bf16[128,4096]{1,0:T(8,128)(2,1)}, u32[]{:S(2)}) copy-start(bf16[128,4096]{1,0:T(8,128)(2,1)} %param.5) | copy-start | bytes 3145732
  7.2 6.8 %copy-start.11 = (s32[1,16]{1,0:T(1,128)S(1)}, s32[1,16]{1,0:T(1,128)}, u32[]{:S(2)}) copy-start(s32[1,16]{1,0:T(1,128)} %param.8) | copy-start | bytes 196
  7.2 36.3 %all-gather.2.cloned.1.call-start = ((), (), s32[]{:S(2)}) async-start(), calls=%async_computation.5 | async-start | bytes 2359296 | tf_op jit(solution)/shard_map/all_gather | solution.py:37
  12.4 0.8 copy-start.4
  52.4 97.9 %all-to-all-start.1 = ((bf16[4,8,64,1024]{3,2,1,0:T(8,128)(2,1)}), bf16[4,8,64,1024]{3,2,1,0:T(8,128)(2,1)}, u32[]{:S(2)}, u32[]{:S(2)}) async-start(bf16[4,8,64,1024]{3,2,1,0:T(8,128)(2,1)} %broadcast_multiply_fusion), calls=%async_computation.1 | async-start | bytes 8388608 | tf_op jit(solution)/shard_map/all_to_all | solution.py:74
  57.4 4.9 copy-start.10
  57.4 5.8 %copy-start.2 = (bf16[1024,1024]{1,0:T(8,128)(2,1)S(1)}, bf16[1024,1024]{1,0:T(8,128)(2,1)}, u32[]{:S(2)}) copy-start(bf16[1024,1024]{1,0:T(8,128)(2,1)} %all-gather.2.cloned.1.call-done) | copy-start | bytes 6291460
  62.3 0.8 copy-start.6
  150.2 4.2 copy-start.8
  154.1 1.0 copy-start.3
  158.4 97.6 %all-to-all-start.2 = ((bf16[4,8,64,1024]{3,2,1,0:T(8,128)(2,1)}), bf16[4,8,64,1024]{3,2,1,0:T(8,128)(2,1)}, u32[]{:S(2)}, u32[]{:S(2)}) async-start(bf16[4,8,64,1024]{3,2,1,0:T(8,128)(2,1)} %bitcast.59), calls=%async_computation.2 | async-start | bytes 8388608 | tf_op jit(solution)/shard_map/all_to_all | solution.py:95
  163.3 148.6 %reduce-scatter.3.cloned.1.call-start = ((), (), s32[]{:S(2)}) async-start(), calls=%async_computation.6 | async-start | bytes 2359296 | tf_op jit(solution)/shard_map/reduce_scatter | solution.py:121
  271.9 238.4 %reduce-scatter.5.cloned.1.call-start = ((), (), s32[]{:S(2)}) async-start(), calls=%async_computation.7 | async-start | bytes 17301504 | tf_op jit(solution)/shard_map/reduce_scatter | solution.py:132
  273.5 3.6 copy-start.7
  277.3 34.6 %copy-start.5 = (f32[128,1024]{1,0:T(8,128)S(1)}, f32[128,1024]{1,0:T(8,128)}, u32[]{:S(2)}) copy-start(f32[128,1024]{1,0:T(8,128)} %copy-done.4) | copy-start | bytes 1572868
  277.3 36.9 %copy-start.9 = (bf16[128,4096]{1,0:T(8,128)(2,1)S(1)}, bf16[128,4096]{1,0:T(8,128)(2,1)}, u32[]{:S(2)}) copy-start(bf16[128,4096]{1,0:T(8,128)(2,1)} %param.6) | copy-start | bytes 3145732
  328.0 184.3 %copy-start.1 = (bf16[128,4096]{1,0:T(8,128)(2,1)S(1)}, bf16[128,4096]{1,0:T(8,128)(2,1)}, u32[]{:S(2)}) copy-start(bf16[128,4096]{1,0:T(8,128)(2,1)} %param.5) | copy-start | bytes 3145732
Sparse Core Ops, SparseCore 0:
  14.1 29.3 all-gather.1
  272.0 39.7 reduce-scatter.2
  328.2 182.1 reduce-scatter.4
where the time goes:
time: 522 us; the launch traced here: 519 us
  waiting for transfers between devices  391 us (75%)
  matrix products  68.3 us (13%)
  local copies, waits for them, and re-layouts  17.7 us (3%)
  between operations  14 us (3%)
  starting transfers between devices  10 us (2%)
  other arithmetic  9.44 us (2%)
  blocking collectives  8.81 us (2%)
    reduce_scatter x1, waiting for transfers between devices, body(): lax.psum_scatter(jnp.einsum('qd,qe->de', query_feat, dz_query, preferred_...  168 us
    all_to_all x1, waiting for transfers between devices, body(): lax.all_to_all(outgoing.reshape(groups, capacity, CB, emb_width), 'group'...  92.4 us
    all_to_all x1, waiting for transfers between devices, body(): lax.all_to_all(picked, 'group', split_axis=0, concat_axis=0, tiled=True)  85.4 us
    reduce_scatter x1, waiting for transfers between devices, body(): lax.psum_scatter(code_terms.astype(jnp.bfloat16), 'member', scatter_dimen...  26 us
    all_gather x1, waiting for transfers between devices, body(): group_codes = lax.all_gather(c_emb, 'member', axis=0, tiled=True)  19 us
    dot_general x1, matrix products, body(): jnp.einsum('qd,qe->de', code_feat, dz_code, preferred_element_type=jnp.fl...  13.9 us
  transfers between devices with their start and end apart: 5, of which 5 were waited for; matrix products, arithmetic and copies ran while one was open for 7% of the time, Pallas kernels for 0%

commit v1 on v0

v1 whole, which is shorter than its diff:
```python
import jax
import jax.numpy as jnp
from jax import lax
from jax.sharding import PartitionSpec as P

CB = 64


inverse_temp = 120.0
epsilon = 1e-06


def embed(features, projection):
    values = jnp.dot(features, projection, preferred_element_type=jnp.float32)
    inverse = lax.rsqrt(jnp.sum(values * values, axis=1) + epsilon)
    unit_vec = values * inverse[:, None]
    return (unit_vec, inverse, unit_vec.astype(jnp.bfloat16))


def norm_back(upstream, unit_vec, inverse):
    inner_prod = jnp.sum(unit_vec * upstream, axis=1, keepdims=True)
    return (inverse[:, None] * (upstream - unit_vec * inner_prod)).astype(jnp.bfloat16)


def body(query_feat, code_feat, projection, hard_ids, loss_weight):
    groups = lax.axis_size("group")
    members = lax.axis_size("member")
    group_index = lax.axis_index("group")
    member_index = lax.axis_index("member")
    queries_dev = query_feat.shape[0]
    feat_width = query_feat.shape[1]
    emb_width = projection.shape[1]
    slot_count = queries_dev // CB
    per_group = members * slot_count
    group_span = members * queries_dev
    rows_dev = feat_width // (groups * members)

    feats = jnp.stack([query_feat, code_feat], axis=0).reshape(
        2, queries_dev, groups, members, rows_dev
    )
    feats = jnp.transpose(feats, (3, 0, 1, 2, 4))
    feat_cols = lax.all_to_all(feats, "member", split_axis=0, concat_axis=0, tiled=True)

    q_unit, q_inv, q_emb = embed(query_feat, projection)
    c_unit, c_inv, c_emb = embed(code_feat, projection)
    group_codes = lax.all_gather(c_emb, "member", axis=0, tiled=True)
    q_all = lax.all_gather(q_emb, "group", axis=0)
    ids_all = lax.all_gather(hard_ids[0], "group", axis=0)
    w_all = lax.all_gather(loss_weight, "group", axis=0)

    block_ids = group_index * per_group + jnp.arange(per_group, dtype=jnp.int32)
    asked = jnp.any(ids_all[:, :, None] == block_ids[None, None, :], axis=1)
    own = jnp.arange(groups, dtype=jnp.int32) == group_index
    block_mask = asked | own[:, None]
    col_mask = jnp.broadcast_to(
        block_mask[:, :, None], (groups, per_group, CB)
    ).reshape(groups, 1, group_span)

    scores = inverse_temp * jnp.einsum(
        "gqe,ke->gqk", q_all, group_codes, preferred_element_type=jnp.float32
    )
    scores = jnp.where(col_mask, scores, -jnp.inf)
    part_max = jnp.max(scores, axis=2)
    safe_max = jnp.where(part_max > -jnp.inf, part_max, 0.0)
    part_sum = jnp.sum(jnp.exp(scores - safe_max[:, :, None]), axis=2)
    stats = lax.all_gather(jnp.stack([part_max, part_sum], axis=0), "group", axis=0)
    row_max = jnp.max(stats[:, 0], axis=0)
    row_sum = jnp.sum(stats[:, 1] * jnp.exp(stats[:, 0] - row_max[None]), axis=0)
    log_total = row_max + jnp.log(row_sum)

    offsets = jnp.arange(queries_dev, dtype=jnp.int32)
    columns = jnp.arange(group_span, dtype=jnp.int32)
    positive = (columns[None, :] == (member_index * queries_dev + offsets)[:, None]).astype(
        jnp.float32
    )
    positive = positive[None] * own[:, None, None].astype(jnp.float32)
    factor = w_all * inverse_temp
    grad = (
        factor[:, :, None] * (jnp.exp(scores - log_total[:, :, None]) - positive)
    ).astype(jnp.bfloat16)

    delta_parts = jnp.einsum("gqk,ke->gqe", grad, group_codes, preferred_element_type=jnp.float32)
    query_delta = lax.psum_scatter(delta_parts, "group", scatter_dimension=0, tiled=True).reshape(
        queries_dev, emb_width
    )

    code_terms = None
    for g in range(groups):
        term = jnp.dot(grad[g].T, q_all[g], preferred_element_type=jnp.float32)
        term = jnp.where(g == group_index, term, term.astype(jnp.bfloat16).astype(jnp.float32))
        code_terms = term if code_terms is None else code_terms + term
    code_delta = lax.psum_scatter(
        code_terms.astype(jnp.bfloat16), "member", scatter_dimension=0, tiled=True
    ).astype(jnp.float32)

    dz_query = norm_back(query_delta, q_unit, q_inv)
    dz_code = norm_back(code_delta, c_unit, c_inv)
    query_grad = jnp.einsum(
        "qe,de->qd", dz_query, projection, preferred_element_type=jnp.float32
    ).astype(jnp.bfloat16)
    code_grad = jnp.einsum(
        "qe,de->qd", dz_code, projection, preferred_element_type=jnp.float32
    ).astype(jnp.bfloat16)

    dz_all = lax.all_gather(jnp.stack([dz_query, dz_code], axis=0), "member", axis=0)
    proj_parts = jnp.einsum(
        "mtqgr,mtqe->gre", feat_cols, dz_all, preferred_element_type=jnp.float32
    )
    projection_grad = lax.psum_scatter(
        proj_parts, "group", scatter_dimension=0, tiled=True
    ).reshape(rows_dev, emb_width)
    return (query_grad, code_grad, projection_grad)


def solution(mesh):
    return jax.shard_map(
        body,
        mesh=mesh,
        in_specs=(
            P(("group", "member"), None),
            P(("group", "member"), None),
            P(),
            P(("group", "member"), None),
            P(("group", "member")),
        ),
        out_specs=(
            P(("group", "member"), None),
            P(("group", "member"), None),
            P(("group", "member"), None),
        ),
        check_vma=False,
    )
```

time: 522 us -> 292 us (0.56)
  waiting for transfers between devices: 391 us -> 159 us
  blocking collectives: 8.81 us -> 61.8 us
  matrix products: 68.3 us -> 42.8 us
  local copies, waits for them, and re-layouts: 17.7 us -> 2.08 us
  starting transfers between devices: 10 us -> 0.25 us
    all_to_all x2 -> x0, waiting for transfers between devices: 178 us -> none  [the longest x1 92.4 us: body(): lax.all_to_all(outgoing.reshape(groups, capacity, CB, emb_width), 'group'...]
    reduce_scatter x1 -> x2, waiting for transfers between devices: 168 us -> 70 us  [the longest x1 43.3 us: body(): lax.psum_scatter(delta_parts, 'group', scatter_dimension=0, tiled=True)]
    all_to_all x1, blocking collectives: 8.81 us -> 35.8 us  [body(): lax.all_to_all(feats, 'member', split_axis=0, concat_axis=0, tiled=True)]
    all_gather x0 -> x3, blocking collectives: none -> 26 us  [the longest x1 10.5 us: body(): lax.all_gather(jnp.stack([part_max, part_sum], axis=0), 'group', axis=0)]
    dot_general x9 -> x7, matrix products: 43.7 us -> 18.5 us  [the longest x1 6.5 us: body(): jnp.einsum('mtqgr,mtqe->gre', feat_cols, dz_all, preferred_element_type=j...]
    all_gather x0 -> x2, waiting for transfers between devices: none -> 18.7 us  [the longest x1 12.7 us: body(): lax.all_gather(jnp.stack([dz_query, dz_code], axis=0), 'member', axis=0)]
    reduce_scatter x1, waiting for transfers between devices: 26 us -> 39.3 us  [body(): lax.psum_scatter(code_terms.astype(jnp.bfloat16), 'member', scatter_dimen...]
    all_gather x1, waiting for transfers between devices: 19 us -> 30.5 us  [body(): group_codes = lax.all_gather(c_emb, 'member', axis=0, tiled=True)]
  transfers between devices with their start and end apart: 5 -> 6, of which waited for: 5 -> 6; matrix products, arithmetic and copies ran while one was open for 7% -> 10% of each run, Pallas kernels for 0% -> 0%
where the time goes in v1:
time: 292 us; the launch traced here: 290 us
  waiting for transfers between devices  159 us (54%)
  blocking collectives  61.8 us (21%)
  matrix products  42.8 us (15%)
  between operations  14.3 us (5%)
  other arithmetic  9.62 us (3%)
    reduce_scatter x1, waiting for transfers between devices, body(): lax.psum_scatter(delta_parts, 'group', scatter_dimension=0, tiled=True)  43.3 us
    reduce_scatter x1, waiting for transfers between devices, body(): lax.psum_scatter(code_terms.astype(jnp.bfloat16), 'member', scatter_dimen...  39.3 us
    all_to_all x1, blocking collectives, body(): lax.all_to_all(feats, 'member', split_axis=0, concat_axis=0, tiled=True)  35.8 us
    all_gather x1, waiting for transfers between devices, body(): group_codes = lax.all_gather(c_emb, 'member', axis=0, tiled=True)  30.5 us
    reduce_scatter x1, waiting for transfers between devices, body(): lax.psum_scatter(proj_parts, 'group', scatter_dimension=0, tiled=True)  26.7 us
    all_gather x1, waiting for transfers between devices, body(): lax.all_gather(jnp.stack([dz_query, dz_code], axis=0), 'member', axis=0)  12.7 us
    all_gather x1, blocking collectives, body(): lax.all_gather(jnp.stack([part_max, part_sum], axis=0), 'group', axis=0)  10.5 us
    dot_general x2, matrix products, embed(): values = jnp.dot(features, projection, preferred_element_type=jnp.float32)  9.77 us
  transfers between devices with their start and end apart: 6, of which 6 were waited for; matrix products, arithmetic and copies ran while one was open for 10% of the time, Pallas kernels for 0%

profile of v1, /device:TPU:3, one launch (start us, length us, event | category | flops | bytes accessed | tf_op | source)
XLA Modules:
  0.0 289.5 jit_solution(1036864795923591170)
XLA Ops:
  7.2 5.1 %multiply_reduce_fusion.1 = (f32[128]{0:T(128)S(1)}, f32[128,1024]{1,0:T(8,128)S(1)}) fusion(bf16[128,4096]{1,0:T(8,128)(2,1)} %param.5, bf16[4096,1024]{1,0:T(8,128)(2,1)} %param.7), kind=kOutput, calls=%fused_computation.25 | convolution fusion | flops 1074003840 | bytes 9961984 | tf_op jit(solution)/shard_map/dot_general | solution.py:14
  13.6 4.7 %multiply_reduce_fusion = (f32[128]{0:T(128)S(1)}, f32[128,1024]{1,0:T(8,128)S(1)}) fusion(bf16[128,4096]{1,0:T(8,128)(2,1)S(1)} %copy-done, bf16[4096,1024]{1,0:T(8,128)(2,1)} %param.7), kind=kOutput, calls=%fused_computation.24 | convolution fusion | flops 1074003840 | bytes 9961984 | tf_op jit(solution)/shard_map/dot_general | solution.py:14
  19.2 9.3 %all-gather.5 = s32[4,1,16]{2,1,0:T(1,128)S(1)} all-gather(s32[1,1,16]{2,1,0:T(1,128)S(1)} %bitcast.92), channel_id=1, replica_groups=mesh['group'=4,'member'=8] {'group'}, dimensions={0}, use_global_device_ids=true | all-gather | bytes 320 | tf_op jit(solution)/shard_map/all_gather | solution.py:48
  28.9 6.2 %all-gather.4 = f32[4,1,128]{2,1,0:T(1,128)S(1)} all-gather(f32[1,1,128]{2,1,0:T(1,128)S(1)} %bitcast.93), channel_id=2, replica_groups=mesh['group'=4,'member'=8] {'group'}, dimensions={0}, use_global_device_ids=true | all-gather | bytes 2560 | tf_op jit(solution)/shard_map/all_gather | solution.py:49
  35.1 0.9 fusion.12
  36.0 6.0 %all-gather.12.cloned.1.call-done = bf16[512,1024]{1,0:T(8,128)(2,1)} async-done(((bf16[128,1024]{1,0:T(8,128)(2,1)}), bf16[512,1024]{1,0:T(8,128)(2,1)}) %all-gather.12.cloned.1.call-update) | async-done | bytes 1048592 | tf_op jit(solution)/shard_map/all_gather | solution.py:47
  42.0 30.5 %all-gather.10.cloned.1.call-done = bf16[1024,1024]{1,0:T(8,128)(2,1)} async-done(((bf16[128,1024]{1,0:T(8,128)(2,1)}), bf16[1024,1024]{1,0:T(8,128)(2,1)}) %all-gather.10.cloned.1.call-update) | async-done | bytes 2097168 | tf_op jit(solution)/shard_map/all_gather | solution.py:46
  72.6 3.3 %fusion.24 = (f32[4,128]{1,0:T(4,128)S(1)}, f32[4,128,1024]{2,1,0:T(8,128)S(1)}) fusion(bf16[4,128,1024]{2,1,0:T(8,128)(2,1)} %bitcast.85, bf16[1024,1024]{1,0:T(8,128)(2,1)} %all-gather.10.cloned.1.call-done, pred[4,1024]{1,0:T(4,128)(4,1)S(1)} %broadcast_in_dim.21), kind=kOutput, calls=%fused_computation.58 | convolution fusion | flops 1075314176 | bytes 5249024 | tf_op jit(solution)/shard_map/gqe,ke->gqk/dot_general | solution.py:59
  76.4 10.5 %all-gather.2 = f32[8,4,128]{2,1,0:T(4,128)S(1)} all-gather(f32[2,4,128]{2,1,0:T(4,128)S(1)} %pad_maximum_fusion.1), channel_id=4, replica_groups=mesh['group'=4,'member'=8] {'group'}, dimensions={0}, use_global_device_ids=true | all-gather | bytes 20480 | tf_op jit(solution)/shard_map/all_gather | solution.py:66
  89.8 2.4 add_convert_fusion
  92.3 4.1 %fusion = f32[4,128,1024]{2,1,0:T(8,128)} fusion(bf16[4,128,1024]{2,1,0:T(8,128)(2,1)S(1)} %multiply_convert_fusion, bf16[1024,1024]{1,0:T(8,128)(2,1)} %all-gather.10.cloned.1.call-done), kind=kOutput, calls=%fused_computation.4 | convolution fusion | flops 1073741824 | bytes 5242880 | tf_op jit(solution)/shard_map/gqk,ke->gqe/dot_general | solution.py:82
  96.5 39.3 %reduce-scatter.6.cloned.1.call-done = bf16[128,1024]{1,0:T(8,128)(2,1)} async-done(((bf16[1024,1024]{1,0:T(8,128)(2,1)}), bf16[128,1024]{1,0:T(8,128)(2,1)}) %reduce-scatter.6.cloned.1.call-update) | async-done | bytes 262160 | tf_op jit(solution)/shard_map/reduce_scatter | solution.py:92
  135.8 1.2 fusion.6
  136.9 1.1 fusion.8
  138.1 43.3 %reduce-scatter.4.cloned.1.call-done = f32[1,128,1024]{2,1,0:T(8,128)} async-done(((f32[4,128,1024]{2,1,0:T(8,128)}), f32[1,128,1024]{2,1,0:T(8,128)}) %reduce-scatter.4.cloned.1.call-update) | async-done | bytes 524304 | tf_op jit(solution)/shard_map/reduce_scatter | solution.py:83
  181.3 1.2 fusion.9
  182.6 1.2 fusion.11
  183.8 0.8 pad_maximum_fusion
  186.4 35.8 %all_to_all.5 = bf16[8,2,128,4,128]{2,4,1,3,0:T(8,128)(2,1)} all-to-all(bf16[8,2,128,4,128]{2,4,1,3,0:T(8,128)(2,1)S(1)} %copy.20), channel_id=1, replica_groups=mesh['group'=4,'member'=8] {'member'}, dimensions={0} | all-to-all | bytes 4194304 | tf_op jit(solution)/shard_map/all_to_all | solution.py:42
  222.2 12.7 %all-gather.14.cloned.1.call-done = bf16[16,128,1024]{2,1,0:T(8,128)(2,1)} async-done(((bf16[2,128,1024]{2,1,0:T(8,128)(2,1)}), bf16[16,128,1024]{2,1,0:T(8,128)(2,1)}) %all-gather.14.cloned.1.call-update) | async-done | bytes 4194320 | tf_op jit(solution)/shard_map/all_gather | solution.py:105
  234.9 6.5 %convolution_bitcast_fusion = f32[4,128,1024]{2,1,0:T(8,128)} fusion(bf16[8,2,128,4,128]{2,4,1,3,0:T(8,128)(2,1)} %all_to_all.5, bf16[8,2,128,1024,1]{3,2,1,4,0:T(8,128)(2,1)} %bitcast.94), kind=kOutput, calls=%fused_computation.11 | convolution fusion | flops 2147483648 | bytes 8388608 | tf_op jit(solution)/shard_map/mtqgr,mtqe->gre/dot_general | solution.py:106
  241.4 7.3 %convolution_convert_fusion = bf16[128,4096]{1,0:T(8,128)(2,1)} fusion(bf16[128,1024]{1,0:T(8,128)(2,1)S(1)} %fusion.8, bf16[4096,1024]{1,0:T(8,128)(2,1)} %param.7), kind=kOutput, calls=%fused_computation | convolution fusion | flops 1074266112 | bytes 9699328 | tf_op jit(solution)/shard_map/qe,de->qd/dot_general | solution.py:101
  248.7 7.2 %convolution_convert_fusion.1 = bf16[128,4096]{1,0:T(8,128)(2,1)} fusion(bf16[128,1024]{1,0:T(8,128)(2,1)S(1)} %copy-done.3, bf16[4096,1024]{1,0:T(8,128)(2,1)} %param.7), kind=kOutput, calls=%fused_computation.1 | convolution fusion | flops 1074266112 | bytes 9699328 | tf_op jit(solution)/shard_map/qe,de->qd/dot_general | solution.py:98
  256.0 26.7 %reduce-scatter.8.cloned.1.call-done = f32[1,128,1024]{2,1,0:T(8,128)} async-done(((f32[4,128,1024]{2,1,0:T(8,128)}), f32[1,128,1024]{2,1,0:T(8,128)}) %reduce-scatter.8.cloned.1.call-update) | async-done | bytes 524304 | tf_op jit(solution)/shard_map/reduce_scatter | solution.py:109
  (55 shorter events, 7.8 us)
Async XLA Ops:
  7.2 34.9 %all-gather.12.cloned.1.call-start = ((), (), s32[]{:S(2)}) async-start(), calls=%async_computation.8 | async-start | bytes 1310720 | tf_op jit(solution)/shard_map/all_gather | solution.py:47
  12.3 1.3 copy-start
  13.1 6.1 %copy-start.6 = (s32[1,16]{1,0:T(1,128)S(1)}, s32[1,16]{1,0:T(1,128)}, u32[]{:S(2)}) copy-start(s32[1,16]{1,0:T(1,128)} %param.8) | copy-start | bytes 196
  13.1 15.8 %copy-start.7 = (f32[128]{0:T(128)S(1)}, f32[128]{0:T(128)}, u32[]{:S(2)}) copy-start(f32[128]{0:T(128)} %param.9) | copy-start | bytes 1540
  13.1 59.4 %all-gather.10.cloned.1.call-start = ((), (), s32[]{:S(2)}) async-start(), calls=%async_computation.4 | async-start | bytes 2359296 | tf_op jit(solution)/shard_map/all_gather | solution.py:46
  19.2 116.6 %reduce-scatter.6.cloned.1.call-start = ((), (), s32[]{:S(2)}) async-start(), calls=%async_computation.6 | async-start | bytes 2359296 | tf_op jit(solution)/shard_map/reduce_scatter | solution.py:92
  75.9 11.1 %copy-start.4 = (f32[128,1024]{1,0:T(8,128)S(1)}, f32[128,1024]{1,0:T(8,128)}, u32[]{:S(2)}) copy-start(f32[128,1024]{1,0:T(8,128)} %fusion.12) | copy-start | bytes 1572868
  76.4 11.2 %copy-start.5 = (bf16[512,1024]{1,0:T(8,128)(2,1)S(1)}, bf16[512,1024]{1,0:T(8,128)(2,1)}, u32[]{:S(2)}) copy-start(bf16[512,1024]{1,0:T(8,128)(2,1)} %all-gather.12.cloned.1.call-done) | copy-start | bytes 3145732
  92.2 89.1 %reduce-scatter.4.cloned.1.call-start = ((), (), s32[]{:S(2)}) async-start(), calls=%async_computation.5 | async-start | bytes 2621440 | tf_op jit(solution)/shard_map/reduce_scatter | solution.py:83
  96.5 138.5 %all-gather.14.cloned.1.call-start = ((), (), s32[]{:S(2)}) async-start(), calls=%async_computation.9 | async-start | bytes 4718592 | tf_op jit(solution)/shard_map/all_gather | solution.py:105
  183.8 0.9 copy-start.2
  183.8 1.6 copy-start.1
  184.7 98.0 %reduce-scatter.8.cloned.1.call-start = ((), (), s32[]{:S(2)}) async-start(), calls=%async_computation.7 | async-start | bytes 2621440 | tf_op jit(solution)/shard_map/reduce_scatter | solution.py:109
  241.4 7.3 %copy-start.3 = (bf16[128,1024]{1,0:T(8,128)(2,1)S(1)}, bf16[128,1024]{1,0:T(8,128)(2,1)}, u32[]{:S(2)}) copy-start(bf16[128,1024]{1,0:T(8,128)(2,1)} %copy-done.2) | copy-start | bytes 786436
Sparse Core Ops, SparseCore 0:
  13.2 28.7 all-gather.11
  44.5 28.0 all-gather.9
  92.4 43.3 reduce-scatter.5
  137.9 43.3 reduce-scatter.3
  184.8 50.0 all-gather.13
  241.5 41.0 reduce-scatter.7

commit v2 on v1

--- a/solution.py
+++ b/solution.py
@@ -22,6 +22,27 @@
     return (inverse[:, None] * (upstream - unit_vec * inner_prod)).astype(jnp.bfloat16)
 
 
+def shift_all(x, axis):
+    size = lax.axis_size(axis)
+    index = lax.axis_index(axis)
+    got = [x]
+    for s in range(1, size):
+        got.append(lax.ppermute(x, axis, [(i, (i + s) % size) for i in range(size)]))
+    order = (index - jnp.arange(size)) % size
+    return jax.tree.map(lambda *xs: jnp.take(jnp.stack(xs, axis=0), order, axis=0), *got)
+
+
+def exchange(parts, axis):
+    size = lax.axis_size(axis)
+    index = lax.axis_index(axis)
+    got = [jnp.take(parts, index, axis=0)]
+    for s in range(1, size):
+        sent = jnp.take(parts, (index + s) % size, axis=0)
+        got.append(lax.ppermute(sent, axis, [(i, (i + s) % size) for i in range(size)]))
+    stacked = jnp.stack(got, axis=0)
+    return jnp.take(stacked, (index - jnp.arange(size)) % size, axis=0)
+
+
 def body(query_feat, code_feat, projection, hard_ids, loss_weight):
     groups = lax.axis_size("group")
     members = lax.axis_size("member")
@@ -39,14 +60,12 @@
         2, queries_dev, groups, members, rows_dev
     )
     feats = jnp.transpose(feats, (3, 0, 1, 2, 4))
-    feat_cols = lax.all_to_all(feats, "member", split_axis=0, concat_axis=0, tiled=True)
+    feat_cols = exchange(feats, "member")
 
     q_unit, q_inv, q_emb = embed(query_feat, projection)
     c_unit, c_inv, c_emb = embed(code_feat, projection)
     group_codes = lax.all_gather(c_emb, "member", axis=0, tiled=True)
-    q_all = lax.all_gather(q_emb, "group", axis=0)
-    ids_all = lax.all_gather(hard_ids[0], "group", axis=0)
-    w_all = lax.all_gather(loss_weight, "group", axis=0)
+    q_all, ids_all, w_all = shift_all((q_emb, hard_ids[0], loss_weight), "group")
 
     block_ids = group_index * per_group + jnp.arange(per_group, dtype=jnp.int32)
     asked = jnp.any(ids_all[:, :, None] == block_ids[None, None, :], axis=1)
@@ -63,7 +82,7 @@
     part_max = jnp.max(scores, axis=2)
     safe_max = jnp.where(part_max > -jnp.inf, part_max, 0.0)
     part_sum = jnp.sum(jnp.exp(scores - safe_max[:, :, None]), axis=2)
-    stats = lax.all_gather(jnp.stack([part_max, part_sum], axis=0), "group", axis=0)
+    stats = shift_all(jnp.stack([part_max, part_sum], axis=0), "group")
     row_max = jnp.max(stats[:, 0], axis=0)
     row_sum = jnp.sum(stats[:, 1] * jnp.exp(stats[:, 0] - row_max[None]), axis=0)
     log_total = row_max + jnp.log(row_sum)
@@ -80,9 +99,9 @@
     ).astype(jnp.bfloat16)
 
     delta_parts = jnp.einsum("gqk,ke->gqe", grad, group_codes, preferred_element_type=jnp.float32)
-    query_delta = lax.psum_scatter(delta_parts, "group", scatter_dimension=0, tiled=True).reshape(
-        queries_dev, emb_width
-    )
+    returned = exchange(delta_parts.astype(jnp.bfloat16), "group").astype(jnp.float32)
+    own_part = jnp.take(delta_parts, group_index, axis=0)
+    query_delta = own_part + jnp.sum(jnp.where(own[:, None, None], 0.0, returned), axis=0)
 
     code_terms = None
     for g in range(groups):

time: 292 us -> 230 us (0.79)
  blocking collectives: 61.8 us -> 0 us
  waiting for transfers between devices: 159 us -> 119 us
  starting transfers between devices: 0.25 us -> 26.6 us
  local copies, waits for them, and re-layouts: 2.08 us -> 12.2 us
  other arithmetic: 9.62 us -> 12.7 us
    ppermute x0 -> x22, waiting for transfers between devices: none -> 63.5 us  [the longest x10 44.5 us: exchange(): lax.ppermute(sent, axis, [(i, (i + s) % size) for i in range(size)])]
    reduce_scatter x1 -> x0, waiting for transfers between devices: 43.3 us -> none  [body(): lax.psum_scatter(delta_parts, 'group', scatter_dimension=0, tiled=True)]
    all_to_all x1 -> x0, blocking collectives: 35.8 us -> none  [body(): lax.all_to_all(feats, 'member', split_axis=0, concat_axis=0, tiled=True)]
    all_gather x1, waiting for transfers between devices: 30.5 us -> 0.01 us  [body(): group_codes = lax.all_gather(c_emb, 'member', axis=0, tiled=True)]
    ppermute x0 -> x22, starting transfers between devices: none -> 26.5 us  [the longest x12 18.3 us: shift_all(): lax.ppermute(x, axis, [(i, (i + s) % size) for i in range(size)])]
    all_gather x3 -> x0, blocking collectives: 26 us -> none  [the longest x1 10.5 us: body(): lax.all_gather(jnp.stack([part_max, part_sum], axis=0), 'group', axis=0)]
    reduce_scatter x1, waiting for transfers between devices: 39.3 us -> 15.3 us  [body(): lax.psum_scatter(code_terms.astype(jnp.bfloat16), 'member', scatter_dimen...]
    all_gather x1 -> x0, waiting for transfers between devices: 6.01 us -> none  [body(): q_all = lax.all_gather(q_emb, 'group', axis=0)]
  transfers between devices with their start and end apart: 6 -> 26, of which waited for: 6 -> 16; matrix products, arithmetic and copies ran while one was open for 10% -> 17% of each run, Pallas kernels for 0% -> 0%
where the time goes in v2:
time: 230 us; the launch traced here: 228 us
  waiting for transfers between devices  119 us (52%)
  matrix products  42.9 us (19%)
  starting transfers between devices  26.6 us (12%)
  between operations  14.4 us (6%)
  other arithmetic  12.7 us (6%)
  local copies, waits for them, and re-layouts  12.2 us (5%)
    ppermute x10, waiting for transfers between devices, exchange(): lax.ppermute(sent, axis, [(i, (i + s) % size) for i in range(size)])  44.5 us
    reduce_scatter x1, waiting for transfers between devices, body(): lax.psum_scatter(proj_parts, 'group', scatter_dimension=0, tiled=True)  27.6 us
    ppermute x12, waiting for transfers between devices, shift_all(): lax.ppermute(x, axis, [(i, (i + s) % size) for i in range(size)])  19 us
    ppermute x12, starting transfers between devices, shift_all(): lax.ppermute(x, axis, [(i, (i + s) % size) for i in range(size)])  18.3 us
    reduce_scatter x1, waiting for transfers between devices, body(): lax.psum_scatter(code_terms.astype(jnp.bfloat16), 'member', scatter_dimen...  15.3 us
    all_gather x1, waiting for transfers between devices, body(): lax.all_gather(jnp.stack([dz_query, dz_code], axis=0), 'member', axis=0)  12.2 us
    dot_general x2, matrix products, embed(): values = jnp.dot(features, projection, preferred_element_type=jnp.float32)  9.77 us
    ppermute x10, starting transfers between devices, exchange(): lax.ppermute(sent, axis, [(i, (i + s) % size) for i in range(size)])  8.16 us
  transfers between devices with their start and end apart: 26, of which 16 were waited for; matrix products, arithmetic and copies ran while one was open for 17% of the time, Pallas kernels for 0%

profile of v2, /device:TPU:3, one launch (start us, length us, event | category | flops | bytes accessed | tf_op | source)
XLA Modules:
  0.0 227.5 jit_solution(4408470070603860099)
XLA Ops:
  7.2 5.1 %multiply_reduce_fusion.1 = (f32[128]{0:T(128)S(1)}, f32[128,1024]{1,0:T(8,128)S(1)}) fusion(bf16[128,4096]{1,0:T(8,128)(2,1)} %param.12, bf16[4096,1024]{1,0:T(8,128)(2,1)} %param.13), kind=kOutput, calls=%fused_computation.36 | convolution fusion | flops 1074003840 | bytes 9961984 | tf_op jit(solution)/shard_map/dot_general | solution.py:14
  13.6 4.7 %multiply_reduce_fusion.2 = (f32[128]{0:T(128)S(1)}, f32[128,1024]{1,0:T(8,128)S(1)}) fusion(bf16[128,4096]{1,0:T(8,128)(2,1)S(1)} %copy-done.1, bf16[4096,1024]{1,0:T(8,128)(2,1)} %param.13), kind=kOutput, calls=%fused_computation.37 | convolution fusion | flops 1074003840 | bytes 9961984 | tf_op jit(solution)/shard_map/dot_general | solution.py:14
  18.4 3.4 %collective-permute-start.8 = (bf16[128,1024]{1,0:T(8,128)(2,1)S(1)}, bf16[128,1024]{1,0:T(8,128)(2,1)S(1)}, u32[]{:S(2)}, u32[]{:S(2)}) collective-permute-start(bf16[128,1024]{1,0:T(8,128)(2,1)S(1)} %multiply_convert_fusion.3), channel_id=1, source_target_pairs={{0,24},{8,0},{16,8},{24,16},{1,25},{9,1},{17,9},{25,17},{2,26},{10... | collective-permute-start | bytes 786440 | tf_op jit(solution)/shard_map/ppermute | solution.py:30
  22.3 2.8 %collective-permute-start.5 = (s32[16]{0:T(128)S(1)}, s32[16]{0:T(128)S(1)}, u32[]{:S(2)}, u32[]{:S(2)}) collective-permute-start(s32[16]{0:T(128)S(1)} %bitcast.161), channel_id=1, source_target_pairs={{0,24},{8,0},{16,8},{24,16},{1,25},{9,1},{17,9},{25,17},{2,26},{10... | collective-permute-start | bytes 200 | tf_op jit(solution)/shard_map/ppermute | solution.py:30
  26.8 11.4 %collective-permute-done.5 = s32[16]{0:T(128)S(1)} collective-permute-done((s32[16]{0:T(128)S(1)}, s32[16]{0:T(128)S(1)}, u32[]{:S(2)}, u32[]{:S(2)}) %collective-permute-start.5) | collective-permute-done | bytes 96 | tf_op jit(solution)/shard_map/ppermute | solution.py:30
  38.2 5.3 %collective-permute-start.3 = (s32[16]{0:T(128)S(1)}, s32[16]{0:T(128)S(1)}, u32[]{:S(2)}, u32[]{:S(2)}) collective-permute-start(s32[16]{0:T(128)S(1)} %bitcast.163), channel_id=1, source_target_pairs={{0,8},{8,16},{16,24},{24,0},{1,9},{9,17},{17,25},{25,1},{2,10},{10... | collective-permute-start | bytes 200 | tf_op jit(solution)/shard_map/ppermute | solution.py:30
  43.6 3.4 %collective-permute-start.2 = (f32[128]{0:T(128)S(1)}, f32[128]{0:T(128)S(1)}, u32[]{:S(2)}, u32[]{:S(2)}) collective-permute-start(f32[128]{0:T(128)S(1)} %copy-done.9), channel_id=1, source_target_pairs={{0,24},{8,0},{16,8},{24,16},{1,25},{9,1},{17,9},{25,17},{2,26},{10... | collective-permute-start | bytes 1544 | tf_op jit(solution)/shard_map/ppermute | solution.py:30
  54.7 3.3 %fusion.32 = (f32[4,128]{1,0:T(4,128)S(1)}, f32[4,128,1024]{2,1,0:T(8,128)S(1)}) fusion(bf16[4,128,1024]{2,1,0:T(8,128)(2,1)} %broadcast_select_fusion, bf16[1024,1024]{1,0:T(8,128)(2,1)} %all-gather.4.cloned.1.call-done, pred[4,1024]{1,0:T(4,128)(4,1)S(1)} %broadcast_in_dim.140), kind=kOutput, calls=%fused_computation.123 | convolution fusion | flops 1075314176 | bytes 5249024 | tf_op jit(solution)/shard_map/gqe,ke->gqk/dot_general | solution.py:78
  61.0 2.4 %collective-permute-done.10 = f32[2,4,128]{2,1,0:T(4,128)S(1)} collective-permute-done((f32[2,4,128]{2,1,0:T(4,128)S(1)}, f32[2,4,128]{2,1,0:T(4,128)S(1)}, u32[]{:S(2)}, u32[]{:S(2)}) %collective-permute-start.10) | collective-permute-done | bytes 4128 | tf_op jit(solution)/shard_map/ppermute | solution.py:30
  68.9 2.4 %add_convert_fusion = bf16[1024,1024]{1,0:T(8,128)(2,1)} fusion(f32[1024,1024]{1,0:T(8,128)S(1)} %fusion.17, f32[1024,1024]{1,0:T(8,128)S(1)} %fusion.18, f32[1024,1024]{1,0:T(8,128)S(1)} %fusion.19, pred[]{:T(512)S(6)} %eq.84, pred[]{:T(512)S(6)} %eq.83, pred[]{:T(512)S(6)} %eq.82, pred[]{:T(512)S(6)} %eq.81, bf16[4,128,1024]{2,1,0:T(8,128)(2,1)S(1)} %copy-done.5, ...), kind=kOutput, calls=%fused_computation.8 | convolution fusion | flops 285212672 | bytes 15204356 | tf_op jit(solution)/shard_map/dot_general | solution.py:108
  72.5 4.2 %fusion.33 = (bf16[4,128,1024]{2,1,0:T(8,128)(2,1)S(1)}, f32[4,128,1024]{2,1,0:T(8,128)}) fusion(bf16[4,128,1024]{2,1,0:T(8,128)(2,1)S(1)} %copy-done.4, bf16[1024,1024]{1,0:T(8,128)(2,1)} %all-gather.4.cloned.1.call-done), kind=kOutput, calls=%fused_computation.124 | convolution fusion | flops 1074266112 | bytes 6291456 | tf_op jit(solution)/shard_map/gqk,ke->gqe/dot_general | solution.py:101
  78.8 4.4 %collective-permute-done.14 = bf16[128,1024]{1,0:T(8,128)(2,1)S(1)} collective-permute-done((bf16[128,1024]{1,0:T(8,128)(2,1)S(1)}, bf16[128,1024]{1,0:T(8,128)(2,1)S(1)}, u32[]{:S(2)}, u32[]{:S(2)}) %collective-permute-start.14) | collective-permute-done | bytes 262176 | tf_op jit(solution)/shard_map/ppermute | solution.py:41
  83.3 13.5 %collective-permute-done.13 = bf16[128,1024]{1,0:T(8,128)(2,1)S(1)} collective-permute-done((bf16[128,1024]{1,0:T(8,128)(2,1)S(1)}, bf16[128,1024]{1,0:T(8,128)(2,1)S(1)}, u32[]{:S(2)}, u32[]{:S(2)}) %collective-permute-start.13) | collective-permute-done | bytes 262176 | tf_op jit(solution)/shard_map/ppermute | solution.py:41
  100.4 15.3 %reduce-scatter.3.cloned.1.call-done = bf16[128,1024]{1,0:T(8,128)(2,1)} async-done(((bf16[1024,1024]{1,0:T(8,128)(2,1)}), bf16[128,1024]{1,0:T(8,128)(2,1)}) %reduce-scatter.3.cloned.1.call-update) | async-done | bytes 262160 | tf_op jit(solution)/shard_map/reduce_scatter | solution.py:111
  124.1 2.0 collective-permute-start.15
  129.6 5.7 %collective-permute-done.15 = bf16[2,128,4,128]{3,1,2,0:T(8,128)(2,1)S(1)} collective-permute-done((bf16[2,128,4,128]{3,1,2,0:T(8,128)(2,1)S(1)}, bf16[2,128,4,128]{3,1,2,0:T(8,128)(2,1)S(1)}, u32[]{:S(2)}, u32[]{:S(2)}) %collective-permute-start.15) | collective-permute-done | bytes 262176 | tf_op jit(solution)/shard_map/ppermute | solution.py:41
  135.9 7.9 %collective-permute-done.16 = bf16[2,128,4,128]{3,1,2,0:T(8,128)(2,1)S(1)} collective-permute-done((bf16[2,128,4,128]{3,1,2,0:T(8,128)(2,1)S(1)}, bf16[2,128,4,128]{3,1,2,0:T(8,128)(2,1)S(1)}, u32[]{:S(2)}, u32[]{:S(2)}) %collective-permute-start.16) | collective-permute-done | bytes 262176 | tf_op jit(solution)/shard_map/ppermute | solution.py:41
  145.1 10.6 %collective-permute-done.18 = bf16[2,128,4,128]{3,1,2,0:T(8,128)(2,1)S(1)} collective-permute-done((bf16[2,128,4,128]{3,1,2,0:T(8,128)(2,1)S(1)}, bf16[2,128,4,128]{3,1,2,0:T(8,128)(2,1)S(1)}, u32[]{:S(2)}, u32[]{:S(2)}) %collective-permute-start.18) | collective-permute-done | bytes 262176 | tf_op jit(solution)/shard_map/ppermute | solution.py:41
  157.0 2.2 gather_fusion.3
  159.2 12.2 %all-gather.6.cloned.1.call-done = bf16[16,128,1024]{2,1,0:T(8,128)(2,1)} async-done(((bf16[2,128,1024]{2,1,0:T(8,128)(2,1)}), bf16[16,128,1024]{2,1,0:T(8,128)(2,1)}) %all-gather.6.cloned.1.call-update) | async-done | bytes 4194320 | tf_op jit(solution)/shard_map/all_gather | solution.py:124
  171.4 6.6 %fusion.7 = f32[4,128,1024]{2,1,0:T(8,128)} fusion(bf16[8,2,128,1024,1]{3,2,4,1,0:T(8,128)(2,1)} %bitcast.171, bf16[8,2,128,4,128]{4,2,3,1,0:T(8,128)(2,1)} %gather_fusion.3, pred[8]{0:T(512)(128)(4,1)S(1)} %compare_and_fusion), kind=kOutput, calls=%fused_computation.21 | convolution fusion | flops 2148532224 | bytes 8388616 | tf_op jit(solution)/shard_map/mtqgr,mtqe->gre/dot_general | solution.py:125
  178.9 7.2 %convolution_convert_fusion.1 = bf16[128,4096]{1,0:T(8,128)(2,1)} fusion(bf16[128,1024]{1,0:T(8,128)(2,1)S(1)} %copy-done.7, bf16[4096,1024]{1,0:T(8,128)(2,1)} %param.13), kind=kOutput, calls=%fused_computation.7 | convolution fusion | flops 1074266112 | bytes 9699328 | tf_op jit(solution)/shard_map/qe,de->qd/dot_general | solution.py:117
  186.2 7.2 %convolution_convert_fusion = bf16[128,4096]{1,0:T(8,128)(2,1)} fusion(bf16[128,1024]{1,0:T(8,128)(2,1)S(1)} %fusion.15, bf16[4096,1024]{1,0:T(8,128)(2,1)} %param.13), kind=kOutput, calls=%fused_computation.6 | convolution fusion | flops 1074266112 | bytes 9699328 | tf_op jit(solution)/shard_map/qe,de->qd/dot_general | solution.py:120
  193.4 27.6 %reduce-scatter.5.cloned.1.call-done = f32[1,128,1024]{2,1,0:T(8,128)} async-done(((f32[4,128,1024]{2,1,0:T(8,128)}), f32[1,128,1024]{2,1,0:T(8,128)}) %reduce-scatter.5.cloned.1.call-update) | async-done | bytes 524304 | tf_op jit(solution)/shard_map/reduce_scatter | solution.py:128
  (126 shorter events, 42.4 us)
Async XLA Ops:
  7.2 47.5 %all-gather.4.cloned.1.call-start = ((), (), s32[]{:S(2)}) async-start(), calls=%async_computation.2 | async-start | bytes 2359296 | tf_op jit(solution)/shard_map/all_gather | solution.py:67
  13.1 102.5 %reduce-scatter.3.cloned.1.call-start = ((), (), s32[]{:S(2)}) async-start(), calls=%async_computation.3 | async-start | bytes 2359296 | tf_op jit(solution)/shard_map/reduce_scatter | solution.py:111
  18.4 34.3 %collective-permute-start.8 = (bf16[128,1024]{1,0:T(8,128)(2,1)S(1)}, bf16[128,1024]{1,0:T(8,128)(2,1)S(1)}, u32[]{:S(2)}, u32[]{:S(2)}) collective-permute-start(bf16[128,1024]{1,0:T(8,128)(2,1)S(1)} %multiply_convert_fusion.3), channel_id=1, source_target_pairs={{0,24},{8,0},{16,8},{24,16},{1,25},{9,1},{17,9},{25,17},{2,26},{10... | collective-permute-start | bytes 786440 | tf_op jit(solution)/shard_map/ppermute | solution.py:30
  21.8 31.0 %collective-permute-start.7 = (bf16[128,1024]{1,0:T(8,128)(2,1)S(1)}, bf16[128,1024]{1,0:T(8,128)(2,1)S(1)}, u32[]{:S(2)}, u32[]{:S(2)}) collective-permute-start(bf16[128,1024]{1,0:T(8,128)(2,1)S(1)} %multiply_convert_fusion.3), channel_id=1, source_target_pairs={{0,16},{8,24},{16,0},{24,8},{1,17},{9,25},{17,1},{25,9},{2,18},{10... | collective-permute-start | bytes 786440 | tf_op jit(solution)/shard_map/ppermute | solution.py:30
  21.8 31.0 %collective-permute-start.6 = (bf16[128,1024]{1,0:T(8,128)(2,1)S(1)}, bf16[128,1024]{1,0:T(8,128)(2,1)S(1)}, u32[]{:S(2)}, u32[]{:S(2)}) collective-permute-start(bf16[128,1024]{1,0:T(8,128)(2,1)S(1)} %multiply_convert_fusion.3), channel_id=1, source_target_pairs={{0,8},{8,16},{16,24},{24,0},{1,9},{9,17},{17,25},{25,1},{2,10},{10... | collective-permute-start | bytes 786440 | tf_op jit(solution)/shard_map/ppermute | solution.py:30
  22.3 15.9 %collective-permute-start.5 = (s32[16]{0:T(128)S(1)}, s32[16]{0:T(128)S(1)}, u32[]{:S(2)}, u32[]{:S(2)}) collective-permute-start(s32[16]{0:T(128)S(1)} %bitcast.161), channel_id=1, source_target_pairs={{0,24},{8,0},{16,8},{24,16},{1,25},{9,1},{17,9},{25,17},{2,26},{10... | collective-permute-start | bytes 200 | tf_op jit(solution)/shard_map/ppermute | solution.py:30
  25.1 18.5 %collective-permute-start.4 = (s32[16]{0:T(128)S(1)}, s32[16]{0:T(128)S(1)}, u32[]{:S(2)}, u32[]{:S(2)}) collective-permute-start(s32[16]{0:T(128)S(1)} %bitcast.162), channel_id=1, source_target_pairs={{0,16},{8,24},{16,0},{24,8},{1,17},{9,25},{17,1},{25,9},{2,18},{10... | collective-permute-start | bytes 200 | tf_op jit(solution)/shard_map/ppermute | solution.py:30
  38.2 8.8 %collective-permute-start.3 = (s32[16]{0:T(128)S(1)}, s32[16]{0:T(128)S(1)}, u32[]{:S(2)}, u32[]{:S(2)}) collective-permute-start(s32[16]{0:T(128)S(1)} %bitcast.163), channel_id=1, source_target_pairs={{0,8},{8,16},{16,24},{24,0},{1,9},{9,17},{17,25},{25,1},{2,10},{10... | collective-permute-start | bytes 200 | tf_op jit(solution)/shard_map/ppermute | solution.py:30
  43.6 4.2 %collective-permute-start.2 = (f32[128]{0:T(128)S(1)}, f32[128]{0:T(128)S(1)}, u32[]{:S(2)}, u32[]{:S(2)}) collective-permute-start(f32[128]{0:T(128)S(1)} %copy-done.9), channel_id=1, source_target_pairs={{0,24},{8,0},{16,8},{24,16},{1,25},{9,1},{17,9},{25,17},{2,26},{10... | collective-permute-start | bytes 1544 | tf_op jit(solution)/shard_map/ppermute | solution.py:30
  47.8 4.4 %collective-permute-start = (f32[128]{0:T(128)S(1)}, f32[128]{0:T(128)S(1)}, u32[]{:S(2)}, u32[]{:S(2)}) collective-permute-start(f32[128]{0:T(128)S(1)} %copy-done.9), channel_id=1, source_target_pairs={{0,8},{8,16},{16,24},{24,0},{1,9},{9,17},{17,25},{25,1},{2,10},{10... | collective-permute-start | bytes 1544 | tf_op jit(solution)/shard_map/ppermute | solution.py:30
  60.0 3.4 %collective-permute-start.10 = (f32[2,4,128]{2,1,0:T(4,128)S(1)}, f32[2,4,128]{2,1,0:T(4,128)S(1)}, u32[]{:S(2)}, u32[]{:S(2)}) collective-permute-start(f32[2,4,128]{2,1,0:T(4,128)S(1)} %get-tuple-element.52), channel_id=1, source_target_pairs={{0,16},{8,24},{16,0},{24,8},{1,17},{9,25},{17,1},{25,9},{2,18},{10... | collective-permute-start | bytes 12296 | tf_op jit(solution)/shard_map/ppermute | solution.py:30
  60.0 4.3 %collective-permute-start.9 = (f32[2,4,128]{2,1,0:T(4,128)S(1)}, f32[2,4,128]{2,1,0:T(4,128)S(1)}, u32[]{:S(2)}, u32[]{:S(2)}) collective-permute-start(f32[2,4,128]{2,1,0:T(4,128)S(1)} %get-tuple-element.52), channel_id=1, source_target_pairs={{0,8},{8,16},{16,24},{24,0},{1,9},{9,17},{17,25},{25,1},{2,10},{10... | collective-permute-start | bytes 12296 | tf_op jit(solution)/shard_map/ppermute | solution.py:30
  71.3 100.1 %all-gather.6.cloned.1.call-start = ((), (), s32[]{:S(2)}) async-start(), calls=%async_computation.5 | async-start | bytes 4718592 | tf_op jit(solution)/shard_map/all_gather | solution.py:124
  76.8 6.5 %collective-permute-start.14 = (bf16[128,1024]{1,0:T(8,128)(2,1)S(1)}, bf16[128,1024]{1,0:T(8,128)(2,1)S(1)}, u32[]{:S(2)}, u32[]{:S(2)}) collective-permute-start(bf16[128,1024]{1,0:T(8,128)(2,1)S(1)} %get-tuple-element.48), channel_id=1, source_target_pairs={{0,24},{8,0},{16,8},{24,16},{1,25},{9,1},{17,9},{25,17},{2,26},{10... | collective-permute-start | bytes 786440 | tf_op jit(solution)/shard_map/ppermute | solution.py:41
  77.1 19.7 %collective-permute-start.13 = (bf16[128,1024]{1,0:T(8,128)(2,1)S(1)}, bf16[128,1024]{1,0:T(8,128)(2,1)S(1)}, u32[]{:S(2)}, u32[]{:S(2)}) collective-permute-start(bf16[128,1024]{1,0:T(8,128)(2,1)S(1)} %get-tuple-element.49), channel_id=1, source_target_pairs={{0,16},{8,24},{16,0},{24,8},{1,17},{9,25},{17,1},{25,9},{2,18},{10... | collective-permute-start | bytes 786440 | tf_op jit(solution)/shard_map/ppermute | solution.py:41
  77.5 19.4 %collective-permute-start.12 = (bf16[128,1024]{1,0:T(8,128)(2,1)S(1)}, bf16[128,1024]{1,0:T(8,128)(2,1)S(1)}, u32[]{:S(2)}, u32[]{:S(2)}) collective-permute-start(bf16[128,1024]{1,0:T(8,128)(2,1)S(1)} %get-tuple-element.50), channel_id=1, source_target_pairs={{0,8},{8,16},{16,24},{24,0},{1,9},{9,17},{17,25},{25,1},{2,10},{10... | collective-permute-start | bytes 786440 | tf_op jit(solution)/shard_map/ppermute | solution.py:41
  118.8 102.1 %reduce-scatter.5.cloned.1.call-start = ((), (), s32[]{:S(2)}) async-start(), calls=%async_computation.4 | async-start | bytes 2621440 | tf_op jit(solution)/shard_map/reduce_scatter | solution.py:128
  124.1 11.2 %collective-permute-start.15 = (bf16[2,128,4,128]{3,1,2,0:T(8,128)(2,1)S(1)}, bf16[2,128,4,128]{3,1,2,0:T(8,128)(2,1)S(1)}, u32[]{:S(2)}, u32[]{:S(2)}) collective-permute-start(bf16[2,128,4,128]{3,1,2,0:T(8,128)(2,1)S(1)} %get-tuple-element.45), channel_id=1, source_target_pairs={{0,1},{1,2},{2,3},{3,4},{4,5},{5,6},{6,7},{7,0},{8,9},{9,10},{10,1... | collective-permute-start | bytes 786440 | tf_op jit(solution)/shard_map/ppermute | solution.py:41
  126.0 17.8 %collective-permute-start.16 = (bf16[2,128,4,128]{3,1,2,0:T(8,128)(2,1)S(1)}, bf16[2,128,4,128]{3,1,2,0:T(8,128)(2,1)S(1)}, u32[]{:S(2)}, u32[]{:S(2)}) collective-permute-start(bf16[2,128,4,128]{3,1,2,0:T(8,128)(2,1)S(1)} %get-tuple-element.44), channel_id=1, source_target_pairs={{0,2},{1,3},{2,4},{3,5},{4,6},{5,7},{6,0},{7,1},{8,10},{9,11},{10,... | collective-permute-start | bytes 786440 | tf_op jit(solution)/shard_map/ppermute | solution.py:41
  126.3 18.8 %collective-permute-start.17 = (bf16[2,128,4,128]{3,1,2,0:T(8,128)(2,1)S(1)}, bf16[2,128,4,128]{3,1,2,0:T(8,128)(2,1)S(1)}, u32[]{:S(2)}, u32[]{:S(2)}) collective-permute-start(bf16[2,128,4,128]{3,1,2,0:T(8,128)(2,1)S(1)} %get-tuple-element.43), channel_id=1, source_target_pairs={{0,3},{1,4},{2,5},{3,6},{4,7},{5,0},{6,1},{7,2},{8,11},{9,12},{10,... | collective-permute-start | bytes 786440 | tf_op jit(solution)/shard_map/ppermute | solution.py:41
  126.7 29.0 %collective-permute-start.18 = (bf16[2,128,4,128]{3,1,2,0:T(8,128)(2,1)S(1)}, bf16[2,128,4,128]{3,1,2,0:T(8,128)(2,1)S(1)}, u32[]{:S(2)}, u32[]{:S(2)}) collective-permute-start(bf16[2,128,4,128]{3,1,2,0:T(8,128)(2,1)S(1)} %get-tuple-element.42), channel_id=1, source_target_pairs={{0,4},{1,5},{2,6},{3,7},{4,0},{5,1},{6,2},{7,3},{8,12},{9,13},{10,... | collective-permute-start | bytes 786440 | tf_op jit(solution)/shard_map/ppermute | solution.py:41
  127.9 29.0 %collective-permute-start.19 = (bf16[2,128,4,128]{3,1,2,0:T(8,128)(2,1)S(1)}, bf16[2,128,4,128]{3,1,2,0:T(8,128)(2,1)S(1)}, u32[]{:S(2)}, u32[]{:S(2)}) collective-permute-start(bf16[2,128,4,128]{3,1,2,0:T(8,128)(2,1)S(1)} %get-tuple-element.41), channel_id=1, source_target_pairs={{0,5},{1,6},{2,7},{3,0},{4,1},{5,2},{6,3},{7,4},{8,13},{9,14},{10,... | collective-permute-start | bytes 786440 | tf_op jit(solution)/shard_map/ppermute | solution.py:41
  135.3 21.6 %collective-permute-start.20 = (bf16[2,128,4,128]{3,1,2,0:T(8,128)(2,1)S(1)}, bf16[2,128,4,128]{3,1,2,0:T(8,128)(2,1)S(1)}, u32[]{:S(2)}, u32[]{:S(2)}) collective-permute-start(bf16[2,128,4,128]{3,1,2,0:T(8,128)(2,1)S(1)} %get-tuple-element.40), channel_id=1, source_target_pairs={{0,6},{1,7},{2,0},{3,1},{4,2},{5,3},{6,4},{7,5},{8,14},{9,15},{10,... | collective-permute-start | bytes 786440 | tf_op jit(solution)/shard_map/ppermute | solution.py:41
  143.8 13.2 %collective-permute-start.21 = (bf16[2,128,4,128]{3,1,2,0:T(8,128)(2,1)S(1)}, bf16[2,128,4,128]{3,1,2,0:T(8,128)(2,1)S(1)}, u32[]{:S(2)}, u32[]{:S(2)}) collective-permute-start(bf16[2,128,4,128]{3,1,2,0:T(8,128)(2,1)S(1)} %get-tuple-element.39), channel_id=1, source_target_pairs={{0,7},{1,0},{2,1},{3,2},{4,3},{5,4},{6,5},{7,6},{8,15},{9,8},{10,9... | collective-permute-start | bytes 786440 | tf_op jit(solution)/shard_map/ppermute | solution.py:41
  (12 other events, 88.3 us)
Sparse Core Ops, SparseCore 0:
  13.2 29.3 all-gather.3
  71.4 44.2 reduce-scatter.2
  119.0 52.3 all-gather.5
  178.1 42.8 reduce-scatter.4

commit v3 on v2

--- a/solution.py
+++ b/solution.py
@@ -108,9 +108,11 @@
         term = jnp.dot(grad[g].T, q_all[g], preferred_element_type=jnp.float32)
         term = jnp.where(g == group_index, term, term.astype(jnp.bfloat16).astype(jnp.float32))
         code_terms = term if code_terms is None else code_terms + term
-    code_delta = lax.psum_scatter(
-        code_terms.astype(jnp.bfloat16), "member", scatter_dimension=0, tiled=True
-    ).astype(jnp.float32)
+    code_delta = jnp.sum(
+        exchange(code_terms.astype(jnp.bfloat16).reshape(members, queries_dev, emb_width), "member")
+        .astype(jnp.float32),
+        axis=0,
+    )
 
     dz_query = norm_back(query_delta, q_unit, q_inv)
     dz_code = norm_back(code_delta, c_unit, c_inv)
@@ -121,13 +123,14 @@
         "qe,de->qd", dz_code, projection, preferred_element_type=jnp.float32
     ).astype(jnp.bfloat16)
 
-    dz_all = lax.all_gather(jnp.stack([dz_query, dz_code], axis=0), "member", axis=0)
+    dz_all = shift_all(jnp.stack([dz_query, dz_code], axis=0), "member")
     proj_parts = jnp.einsum(
         "mtqgr,mtqe->gre", feat_cols, dz_all, preferred_element_type=jnp.float32
     )
-    projection_grad = lax.psum_scatter(
-        proj_parts, "group", scatter_dimension=0, tiled=True
-    ).reshape(rows_dev, emb_width)
+    proj_back = exchange(proj_parts.astype(jnp.bfloat16), "group").astype(jnp.float32)
+    projection_grad = jnp.take(proj_parts, group_index, axis=0) + jnp.sum(
+        jnp.where(own[:, None, None], 0.0, proj_back), axis=0
+    )
     return (query_grad, code_grad, projection_grad)
 
 

time: 230 us -> 250 us (1.087)
  waiting for transfers between devices: 119 us -> 79.6 us
  starting transfers between devices: 26.6 us -> 59.5 us
  local copies, waits for them, and re-layouts: 12.2 us -> 42.3 us
  matrix products: 42.9 us -> 36.1 us
  other arithmetic: 12.7 us -> 17.1 us
    reduce_scatter x2 -> x0, waiting for transfers between devices: 42.8 us -> none  [the longest x1 27.6 us: body(): lax.psum_scatter(proj_parts, 'group', scatter_dimension=0, tiled=True)]
    ppermute x10 -> x20, starting transfers between devices: 8.16 us -> 37 us  [exchange(): lax.ppermute(sent, axis, [(i, (i + s) % size) for i in range(size)])]
    ppermute x12 -> x19, waiting for transfers between devices: 19 us -> 39.6 us  [shift_all(): lax.ppermute(x, axis, [(i, (i + s) % size) for i in range(size)])]
    unnamed x28 -> x40, local copies, waits for them, and re-layouts: 4.65 us -> 20.2 us
    all_gather x1 -> x0, waiting for transfers between devices: 12.2 us -> none  [body(): lax.all_gather(jnp.stack([dz_query, dz_code], axis=0), 'member', axis=0)]
    gather x4 -> x5, local copies, waits for them, and re-layouts: 2.3 us -> 7.41 us  [shift_all(): jnp.take(jnp.stack(xs, axis=0), order, axis=0)]
    gather x2 -> x4, local copies, waits for them, and re-layouts: 2.78 us -> 7.29 us  [exchange(): return jnp.take(stacked, (index - jnp.arange(size)) % size, axis=0)]
    ppermute x10 -> x20, waiting for transfers between devices: 44.5 us -> 40 us  [exchange(): lax.ppermute(sent, axis, [(i, (i + s) % size) for i in range(size)])]
  transfers between devices with their start and end apart: 26 -> 40, of which waited for: 16 -> 13; matrix products, arithmetic and copies ran while one was open for 17% -> 25% of each run, Pallas kernels for 0% -> 0%
where the time goes in v3:
time: 250 us; the launch traced here: 249 us
  waiting for transfers between devices  79.6 us (32%)
  starting transfers between devices  59.5 us (24%)
  local copies, waits for them, and re-layouts  42.3 us (17%)
  matrix products  36.1 us (14%)
  other arithmetic  17.1 us (7%)
  between operations  14.7 us (6%)
    ppermute x20, waiting for transfers between devices, exchange(): lax.ppermute(sent, axis, [(i, (i + s) % size) for i in range(size)])  40 us
    ppermute x19, waiting for transfers between devices, shift_all(): lax.ppermute(x, axis, [(i, (i + s) % size) for i in range(size)])  39.6 us
    ppermute x20, starting transfers between devices, exchange(): lax.ppermute(sent, axis, [(i, (i + s) % size) for i in range(size)])  37 us
    ppermute x19, starting transfers between devices, shift_all(): lax.ppermute(x, axis, [(i, (i + s) % size) for i in range(size)])  22.4 us
    unnamed x40, local copies, waits for them, and re-layouts  20.2 us
    gather x5, local copies, waits for them, and re-layouts, shift_all(): jnp.take(jnp.stack(xs, axis=0), order, axis=0)  7.41 us
    gather x4, local copies, waits for them, and re-layouts, exchange(): return jnp.take(stacked, (index - jnp.arange(size)) % size, axis=0)  7.29 us
    dot_general x1, matrix products, body(): jnp.einsum('qe,de->qd', dz_code, projection, preferred_element_type=jnp.f...  7.24 us
  transfers between devices with their start and end apart: 40, of which 13 were waited for; matrix products, arithmetic and copies ran while one was open for 25% of the time, Pallas kernels for 0%

profile of v3, /device:TPU:3, one launch (start us, length us, event | category | flops | bytes accessed | tf_op | source)
XLA Modules:
  0.0 249.3 jit_solution(12497698446032475694)
XLA Ops:
  7.2 5.2 %multiply_reduce_fusion.3 = (f32[128]{0:T(128)S(1)}, f32[128,1024]{1,0:T(8,128)S(1)}) fusion(bf16[128,4096]{1,0:T(8,128)(2,1)} %param.15, bf16[4096,1024]{1,0:T(8,128)(2,1)} %param.17), kind=kOutput, calls=%fused_computation.53 | convolution fusion | flops 1074003840 | bytes 9961984 | tf_op jit(solution)/shard_map/dot_general | solution.py:14
  13.3 3.3 %collective-permute-start.8 = (bf16[128,1024]{1,0:T(8,128)(2,1)}, bf16[128,1024]{1,0:T(8,128)(2,1)}, u32[]{:S(2)}, u32[]{:S(2)}) collective-permute-start(bf16[128,1024]{1,0:T(8,128)(2,1)} %multiply_convert_fusion.4), channel_id=1, source_target_pairs={{0,24},{8,0},{16,8},{24,16},{1,25},{9,1},{17,9},{25,17},{2,26},{10... | collective-permute-start | bytes 786440 | tf_op jit(solution)/shard_map/ppermute | solution.py:30
  34.1 2.9 %collective-permute-start = (f32[128]{0:T(128)S(1)}, f32[128]{0:T(128)S(1)}, u32[]{:S(2)}, u32[]{:S(2)}) collective-permute-start(f32[128]{0:T(128)S(1)} %copy-done.8), channel_id=1, source_target_pairs={{0,8},{8,16},{16,24},{24,0},{1,9},{9,17},{17,25},{25,1},{2,10},{10... | collective-permute-start | bytes 1544 | tf_op jit(solution)/shard_map/ppermute | solution.py:30
  38.1 3.3 %collective-permute-start.22 = (bf16[2,128,4,128]{3,1,2,0:T(8,128)(2,1)S(1)}, bf16[2,128,4,128]{3,1,2,0:T(8,128)(2,1)S(1)}, u32[]{:S(2)}, u32[]{:S(2)}) collective-permute-start(bf16[2,128,4,128]{3,1,2,0:T(8,128)(2,1)S(1)} %get-tuple-element.58), channel_id=1, source_target_pairs={{0,1},{1,2},{2,3},{3,4},{4,5},{5,6},{6,7},{7,0},{8,9},{9,10},{10,1... | collective-permute-start | bytes 786440 | tf_op jit(solution)/shard_map/ppermute | solution.py:41
  43.3 7.1 %collective-permute-done.22 = bf16[2,128,4,128]{3,1,2,0:T(8,128)(2,1)S(1)} collective-permute-done((bf16[2,128,4,128]{3,1,2,0:T(8,128)(2,1)S(1)}, bf16[2,128,4,128]{3,1,2,0:T(8,128)(2,1)S(1)}, u32[]{:S(2)}, u32[]{:S(2)}) %collective-permute-start.22) | collective-permute-done | bytes 262176 | tf_op jit(solution)/shard_map/ppermute | solution.py:41
  50.4 2.6 %collective-permute-start.24 = (bf16[2,128,4,128]{3,1,2,0:T(8,128)(2,1)S(1)}, bf16[2,128,4,128]{3,1,2,0:T(8,128)(2,1)S(1)}, u32[]{:S(2)}, u32[]{:S(2)}) collective-permute-start(bf16[2,128,4,128]{3,1,2,0:T(8,128)(2,1)S(1)} %get-tuple-element.56), channel_id=1, source_target_pairs={{0,3},{1,4},{2,5},{3,6},{4,7},{5,0},{6,1},{7,2},{8,11},{9,12},{10,... | collective-permute-start | bytes 786440 | tf_op jit(solution)/shard_map/ppermute | solution.py:41
  53.7 4.8 %collective-permute-done.23 = bf16[2,128,4,128]{3,1,2,0:T(8,128)(2,1)S(1)} collective-permute-done((bf16[2,128,4,128]{3,1,2,0:T(8,128)(2,1)S(1)}, bf16[2,128,4,128]{3,1,2,0:T(8,128)(2,1)S(1)}, u32[]{:S(2)}, u32[]{:S(2)}) %collective-permute-start.23) | collective-permute-done | bytes 262176 | tf_op jit(solution)/shard_map/ppermute | solution.py:41
  60.2 6.0 %collective-permute-start.26 = (bf16[2,128,4,128]{3,1,2,0:T(8,128)(2,1)}, bf16[2,128,4,128]{3,1,2,0:T(8,128)(2,1)}, u32[]{:S(2)}, u32[]{:S(2)}) collective-permute-start(bf16[2,128,4,128]{3,1,2,0:T(8,128)(2,1)} %get-tuple-element.54), channel_id=1, source_target_pairs={{0,5},{1,6},{2,7},{3,0},{4,1},{5,2},{6,3},{7,4},{8,13},{9,14},{10,... | collective-permute-start | bytes 786440 | tf_op jit(solution)/shard_map/ppermute | solution.py:41
  79.6 3.3 %fusion.35 = (f32[4,128]{1,0:T(4,128)S(1)}, f32[4,128,1024]{2,1,0:T(8,128)S(1)}) fusion(bf16[4,128,1024]{2,1,0:T(8,128)(2,1)} %broadcast_select_fusion, bf16[1024,1024]{1,0:T(8,128)(2,1)} %all-gather.2.cloned.1.call-done, pred[4,1024]{1,0:T(4,128)(4,1)S(1)} %broadcast_in_dim.169), kind=kOutput, calls=%fused_computation.158 | convolution fusion | flops 1075314176 | bytes 5249024 | tf_op jit(solution)/shard_map/gqe,ke->gqk/dot_general | solution.py:78
  83.4 3.8 %collective-permute-start.11 = (f32[2,4,128]{2,1,0:T(4,128)S(1)}, f32[2,4,128]{2,1,0:T(4,128)S(1)}, u32[]{:S(2)}, u32[]{:S(2)}) collective-permute-start(f32[2,4,128]{2,1,0:T(4,128)S(1)} %get-tuple-element.77), channel_id=1, source_target_pairs={{0,24},{8,0},{16,8},{24,16},{1,25},{9,1},{17,9},{25,17},{2,26},{10... | collective-permute-start | bytes 12296 | tf_op jit(solution)/shard_map/ppermute | solution.py:30
  90.4 3.8 %gather_fusion.4 = bf16[8,2,128,4,128]{4,2,3,1,0:T(8,128)(2,1)} fusion(bf16[8,2,128,4,128]{4,2,3,1,0:T(8,128)(2,1)} %bitcast_dynamic-update-slice_fusion.8, s32[1024]{0:T(1024)S(1)} %pad_clamp_fusion), kind=kCustom, calls=%fused_computation.7 | custom fusion | bytes 4194336 | tf_op jit(solution)/shard_map/jit(_take)/gather | solution.py:43
  103.0 2.6 %fusion.36 = (bf16[4,128,1024]{2,1,0:T(8,128)(2,1)S(1)}, f32[4,128,1024]{2,1,0:T(8,128)}) fusion(bf16[4,128,1024]{2,1,0:T(8,128)(2,1)S(1)} %multiply_convert_fusion, bf16[1024,1024]{1,0:T(8,128)(2,1)S(1)} %copy-done.9), kind=kOutput, calls=%fused_computation.159 | convolution fusion | flops 1074266112 | bytes 6291456 | tf_op jit(solution)/shard_map/gqk,ke->gqe/dot_general | solution.py:101
  105.6 3.0 %collective-permute-start.14 = (bf16[128,1024]{1,0:T(8,128)(2,1)S(1)}, bf16[128,1024]{1,0:T(8,128)(2,1)S(1)}, u32[]{:S(2)}, u32[]{:S(2)}) collective-permute-start(bf16[128,1024]{1,0:T(8,128)(2,1)S(1)} %get-tuple-element.73), channel_id=1, source_target_pairs={{0,24},{8,0},{16,8},{24,16},{1,25},{9,1},{17,9},{25,17},{2,26},{10... | collective-permute-start | bytes 786440 | tf_op jit(solution)/shard_map/ppermute | solution.py:41
  115.6 7.5 %collective-permute-start.19 = (bf16[128,1024]{1,0:T(8,128)(2,1)}, bf16[128,1024]{1,0:T(8,128)(2,1)}, u32[]{:S(2)}, u32[]{:S(2)}) collective-permute-start(bf16[128,1024]{1,0:T(8,128)(2,1)} %get-tuple-element.62), channel_id=1, source_target_pairs={{0,5},{1,6},{2,7},{3,0},{4,1},{5,2},{6,3},{7,4},{8,13},{9,14},{10,... | collective-permute-start | bytes 786440 | tf_op jit(solution)/shard_map/ppermute | solution.py:41
  126.5 5.1 %collective-permute-done.13 = bf16[128,1024]{1,0:T(8,128)(2,1)S(1)} collective-permute-done((bf16[128,1024]{1,0:T(8,128)(2,1)S(1)}, bf16[128,1024]{1,0:T(8,128)(2,1)S(1)}, u32[]{:S(2)}, u32[]{:S(2)}) %collective-permute-start.13) | collective-permute-done | bytes 262176 | tf_op jit(solution)/shard_map/ppermute | solution.py:41
  132.8 2.9 %collective-permute-done.19 = bf16[128,1024]{1,0:T(8,128)(2,1)} collective-permute-done((bf16[128,1024]{1,0:T(8,128)(2,1)}, bf16[128,1024]{1,0:T(8,128)(2,1)}, u32[]{:S(2)}, u32[]{:S(2)}) %collective-permute-start.19) | collective-permute-done | bytes 262176 | tf_op jit(solution)/shard_map/ppermute | solution.py:41
  145.6 7.2 %convolution_convert_fusion.1 = bf16[128,4096]{1,0:T(8,128)(2,1)} fusion(bf16[128,1024]{1,0:T(8,128)(2,1)S(1)} %multiply_convert_fusion.2, bf16[4096,1024]{1,0:T(8,128)(2,1)} %param.17), kind=kOutput, calls=%fused_computation.10 | convolution fusion | flops 1074266112 | bytes 9699328 | tf_op jit(solution)/shard_map/qe,de->qd/dot_general | solution.py:119
  158.2 9.3 %collective-permute-done.30 = bf16[2,128,1024]{2,1,0:T(8,128)(2,1)S(1)} collective-permute-done((bf16[2,128,1024]{2,1,0:T(8,128)(2,1)S(1)}, bf16[2,128,1024]{2,1,0:T(8,128)(2,1)S(1)}, u32[]{:S(2)}, u32[]{:S(2)}) %collective-permute-start.30) | collective-permute-done | bytes 524320 | tf_op jit(solution)/shard_map/ppermute | solution.py:30
  171.3 26.4 %collective-permute-done.32 = bf16[2,128,1024]{2,1,0:T(8,128)(2,1)S(1)} collective-permute-done((bf16[2,128,1024]{2,1,0:T(8,128)(2,1)S(1)}, bf16[2,128,1024]{2,1,0:T(8,128)(2,1)S(1)}, u32[]{:S(2)}, u32[]{:S(2)}) %collective-permute-start.32) | collective-permute-done | bytes 524320 | tf_op jit(solution)/shard_map/ppermute | solution.py:30
  202.6 5.1 %gather_fusion.5 = bf16[8,2,128,1024]{3,2,1,0:T(8,128)(2,1)} fusion(bf16[8,2,128,1024]{3,2,1,0:T(8,128)(2,1)} %bitcast_dynamic-update-slice_fusion, s32[1024]{0:T(1024)S(1)} %pad_clamp_fusion), kind=kCustom, calls=%fused_computation.8 | custom fusion | bytes 8388640 | tf_op jit(solution)/shard_map/jit(_take)/gather | solution.py:32
  207.7 6.0 %fusion.37 = (bf16[4,128,1024]{2,1,0:T(8,128)(2,1)S(1)}, f32[4,128,1024]{2,1,0:T(8,128)}) fusion(bf16[8,2,128,1024]{3,2,1,0:T(8,128)(2,1)} %gather_fusion.5, pred[8]{0:T(512)(128)(4,1)S(1)} %compare_and_fusion, bf16[8,2,128,4,128]{4,2,3,1,0:T(8,128)(2,1)S(1)} %copy-done.4), kind=kOutput, calls=%fused_computation.160 | convolution fusion | flops 2151153664 | bytes 9437192 | tf_op jit(solution)/shard_map/mtqgr,mtqe->gre/dot_general | solution.py:127
  213.7 2.7 %collective-permute-start.38 = (bf16[128,1024]{1,0:T(8,128)(2,1)S(1)}, bf16[128,1024]{1,0:T(8,128)(2,1)S(1)}, u32[]{:S(2)}, u32[]{:S(2)}) collective-permute-start(bf16[128,1024]{1,0:T(8,128)(2,1)S(1)} %get-tuple-element.69), channel_id=1, source_target_pairs={{0,24},{8,0},{16,8},{24,16},{1,25},{9,1},{17,9},{25,17},{2,26},{10... | collective-permute-start | bytes 786440 | tf_op jit(solution)/shard_map/ppermute | solution.py:41
  216.8 7.2 %convolution_convert_fusion = bf16[128,4096]{1,0:T(8,128)(2,1)} fusion(bf16[128,1024]{1,0:T(8,128)(2,1)S(1)} %multiply_convert_fusion.1, bf16[4096,1024]{1,0:T(8,128)(2,1)} %param.17), kind=kOutput, calls=%fused_computation.9 | convolution fusion | flops 1074266112 | bytes 9699328 | tf_op jit(solution)/shard_map/qe,de->qd/dot_general | solution.py:122
  224.0 15.4 %collective-permute-done.37 = bf16[128,1024]{1,0:T(8,128)(2,1)S(1)} collective-permute-done((bf16[128,1024]{1,0:T(8,128)(2,1)S(1)}, bf16[128,1024]{1,0:T(8,128)(2,1)S(1)}, u32[]{:S(2)}, u32[]{:S(2)}) %collective-permute-start.37) | collective-permute-done | bytes 262176 | tf_op jit(solution)/shard_map/ppermute | solution.py:41
  (175 shorter events, 88.2 us)
Async XLA Ops:
  7.2 72.4 %all-gather.2.cloned.1.call-start = ((), (), s32[]{:S(2)}) async-start(), calls=%async_computation | async-start | bytes 2359296 | tf_op jit(solution)/shard_map/all_gather | solution.py:67
  13.3 56.9 %collective-permute-start.8 = (bf16[128,1024]{1,0:T(8,128)(2,1)}, bf16[128,1024]{1,0:T(8,128)(2,1)}, u32[]{:S(2)}, u32[]{:S(2)}) collective-permute-start(bf16[128,1024]{1,0:T(8,128)(2,1)} %multiply_convert_fusion.4), channel_id=1, source_target_pairs={{0,24},{8,0},{16,8},{24,16},{1,25},{9,1},{17,9},{25,17},{2,26},{10... | collective-permute-start | bytes 786440 | tf_op jit(solution)/shard_map/ppermute | solution.py:30
  16.6 53.6 %collective-permute-start.7 = (bf16[128,1024]{1,0:T(8,128)(2,1)}, bf16[128,1024]{1,0:T(8,128)(2,1)}, u32[]{:S(2)}, u32[]{:S(2)}) collective-permute-start(bf16[128,1024]{1,0:T(8,128)(2,1)} %multiply_convert_fusion.4), channel_id=1, source_target_pairs={{0,16},{8,24},{16,0},{24,8},{1,17},{9,25},{17,1},{25,9},{2,18},{10... | collective-permute-start | bytes 786440 | tf_op jit(solution)/shard_map/ppermute | solution.py:30
  16.6 15.2 %collective-permute-start.5 = (s32[16]{0:T(128)S(1)}, s32[16]{0:T(128)S(1)}, u32[]{:S(2)}, u32[]{:S(2)}) collective-permute-start(s32[16]{0:T(128)S(1)} %bitcast.225), channel_id=1, source_target_pairs={{0,24},{8,0},{16,8},{24,16},{1,25},{9,1},{17,9},{25,17},{2,26},{10... | collective-permute-start | bytes 200 | tf_op jit(solution)/shard_map/ppermute | solution.py:30
  16.8 16.9 %collective-permute-start.4 = (s32[16]{0:T(128)S(1)}, s32[16]{0:T(128)S(1)}, u32[]{:S(2)}, u32[]{:S(2)}) collective-permute-start(s32[16]{0:T(128)S(1)} %bitcast.226), channel_id=1, source_target_pairs={{0,16},{8,24},{16,0},{24,8},{1,17},{9,25},{17,1},{25,9},{2,18},{10... | collective-permute-start | bytes 200 | tf_op jit(solution)/shard_map/ppermute | solution.py:30
  18.9 15.2 %collective-permute-start.3 = (s32[16]{0:T(128)S(1)}, s32[16]{0:T(128)S(1)}, u32[]{:S(2)}, u32[]{:S(2)}) collective-permute-start(s32[16]{0:T(128)S(1)} %bitcast.227), channel_id=1, source_target_pairs={{0,8},{8,16},{16,24},{24,0},{1,9},{9,17},{17,25},{25,1},{2,10},{10... | collective-permute-start | bytes 200 | tf_op jit(solution)/shard_map/ppermute | solution.py:30
  38.0 32.2 %collective-permute-start.6 = (bf16[128,1024]{1,0:T(8,128)(2,1)}, bf16[128,1024]{1,0:T(8,128)(2,1)S(1)}, u32[]{:S(2)}, u32[]{:S(2)}) collective-permute-start(bf16[128,1024]{1,0:T(8,128)(2,1)} %multiply_convert_fusion.4), channel_id=1, source_target_pairs={{0,8},{8,16},{16,24},{24,0},{1,9},{9,17},{17,25},{25,1},{2,10},{10... | collective-permute-start | bytes 786440 | tf_op jit(solution)/shard_map/ppermute | solution.py:30
  41.4 17.0 %collective-permute-start.23 = (bf16[2,128,4,128]{3,1,2,0:T(8,128)(2,1)S(1)}, bf16[2,128,4,128]{3,1,2,0:T(8,128)(2,1)S(1)}, u32[]{:S(2)}, u32[]{:S(2)}) collective-permute-start(bf16[2,128,4,128]{3,1,2,0:T(8,128)(2,1)S(1)} %get-tuple-element.57), channel_id=1, source_target_pairs={{0,2},{1,3},{2,4},{3,5},{4,6},{5,7},{6,0},{7,1},{8,10},{9,11},{10,... | collective-permute-start | bytes 786440 | tf_op jit(solution)/shard_map/ppermute | solution.py:41
  60.2 12.6 %collective-permute-start.26 = (bf16[2,128,4,128]{3,1,2,0:T(8,128)(2,1)}, bf16[2,128,4,128]{3,1,2,0:T(8,128)(2,1)}, u32[]{:S(2)}, u32[]{:S(2)}) collective-permute-start(bf16[2,128,4,128]{3,1,2,0:T(8,128)(2,1)} %get-tuple-element.54), channel_id=1, source_target_pairs={{0,5},{1,6},{2,7},{3,0},{4,1},{5,2},{6,3},{7,4},{8,13},{9,14},{10,... | collective-permute-start | bytes 786440 | tf_op jit(solution)/shard_map/ppermute | solution.py:41
  70.2 18.5 %collective-permute-start.28 = (bf16[2,128,4,128]{3,1,2,0:T(8,128)(2,1)S(1)}, bf16[2,128,4,128]{3,1,2,0:T(8,128)(2,1)}, u32[]{:S(2)}, u32[]{:S(2)}) collective-permute-start(bf16[2,128,4,128]{3,1,2,0:T(8,128)(2,1)S(1)} %get-tuple-element.52), channel_id=1, source_target_pairs={{0,7},{1,0},{2,1},{3,2},{4,3},{5,4},{6,5},{7,6},{8,15},{9,8},{10,9... | collective-permute-start | bytes 786440 | tf_op jit(solution)/shard_map/ppermute | solution.py:41
  105.6 20.8 %collective-permute-start.14 = (bf16[128,1024]{1,0:T(8,128)(2,1)S(1)}, bf16[128,1024]{1,0:T(8,128)(2,1)S(1)}, u32[]{:S(2)}, u32[]{:S(2)}) collective-permute-start(bf16[128,1024]{1,0:T(8,128)(2,1)S(1)} %get-tuple-element.73), channel_id=1, source_target_pairs={{0,24},{8,0},{16,8},{24,16},{1,25},{9,1},{17,9},{25,17},{2,26},{10... | collective-permute-start | bytes 786440 | tf_op jit(solution)/shard_map/ppermute | solution.py:41
  108.6 23.0 %collective-permute-start.13 = (bf16[128,1024]{1,0:T(8,128)(2,1)S(1)}, bf16[128,1024]{1,0:T(8,128)(2,1)S(1)}, u32[]{:S(2)}, u32[]{:S(2)}) collective-permute-start(bf16[128,1024]{1,0:T(8,128)(2,1)S(1)} %get-tuple-element.74), channel_id=1, source_target_pairs={{0,16},{8,24},{16,0},{24,8},{1,17},{9,25},{17,1},{25,9},{2,18},{10... | collective-permute-start | bytes 786440 | tf_op jit(solution)/shard_map/ppermute | solution.py:41
  109.2 22.5 %collective-permute-start.12 = (bf16[128,1024]{1,0:T(8,128)(2,1)S(1)}, bf16[128,1024]{1,0:T(8,128)(2,1)S(1)}, u32[]{:S(2)}, u32[]{:S(2)}) collective-permute-start(bf16[128,1024]{1,0:T(8,128)(2,1)S(1)} %get-tuple-element.75), channel_id=1, source_target_pairs={{0,8},{8,16},{16,24},{24,0},{1,9},{9,17},{17,25},{25,1},{2,10},{10... | collective-permute-start | bytes 786440 | tf_op jit(solution)/shard_map/ppermute | solution.py:41
  115.6 20.0 %collective-permute-start.19 = (bf16[128,1024]{1,0:T(8,128)(2,1)}, bf16[128,1024]{1,0:T(8,128)(2,1)}, u32[]{:S(2)}, u32[]{:S(2)}) collective-permute-start(bf16[128,1024]{1,0:T(8,128)(2,1)} %get-tuple-element.62), channel_id=1, source_target_pairs={{0,5},{1,6},{2,7},{3,0},{4,1},{5,2},{6,3},{7,4},{8,13},{9,14},{10,... | collective-permute-start | bytes 786440 | tf_op jit(solution)/shard_map/ppermute | solution.py:41
  123.8 13.5 %collective-permute-start.20 = (bf16[128,1024]{1,0:T(8,128)(2,1)S(1)}, bf16[128,1024]{1,0:T(8,128)(2,1)}, u32[]{:S(2)}, u32[]{:S(2)}) collective-permute-start(bf16[128,1024]{1,0:T(8,128)(2,1)S(1)} %get-tuple-element.61), channel_id=1, source_target_pairs={{0,6},{1,7},{2,0},{3,1},{4,2},{5,3},{6,4},{7,5},{8,14},{9,15},{10,... | collective-permute-start | bytes 786440 | tf_op jit(solution)/shard_map/ppermute | solution.py:41
  126.5 12.9 %collective-permute-start.21 = (bf16[128,1024]{1,0:T(8,128)(2,1)}, bf16[128,1024]{1,0:T(8,128)(2,1)}, u32[]{:S(2)}, u32[]{:S(2)}) collective-permute-start(bf16[128,1024]{1,0:T(8,128)(2,1)} %get-tuple-element.60), channel_id=1, source_target_pairs={{0,7},{1,0},{2,1},{3,2},{4,3},{5,4},{6,5},{7,6},{8,15},{9,8},{10,9... | collective-permute-start | bytes 786440 | tf_op jit(solution)/shard_map/ppermute | solution.py:41
  145.1 22.4 %collective-permute-start.30 = (bf16[2,128,1024]{2,1,0:T(8,128)(2,1)S(1)}, bf16[2,128,1024]{2,1,0:T(8,128)(2,1)S(1)}, u32[]{:S(2)}, u32[]{:S(2)}) collective-permute-start(bf16[2,128,1024]{2,1,0:T(8,128)(2,1)S(1)} %pad_maximum_fusion.3), channel_id=1, source_target_pairs={{0,2},{1,3},{2,4},{3,5},{4,6},{5,7},{6,0},{7,1},{8,10},{9,11},{10,... | collective-permute-start | bytes 1572872 | tf_op jit(solution)/shard_map/ppermute | solution.py:30
  152.9 17.6 %collective-permute-start.31 = (bf16[2,128,1024]{2,1,0:T(8,128)(2,1)S(1)}, bf16[2,128,1024]{2,1,0:T(8,128)(2,1)S(1)}, u32[]{:S(2)}, u32[]{:S(2)}) collective-permute-start(bf16[2,128,1024]{2,1,0:T(8,128)(2,1)S(1)} %pad_maximum_fusion.3), channel_id=1, source_target_pairs={{0,3},{1,4},{2,5},{3,6},{4,7},{5,0},{6,1},{7,2},{8,11},{9,12},{10,... | collective-permute-start | bytes 1572872 | tf_op jit(solution)/shard_map/ppermute | solution.py:30
  153.7 44.0 %collective-permute-start.32 = (bf16[2,128,1024]{2,1,0:T(8,128)(2,1)S(1)}, bf16[2,128,1024]{2,1,0:T(8,128)(2,1)S(1)}, u32[]{:S(2)}, u32[]{:S(2)}) collective-permute-start(bf16[2,128,1024]{2,1,0:T(8,128)(2,1)S(1)} %pad_maximum_fusion.3), channel_id=1, source_target_pairs={{0,4},{1,5},{2,6},{3,7},{4,0},{5,1},{6,2},{7,3},{8,12},{9,13},{10,... | collective-permute-start | bytes 1572872 | tf_op jit(solution)/shard_map/ppermute | solution.py:30
  155.0 45.1 %collective-permute-start.33 = (bf16[2,128,1024]{2,1,0:T(8,128)(2,1)S(1)}, bf16[2,128,1024]{2,1,0:T(8,128)(2,1)S(1)}, u32[]{:S(2)}, u32[]{:S(2)}) collective-permute-start(bf16[2,128,1024]{2,1,0:T(8,128)(2,1)S(1)} %pad_maximum_fusion.3), channel_id=1, source_target_pairs={{0,5},{1,6},{2,7},{3,0},{4,1},{5,2},{6,3},{7,4},{8,13},{9,14},{10,... | collective-permute-start | bytes 1572872 | tf_op jit(solution)/shard_map/ppermute | solution.py:30
  156.2 44.6 %collective-permute-start.34 = (bf16[2,128,1024]{2,1,0:T(8,128)(2,1)S(1)}, bf16[2,128,1024]{2,1,0:T(8,128)(2,1)S(1)}, u32[]{:S(2)}, u32[]{:S(2)}) collective-permute-start(bf16[2,128,1024]{2,1,0:T(8,128)(2,1)S(1)} %pad_maximum_fusion.3), channel_id=1, source_target_pairs={{0,6},{1,7},{2,0},{3,1},{4,2},{5,3},{6,4},{7,5},{8,14},{9,15},{10,... | collective-permute-start | bytes 1572872 | tf_op jit(solution)/shard_map/ppermute | solution.py:30
  167.5 34.2 %collective-permute-start.35 = (bf16[2,128,1024]{2,1,0:T(8,128)(2,1)S(1)}, bf16[2,128,1024]{2,1,0:T(8,128)(2,1)S(1)}, u32[]{:S(2)}, u32[]{:S(2)}) collective-permute-start(bf16[2,128,1024]{2,1,0:T(8,128)(2,1)S(1)} %pad_maximum_fusion.3), channel_id=1, source_target_pairs={{0,7},{1,0},{2,1},{3,2},{4,3},{5,4},{6,5},{7,6},{8,15},{9,8},{10,9... | collective-permute-start | bytes 1572872 | tf_op jit(solution)/shard_map/ppermute | solution.py:30
  216.4 23.0 %collective-permute-start.37 = (bf16[128,1024]{1,0:T(8,128)(2,1)S(1)}, bf16[128,1024]{1,0:T(8,128)(2,1)S(1)}, u32[]{:S(2)}, u32[]{:S(2)}) collective-permute-start(bf16[128,1024]{1,0:T(8,128)(2,1)S(1)} %get-tuple-element.70), channel_id=1, source_target_pairs={{0,16},{8,24},{16,0},{24,8},{1,17},{9,25},{17,1},{25,9},{2,18},{10... | collective-permute-start | bytes 786440 | tf_op jit(solution)/shard_map/ppermute | solution.py:41
  216.4 23.0 %collective-permute-start.36 = (bf16[128,1024]{1,0:T(8,128)(2,1)S(1)}, bf16[128,1024]{1,0:T(8,128)(2,1)S(1)}, u32[]{:S(2)}, u32[]{:S(2)}) collective-permute-start(bf16[128,1024]{1,0:T(8,128)(2,1)S(1)} %get-tuple-element.71), channel_id=1, source_target_pairs={{0,8},{8,16},{16,24},{24,0},{1,9},{9,17},{17,25},{25,1},{2,10},{10... | collective-permute-start | bytes 786440 | tf_op jit(solution)/shard_map/ppermute | solution.py:41
  (26 other events, 199.2 us)
Sparse Core Ops, SparseCore 0:
  22.8 32.9 all-gather.1

commit v4 on v2

--- a/solution.py
+++ b/solution.py
@@ -121,13 +121,16 @@
         "qe,de->qd", dz_code, projection, preferred_element_type=jnp.float32
     ).astype(jnp.bfloat16)
 
-    dz_all = lax.all_gather(jnp.stack([dz_query, dz_code], axis=0), "member", axis=0)
+    dzq_all = shift_all(dz_query, "member")
+    dzc_all = lax.all_gather(dz_code, "member", axis=0)
     proj_parts = jnp.einsum(
-        "mtqgr,mtqe->gre", feat_cols, dz_all, preferred_element_type=jnp.float32
-    )
-    projection_grad = lax.psum_scatter(
-        proj_parts, "group", scatter_dimension=0, tiled=True
-    ).reshape(rows_dev, emb_width)
+        "mqgr,mqe->gre", feat_cols[:, 0], dzq_all, preferred_element_type=jnp.float32
+    ) + jnp.einsum("mqgr,mqe->gre", feat_cols[:, 1], dzc_all, preferred_element_type=jnp.float32)
+    own_proj = jnp.take(proj_parts, group_index, axis=0)
+    sent_proj = jnp.where(own[:, None, None], 0.0, proj_parts).astype(jnp.bfloat16)
+    projection_grad = own_proj + lax.psum_scatter(
+        sent_proj, "group", scatter_dimension=0, tiled=True
+    ).reshape(rows_dev, emb_width).astype(jnp.float32)
     return (query_grad, code_grad, projection_grad)
 
 

time: 230 us -> 250 us (1.087)
  waiting for transfers between devices: 119 us -> 92.3 us
  local copies, waits for them, and re-layouts: 12.2 us -> 36.1 us
  starting transfers between devices: 26.6 us -> 39.1 us
  other arithmetic: 12.7 us -> 23.3 us
    ppermute x10, waiting for transfers between devices: 44.5 us -> 26.4 us  [exchange(): lax.ppermute(sent, axis, [(i, (i + s) % size) for i in range(size)])]
    ppermute x12 -> x19, waiting for transfers between devices: 19 us -> 37 us  [shift_all(): lax.ppermute(x, axis, [(i, (i + s) % size) for i in range(size)])]
    reduce_scatter x1, waiting for transfers between devices: 27.6 us -> 11.4 us  [body(): lax.psum_scatter(sent_proj, 'group', scatter_dimension=0, tiled=True)]
    unnamed x28 -> x40, local copies, waits for them, and re-layouts: 4.65 us -> 17.2 us
    all_gather x1, waiting for transfers between devices: 12.2 us -> 0.01 us  [body(): dzc_all = lax.all_gather(dz_code, 'member', axis=0)]
    ppermute x12 -> x19, starting transfers between devices: 18.3 us -> 25.3 us  [shift_all(): lax.ppermute(x, axis, [(i, (i + s) % size) for i in range(size)])]
    ppermute x10, starting transfers between devices: 8.16 us -> 13.7 us  [exchange(): lax.ppermute(sent, axis, [(i, (i + s) % size) for i in range(size)])]
    gather x2 -> x3, local copies, waits for them, and re-layouts: 2.78 us -> 7.98 us  [exchange(): return jnp.take(stacked, (index - jnp.arange(size)) % size, axis=0)]
  transfers between devices with their start and end apart: 26 -> 33, of which waited for: 16 -> 17; matrix products, arithmetic and copies ran while one was open for 17% -> 30% of each run, Pallas kernels for 0% -> 0%
where the time goes in v4:
time: 250 us; the launch traced here: 248 us
  waiting for transfers between devices  92.3 us (37%)
  matrix products  42.4 us (17%)
  starting transfers between devices  39.1 us (16%)
  local copies, waits for them, and re-layouts  36.1 us (14%)
  other arithmetic  23.3 us (9%)
  between operations  14.3 us (6%)
    ppermute x19, waiting for transfers between devices, shift_all(): lax.ppermute(x, axis, [(i, (i + s) % size) for i in range(size)])  37 us
    ppermute x10, waiting for transfers between devices, exchange(): lax.ppermute(sent, axis, [(i, (i + s) % size) for i in range(size)])  26.4 us
    ppermute x19, starting transfers between devices, shift_all(): lax.ppermute(x, axis, [(i, (i + s) % size) for i in range(size)])  25.3 us
    reduce_scatter x1, waiting for transfers between devices, body(): lax.psum_scatter(code_terms.astype(jnp.bfloat16), 'member', scatter_dimen...  17.4 us
    unnamed x40, local copies, waits for them, and re-layouts  17.2 us
    ppermute x10, starting transfers between devices, exchange(): lax.ppermute(sent, axis, [(i, (i + s) % size) for i in range(size)])  13.7 us
    reduce_scatter x1, waiting for transfers between devices, body(): lax.psum_scatter(sent_proj, 'group', scatter_dimension=0, tiled=True)  11.4 us
    dot_general x2, matrix products, embed(): values = jnp.dot(features, projection, preferred_element_type=jnp.float32)  9.77 us
  transfers between devices with their start and end apart: 33, of which 17 were waited for; matrix products, arithmetic and copies ran while one was open for 30% of the time, Pallas kernels for 0%

profile of v4, /device:TPU:3, one launch (start us, length us, event | category | flops | bytes accessed | tf_op | source)
XLA Modules:
  0.0 247.5 jit_solution(1422582305362658616)
XLA Ops:
  7.2 5.1 %multiply_reduce_fusion.1 = (f32[128]{0:T(128)S(1)}, f32[128,1024]{1,0:T(8,128)S(1)}) fusion(bf16[128,4096]{1,0:T(8,128)(2,1)} %param.14, bf16[4096,1024]{1,0:T(8,128)(2,1)} %param.15), kind=kOutput, calls=%fused_computation.43 | convolution fusion | flops 1074003840 | bytes 9961984 | tf_op jit(solution)/shard_map/dot_general | solution.py:14
  13.6 4.7 %multiply_reduce_fusion.2 = (f32[128]{0:T(128)S(1)}, f32[128,1024]{1,0:T(8,128)S(1)}) fusion(bf16[128,4096]{1,0:T(8,128)(2,1)S(1)} %copy-done.1, bf16[4096,1024]{1,0:T(8,128)(2,1)} %param.15), kind=kOutput, calls=%fused_computation.44 | convolution fusion | flops 1074003840 | bytes 9961984 | tf_op jit(solution)/shard_map/dot_general | solution.py:14
  18.4 3.4 %collective-permute-start.8 = (bf16[128,1024]{1,0:T(8,128)(2,1)S(1)}, bf16[128,1024]{1,0:T(8,128)(2,1)S(1)}, u32[]{:S(2)}, u32[]{:S(2)}) collective-permute-start(bf16[128,1024]{1,0:T(8,128)(2,1)S(1)} %multiply_convert_fusion.3), channel_id=1, source_target_pairs={{0,24},{8,0},{16,8},{24,16},{1,25},{9,1},{17,9},{25,17},{2,26},{10... | collective-permute-start | bytes 786440 | tf_op jit(solution)/shard_map/ppermute | solution.py:30
  22.3 2.8 %collective-permute-start.5 = (s32[16]{0:T(128)S(1)}, s32[16]{0:T(128)S(1)}, u32[]{:S(2)}, u32[]{:S(2)}) collective-permute-start(s32[16]{0:T(128)S(1)} %bitcast.190), channel_id=1, source_target_pairs={{0,24},{8,0},{16,8},{24,16},{1,25},{9,1},{17,9},{25,17},{2,26},{10... | collective-permute-start | bytes 200 | tf_op jit(solution)/shard_map/ppermute | solution.py:30
  26.8 11.4 %collective-permute-done.5 = s32[16]{0:T(128)S(1)} collective-permute-done((s32[16]{0:T(128)S(1)}, s32[16]{0:T(128)S(1)}, u32[]{:S(2)}, u32[]{:S(2)}) %collective-permute-start.5) | collective-permute-done | bytes 96 | tf_op jit(solution)/shard_map/ppermute | solution.py:30
  38.2 5.3 %collective-permute-start.3 = (s32[16]{0:T(128)S(1)}, s32[16]{0:T(128)S(1)}, u32[]{:S(2)}, u32[]{:S(2)}) collective-permute-start(s32[16]{0:T(128)S(1)} %bitcast.192), channel_id=1, source_target_pairs={{0,8},{8,16},{16,24},{24,0},{1,9},{9,17},{17,25},{25,1},{2,10},{10... | collective-permute-start | bytes 200 | tf_op jit(solution)/shard_map/ppermute | solution.py:30
  43.6 3.4 %collective-permute-start.2 = (f32[128]{0:T(128)S(1)}, f32[128]{0:T(128)S(1)}, u32[]{:S(2)}, u32[]{:S(2)}) collective-permute-start(f32[128]{0:T(128)S(1)} %copy-done.12), channel_id=1, source_target_pairs={{0,24},{8,0},{16,8},{24,16},{1,25},{9,1},{17,9},{25,17},{2,26},{10... | collective-permute-start | bytes 1544 | tf_op jit(solution)/shard_map/ppermute | solution.py:30
  54.7 3.3 %fusion.33 = (f32[4,128]{1,0:T(4,128)S(1)}, f32[4,128,1024]{2,1,0:T(8,128)S(1)}) fusion(bf16[4,128,1024]{2,1,0:T(8,128)(2,1)} %broadcast_select_fusion.1, bf16[1024,1024]{1,0:T(8,128)(2,1)} %all-gather.4.cloned.1.call-done, pred[4,1024]{1,0:T(4,128)(4,1)S(1)} %broadcast_in_dim.150), kind=kOutput, calls=%fused_computation.138 | convolution fusion | flops 1075314176 | bytes 5249024 | tf_op jit(solution)/shard_map/gqe,ke->gqk/dot_general | solution.py:78
  80.4 6.4 %collective-permute-start.15 = (bf16[2,128,4,128]{3,1,2,0:T(8,128)(2,1)S(1)}, bf16[2,128,4,128]{3,1,2,0:T(8,128)(2,1)S(1)}, u32[]{:S(2)}, u32[]{:S(2)}) collective-permute-start(bf16[2,128,4,128]{3,1,2,0:T(8,128)(2,1)S(1)} %get-tuple-element.48), channel_id=1, source_target_pairs={{0,1},{1,2},{2,3},{3,4},{4,5},{5,6},{6,7},{7,0},{8,9},{9,10},{10,1... | collective-permute-start | bytes 786440 | tf_op jit(solution)/shard_map/ppermute | solution.py:41
  93.4 7.8 %collective-permute-done.16 = bf16[2,128,4,128]{3,1,2,0:T(8,128)(2,1)S(1)} collective-permute-done((bf16[2,128,4,128]{3,1,2,0:T(8,128)(2,1)S(1)}, bf16[2,128,4,128]{3,1,2,0:T(8,128)(2,1)S(1)}, u32[]{:S(2)}, u32[]{:S(2)}) %collective-permute-start.16) | collective-permute-done | bytes 262176 | tf_op jit(solution)/shard_map/ppermute | solution.py:41
  111.0 17.4 %reduce-scatter.3.cloned.1.call-done = bf16[128,1024]{1,0:T(8,128)(2,1)} async-done(((bf16[1024,1024]{1,0:T(8,128)(2,1)}), bf16[128,1024]{1,0:T(8,128)(2,1)}) %reduce-scatter.3.cloned.1.call-update) | async-done | bytes 262160 | tf_op jit(solution)/shard_map/reduce_scatter | solution.py:111
  131.5 4.2 %fusion.34 = (bf16[4,128,1024]{2,1,0:T(8,128)(2,1)S(1)}, f32[4,128,1024]{2,1,0:T(8,128)}) fusion(bf16[4,128,1024]{2,1,0:T(8,128)(2,1)S(1)} %copy-done.4, bf16[1024,1024]{1,0:T(8,128)(2,1)} %all-gather.4.cloned.1.call-done), kind=kOutput, calls=%fused_computation.139 | convolution fusion | flops 1074266112 | bytes 6291456 | tf_op jit(solution)/shard_map/gqk,ke->gqe/dot_general | solution.py:101
  136.6 3.1 %collective-permute-start.14 = (bf16[128,1024]{1,0:T(8,128)(2,1)}, bf16[128,1024]{1,0:T(8,128)(2,1)}, u32[]{:S(2)}, u32[]{:S(2)}) collective-permute-start(bf16[128,1024]{1,0:T(8,128)(2,1)} %get-tuple-element.51), channel_id=1, source_target_pairs={{0,24},{8,0},{16,8},{24,16},{1,25},{9,1},{17,9},{25,17},{2,26},{10... | collective-permute-start | bytes 786440 | tf_op jit(solution)/shard_map/ppermute | solution.py:41
  144.4 3.0 %copy.29 = bf16[8,2,128,4,128]{2,4,0,3,1:T(8,128)(2,1)S(1)} copy(bf16[8,2,128,4,128]{4,2,3,1,0:T(8,128)(2,1)} %gather_fusion.3) | data formatting | bytes 4194304 | tf_op jit(solution)/shard_map/jit(_take)/gather | solution.py:43
  147.4 14.3 %collective-permute-done.13 = bf16[128,1024]{1,0:T(8,128)(2,1)} collective-permute-done((bf16[128,1024]{1,0:T(8,128)(2,1)}, bf16[128,1024]{1,0:T(8,128)(2,1)}, u32[]{:S(2)}, u32[]{:S(2)}) %collective-permute-start.13) | collective-permute-done | bytes 262176 | tf_op jit(solution)/shard_map/ppermute | solution.py:41
  164.0 2.8 %gather_fusion.6 = bf16[4,128,1024]{2,1,0:T(8,128)(2,1)} fusion(bf16[4,128,1024]{2,1,0:T(8,128)(2,1)} %pad_maximum_fusion.1, s32[1024]{0:T(1024)S(1)} %pad_clamp_fusion.1), kind=kCustom, calls=%fused_computation.1.clone | custom fusion | bytes 2097168 | tf_op jit(solution)/shard_map/jit(_take)/gather | solution.py:43
  181.4 5.1 %collective-permute-done.23 = bf16[128,1024]{1,0:T(8,128)(2,1)S(1)} collective-permute-done((bf16[128,1024]{1,0:T(8,128)(2,1)S(1)}, bf16[128,1024]{1,0:T(8,128)(2,1)S(1)}, u32[]{:S(2)}, u32[]{:S(2)}) %collective-permute-start.23) | collective-permute-done | bytes 262176 | tf_op jit(solution)/shard_map/ppermute | solution.py:30
  188.4 10.7 %collective-permute-done.25 = bf16[128,1024]{1,0:T(8,128)(2,1)S(1)} collective-permute-done((bf16[128,1024]{1,0:T(8,128)(2,1)S(1)}, bf16[128,1024]{1,0:T(8,128)(2,1)S(1)}, u32[]{:S(2)}, u32[]{:S(2)}) %collective-permute-start.25) | collective-permute-done | bytes 262176 | tf_op jit(solution)/shard_map/ppermute | solution.py:30
  203.3 3.8 %gather_fusion.4 = bf16[8,128,1024]{2,1,0:T(8,128)(2,1)} fusion(bf16[8,128,1024]{2,1,0:T(8,128)(2,1)} %bitcast_dynamic-update-slice_fusion, s32[1024]{0:T(1024)S(1)} %pad_clamp_fusion), kind=kCustom, calls=%fused_computation.6 | custom fusion | bytes 4194336 | tf_op jit(solution)/shard_map/jit(_take)/gather | solution.py:32
  207.1 3.0 %fusion.12 = f32[4,128,1024,1]{2,1,3,0:T(8,128)S(1)} fusion(bf16[8,128,1024,1]{2,1,0,3:T(8,128)(2,1)} %bitcast.200, bf16[8,2,128,4,128]{2,4,0,3,1:T(8,128)(2,1)S(1)} %copy-done.8), kind=kOutput, calls=%fused_computation.27 | convolution fusion | flops 1073741824 | bytes 5242880 | tf_op jit(solution)/shard_map/mqgr,mqe->gre/dot_general | solution.py:128
  210.1 3.0 %select_convert_fusion = (bf16[4,128,1024]{2,1,0:T(8,128)(2,1)}, f32[4,128,1024]{2,1,0:T(8,128)}) fusion(pred[4]{0:T(512)(128)(4,1)S(1)} %get-tuple-element.67, f32[4,128,1024,1]{2,1,3,0:T(8,128)S(1)} %fusion.12, bf16[8,128,1024]{2,1,0:T(8,128)(2,1)S(1)} %copy-done.9, pred[8]{0:T(512)(128)(4,1)S(1)} %compare_and_fusion, ...), kind=kOutput, calls=%fused_computation.18 | convolution fusion | flops 1075838976 | bytes 8389632 | tf_op jit(solution)/shard_map/mqgr,mqe->gre/dot_general | solution.py:126
  213.2 7.3 %convolution_convert_fusion.1 = bf16[128,4096]{1,0:T(8,128)(2,1)} fusion(bf16[128,1024]{1,0:T(8,128)(2,1)S(1)} %get-tuple-element.41, bf16[4096,1024]{1,0:T(8,128)(2,1)} %param.15), kind=kOutput, calls=%fused_computation.8 | convolution fusion | flops 1074266112 | bytes 9699328 | tf_op jit(solution)/shard_map/qe,de->qd/dot_general | solution.py:117
  220.4 7.2 %convolution_convert_fusion = bf16[128,4096]{1,0:T(8,128)(2,1)} fusion(bf16[128,1024]{1,0:T(8,128)(2,1)S(1)} %copy-done.7, bf16[4096,1024]{1,0:T(8,128)(2,1)} %param.15), kind=kOutput, calls=%fused_computation.7 | convolution fusion | flops 1074266112 | bytes 9699328 | tf_op jit(solution)/shard_map/qe,de->qd/dot_general | solution.py:120
  227.7 11.4 %reduce-scatter.5.cloned.1.call-done = bf16[1,128,1024]{2,1,0:T(8,128)(2,1)} async-done(((bf16[4,128,1024]{2,1,0:T(8,128)(2,1)}), bf16[1,128,1024]{2,1,0:T(8,128)(2,1)}) %reduce-scatter.5.cloned.1.call-update) | async-done | bytes 262160 | tf_op jit(solution)/shard_map/reduce_scatter | solution.py:131
  (157 shorter events, 83.1 us)
Async XLA Ops:
  7.2 47.5 %all-gather.4.cloned.1.call-start = ((), (), s32[]{:S(2)}) async-start(), calls=%async_computation.2 | async-start | bytes 2359296 | tf_op jit(solution)/shard_map/all_gather | solution.py:67
  13.1 115.3 %reduce-scatter.3.cloned.1.call-start = ((), (), s32[]{:S(2)}) async-start(), calls=%async_computation.3 | async-start | bytes 2359296 | tf_op jit(solution)/shard_map/reduce_scatter | solution.py:111
  18.4 34.3 %collective-permute-start.8 = (bf16[128,1024]{1,0:T(8,128)(2,1)S(1)}, bf16[128,1024]{1,0:T(8,128)(2,1)S(1)}, u32[]{:S(2)}, u32[]{:S(2)}) collective-permute-start(bf16[128,1024]{1,0:T(8,128)(2,1)S(1)} %multiply_convert_fusion.3), channel_id=1, source_target_pairs={{0,24},{8,0},{16,8},{24,16},{1,25},{9,1},{17,9},{25,17},{2,26},{10... | collective-permute-start | bytes 786440 | tf_op jit(solution)/shard_map/ppermute | solution.py:30
  21.8 31.0 %collective-permute-start.7 = (bf16[128,1024]{1,0:T(8,128)(2,1)S(1)}, bf16[128,1024]{1,0:T(8,128)(2,1)S(1)}, u32[]{:S(2)}, u32[]{:S(2)}) collective-permute-start(bf16[128,1024]{1,0:T(8,128)(2,1)S(1)} %multiply_convert_fusion.3), channel_id=1, source_target_pairs={{0,16},{8,24},{16,0},{24,8},{1,17},{9,25},{17,1},{25,9},{2,18},{10... | collective-permute-start | bytes 786440 | tf_op jit(solution)/shard_map/ppermute | solution.py:30
  21.8 31.0 %collective-permute-start.6 = (bf16[128,1024]{1,0:T(8,128)(2,1)S(1)}, bf16[128,1024]{1,0:T(8,128)(2,1)S(1)}, u32[]{:S(2)}, u32[]{:S(2)}) collective-permute-start(bf16[128,1024]{1,0:T(8,128)(2,1)S(1)} %multiply_convert_fusion.3), channel_id=1, source_target_pairs={{0,8},{8,16},{16,24},{24,0},{1,9},{9,17},{17,25},{25,1},{2,10},{10... | collective-permute-start | bytes 786440 | tf_op jit(solution)/shard_map/ppermute | solution.py:30
  22.3 15.9 %collective-permute-start.5 = (s32[16]{0:T(128)S(1)}, s32[16]{0:T(128)S(1)}, u32[]{:S(2)}, u32[]{:S(2)}) collective-permute-start(s32[16]{0:T(128)S(1)} %bitcast.190), channel_id=1, source_target_pairs={{0,24},{8,0},{16,8},{24,16},{1,25},{9,1},{17,9},{25,17},{2,26},{10... | collective-permute-start | bytes 200 | tf_op jit(solution)/shard_map/ppermute | solution.py:30
  25.1 18.5 %collective-permute-start.4 = (s32[16]{0:T(128)S(1)}, s32[16]{0:T(128)S(1)}, u32[]{:S(2)}, u32[]{:S(2)}) collective-permute-start(s32[16]{0:T(128)S(1)} %bitcast.191), channel_id=1, source_target_pairs={{0,16},{8,24},{16,0},{24,8},{1,17},{9,25},{17,1},{25,9},{2,18},{10... | collective-permute-start | bytes 200 | tf_op jit(solution)/shard_map/ppermute | solution.py:30
  71.3 135.8 %all-gather.6.cloned.1.call-start = ((), (), s32[]{:S(2)}) async-start(), calls=%async_computation.5 | async-start | bytes 2359296 | tf_op jit(solution)/shard_map/all_gather | solution.py:125
  80.4 12.0 %collective-permute-start.15 = (bf16[2,128,4,128]{3,1,2,0:T(8,128)(2,1)S(1)}, bf16[2,128,4,128]{3,1,2,0:T(8,128)(2,1)S(1)}, u32[]{:S(2)}, u32[]{:S(2)}) collective-permute-start(bf16[2,128,4,128]{3,1,2,0:T(8,128)(2,1)S(1)} %get-tuple-element.48), channel_id=1, source_target_pairs={{0,1},{1,2},{2,3},{3,4},{4,5},{5,6},{6,7},{7,0},{8,9},{9,10},{10,1... | collective-permute-start | bytes 786440 | tf_op jit(solution)/shard_map/ppermute | solution.py:41
  86.9 14.3 %collective-permute-start.16 = (bf16[2,128,4,128]{3,1,2,0:T(8,128)(2,1)S(1)}, bf16[2,128,4,128]{3,1,2,0:T(8,128)(2,1)S(1)}, u32[]{:S(2)}, u32[]{:S(2)}) collective-permute-start(bf16[2,128,4,128]{3,1,2,0:T(8,128)(2,1)S(1)} %get-tuple-element.47), channel_id=1, source_target_pairs={{0,2},{1,3},{2,4},{3,5},{4,6},{5,7},{6,0},{7,1},{8,10},{9,11},{10,... | collective-permute-start | bytes 786440 | tf_op jit(solution)/shard_map/ppermute | solution.py:41
  88.1 15.6 %collective-permute-start.17 = (bf16[2,128,4,128]{3,1,2,0:T(8,128)(2,1)S(1)}, bf16[2,128,4,128]{3,1,2,0:T(8,128)(2,1)}, u32[]{:S(2)}, u32[]{:S(2)}) collective-permute-start(bf16[2,128,4,128]{3,1,2,0:T(8,128)(2,1)S(1)} %get-tuple-element.46), channel_id=1, source_target_pairs={{0,3},{1,4},{2,5},{3,6},{4,7},{5,0},{6,1},{7,2},{8,11},{9,12},{10,... | collective-permute-start | bytes 786440 | tf_op jit(solution)/shard_map/ppermute | solution.py:41
  88.1 17.3 %collective-permute-start.18 = (bf16[2,128,4,128]{3,1,2,0:T(8,128)(2,1)S(1)}, bf16[2,128,4,128]{3,1,2,0:T(8,128)(2,1)}, u32[]{:S(2)}, u32[]{:S(2)}) collective-permute-start(bf16[2,128,4,128]{3,1,2,0:T(8,128)(2,1)S(1)} %get-tuple-element.45), channel_id=1, source_target_pairs={{0,4},{1,5},{2,6},{3,7},{4,0},{5,1},{6,2},{7,3},{8,12},{9,13},{10,... | collective-permute-start | bytes 786440 | tf_op jit(solution)/shard_map/ppermute | solution.py:41
  88.6 20.7 %collective-permute-start.19 = (bf16[2,128,4,128]{3,1,2,0:T(8,128)(2,1)S(1)}, bf16[2,128,4,128]{3,1,2,0:T(8,128)(2,1)}, u32[]{:S(2)}, u32[]{:S(2)}) collective-permute-start(bf16[2,128,4,128]{3,1,2,0:T(8,128)(2,1)S(1)} %get-tuple-element.44), channel_id=1, source_target_pairs={{0,5},{1,6},{2,7},{3,0},{4,1},{5,2},{6,3},{7,4},{8,13},{9,14},{10,... | collective-permute-start | bytes 786440 | tf_op jit(solution)/shard_map/ppermute | solution.py:41
  92.5 47.8 %collective-permute-start.20 = (bf16[2,128,4,128]{3,1,2,0:T(8,128)(2,1)}, bf16[2,128,4,128]{3,1,2,0:T(8,128)(2,1)}, u32[]{:S(2)}, u32[]{:S(2)}) collective-permute-start(bf16[2,128,4,128]{3,1,2,0:T(8,128)(2,1)} %get-tuple-element.43), channel_id=1, source_target_pairs={{0,6},{1,7},{2,0},{3,1},{4,2},{5,3},{6,4},{7,5},{8,14},{9,15},{10,... | collective-permute-start | bytes 786440 | tf_op jit(solution)/shard_map/ppermute | solution.py:41
  101.9 39.3 %collective-permute-start.21 = (bf16[2,128,4,128]{3,1,2,0:T(8,128)(2,1)S(1)}, bf16[2,128,4,128]{3,1,2,0:T(8,128)(2,1)}, u32[]{:S(2)}, u32[]{:S(2)}) collective-permute-start(bf16[2,128,4,128]{3,1,2,0:T(8,128)(2,1)S(1)} %get-tuple-element.42), channel_id=1, source_target_pairs={{0,7},{1,0},{2,1},{3,2},{4,3},{5,4},{6,5},{7,6},{8,15},{9,8},{10,9... | collective-permute-start | bytes 786440 | tf_op jit(solution)/shard_map/ppermute | solution.py:41
  131.4 107.6 %reduce-scatter.5.cloned.1.call-start = ((), (), s32[]{:S(2)}) async-start(), calls=%async_computation.4 | async-start | bytes 1310720 | tf_op jit(solution)/shard_map/reduce_scatter | solution.py:131
  139.7 22.1 %collective-permute-start.13 = (bf16[128,1024]{1,0:T(8,128)(2,1)}, bf16[128,1024]{1,0:T(8,128)(2,1)}, u32[]{:S(2)}, u32[]{:S(2)}) collective-permute-start(bf16[128,1024]{1,0:T(8,128)(2,1)} %get-tuple-element.52), channel_id=1, source_target_pairs={{0,16},{8,24},{16,0},{24,8},{1,17},{9,25},{17,1},{25,9},{2,18},{10... | collective-permute-start | bytes 786440 | tf_op jit(solution)/shard_map/ppermute | solution.py:41
  139.7 22.1 %collective-permute-start.12 = (bf16[128,1024]{1,0:T(8,128)(2,1)S(1)}, bf16[128,1024]{1,0:T(8,128)(2,1)}, u32[]{:S(2)}, u32[]{:S(2)}) collective-permute-start(bf16[128,1024]{1,0:T(8,128)(2,1)S(1)} %get-tuple-element.53), channel_id=1, source_target_pairs={{0,8},{8,16},{16,24},{24,0},{1,9},{9,17},{17,25},{25,1},{2,10},{10... | collective-permute-start | bytes 786440 | tf_op jit(solution)/shard_map/ppermute | solution.py:41
  174.3 12.2 %collective-permute-start.23 = (bf16[128,1024]{1,0:T(8,128)(2,1)S(1)}, bf16[128,1024]{1,0:T(8,128)(2,1)S(1)}, u32[]{:S(2)}, u32[]{:S(2)}) collective-permute-start(bf16[128,1024]{1,0:T(8,128)(2,1)S(1)} %get-tuple-element.41), channel_id=1, source_target_pairs={{0,2},{1,3},{2,4},{3,5},{4,6},{5,7},{6,0},{7,1},{8,10},{9,11},{10,... | collective-permute-start | bytes 786440 | tf_op jit(solution)/shard_map/ppermute | solution.py:30
  176.3 11.4 %collective-permute-start.24 = (bf16[128,1024]{1,0:T(8,128)(2,1)S(1)}, bf16[128,1024]{1,0:T(8,128)(2,1)S(1)}, u32[]{:S(2)}, u32[]{:S(2)}) collective-permute-start(bf16[128,1024]{1,0:T(8,128)(2,1)S(1)} %get-tuple-element.41), channel_id=1, source_target_pairs={{0,3},{1,4},{2,5},{3,6},{4,7},{5,0},{6,1},{7,2},{8,11},{9,12},{10,... | collective-permute-start | bytes 786440 | tf_op jit(solution)/shard_map/ppermute | solution.py:30
  176.5 22.6 %collective-permute-start.25 = (bf16[128,1024]{1,0:T(8,128)(2,1)S(1)}, bf16[128,1024]{1,0:T(8,128)(2,1)S(1)}, u32[]{:S(2)}, u32[]{:S(2)}) collective-permute-start(bf16[128,1024]{1,0:T(8,128)(2,1)S(1)} %get-tuple-element.41), channel_id=1, source_target_pairs={{0,4},{1,5},{2,6},{3,7},{4,0},{5,1},{6,2},{7,3},{8,12},{9,13},{10,... | collective-permute-start | bytes 786440 | tf_op jit(solution)/shard_map/ppermute | solution.py:30
  177.7 23.4 %collective-permute-start.26 = (bf16[128,1024]{1,0:T(8,128)(2,1)S(1)}, bf16[128,1024]{1,0:T(8,128)(2,1)S(1)}, u32[]{:S(2)}, u32[]{:S(2)}) collective-permute-start(bf16[128,1024]{1,0:T(8,128)(2,1)S(1)} %get-tuple-element.41), channel_id=1, source_target_pairs={{0,5},{1,6},{2,7},{3,0},{4,1},{5,2},{6,3},{7,4},{8,13},{9,14},{10,... | collective-permute-start | bytes 786440 | tf_op jit(solution)/shard_map/ppermute | solution.py:30
  179.9 21.9 %collective-permute-start.27 = (bf16[128,1024]{1,0:T(8,128)(2,1)S(1)}, bf16[128,1024]{1,0:T(8,128)(2,1)S(1)}, u32[]{:S(2)}, u32[]{:S(2)}) collective-permute-start(bf16[128,1024]{1,0:T(8,128)(2,1)S(1)} %get-tuple-element.41), channel_id=1, source_target_pairs={{0,6},{1,7},{2,0},{3,1},{4,2},{5,3},{6,4},{7,5},{8,14},{9,15},{10,... | collective-permute-start | bytes 786440 | tf_op jit(solution)/shard_map/ppermute | solution.py:30
  186.5 16.0 %collective-permute-start.28 = (bf16[128,1024]{1,0:T(8,128)(2,1)S(1)}, bf16[128,1024]{1,0:T(8,128)(2,1)S(1)}, u32[]{:S(2)}, u32[]{:S(2)}) collective-permute-start(bf16[128,1024]{1,0:T(8,128)(2,1)S(1)} %get-tuple-element.41), channel_id=1, source_target_pairs={{0,7},{1,0},{2,1},{3,2},{4,3},{5,4},{6,5},{7,6},{8,15},{9,8},{10,9... | collective-permute-start | bytes 786440 | tf_op jit(solution)/shard_map/ppermute | solution.py:30
  (22 other events, 142.4 us)
Sparse Core Ops, SparseCore 0:
  13.2 29.3 all-gather.3
  71.4 56.9 reduce-scatter.2
  131.5 28.3 all-gather.5
  213.3 25.7 reduce-scatter.4

commit v5 on v4

--- a/solution.py
+++ b/solution.py
@@ -121,11 +121,10 @@
         "qe,de->qd", dz_code, projection, preferred_element_type=jnp.float32
     ).astype(jnp.bfloat16)
 
-    dzq_all = shift_all(dz_query, "member")
-    dzc_all = lax.all_gather(dz_code, "member", axis=0)
+    dz_all = lax.all_gather(jnp.stack([dz_query, dz_code], axis=0), "member", axis=0)
     proj_parts = jnp.einsum(
-        "mqgr,mqe->gre", feat_cols[:, 0], dzq_all, preferred_element_type=jnp.float32
-    ) + jnp.einsum("mqgr,mqe->gre", feat_cols[:, 1], dzc_all, preferred_element_type=jnp.float32)
+        "mtqgr,mtqe->gre", feat_cols, dz_all, preferred_element_type=jnp.float32
+    )
     own_proj = jnp.take(proj_parts, group_index, axis=0)
     sent_proj = jnp.where(own[:, None, None], 0.0, proj_parts).astype(jnp.bfloat16)
     projection_grad = own_proj + lax.psum_scatter(

time: 250 us -> 214 us (0.86)
  local copies, waits for them, and re-layouts: 36.1 us -> 9.71 us
  starting transfers between devices: 39.1 us -> 26.6 us
  waiting for transfers between devices: 92.3 us -> 104 us
  other arithmetic: 23.3 us -> 14.6 us
    ppermute x10, waiting for transfers between devices: 26.4 us -> 44.6 us  [exchange(): lax.ppermute(sent, axis, [(i, (i + s) % size) for i in range(size)])]
    ppermute x19 -> x12, waiting for transfers between devices: 37 us -> 19 us  [shift_all(): lax.ppermute(x, axis, [(i, (i + s) % size) for i in range(size)])]
    unnamed x40 -> x28, local copies, waits for them, and re-layouts: 17.2 us -> 3.09 us
    all_gather x1, waiting for transfers between devices: 0.01 us -> 12.5 us  [body(): lax.all_gather(jnp.stack([dz_query, dz_code], axis=0), 'member', axis=0)]
    ppermute x19 -> x12, starting transfers between devices: 25.3 us -> 18.3 us  [shift_all(): lax.ppermute(x, axis, [(i, (i + s) % size) for i in range(size)])]
    ppermute x10, starting transfers between devices: 13.7 us -> 8.07 us  [exchange(): lax.ppermute(sent, axis, [(i, (i + s) % size) for i in range(size)])]
    gather x3 -> x2, local copies, waits for them, and re-layouts: 7.98 us -> 2.78 us  [exchange(): return jnp.take(stacked, (index - jnp.arange(size)) % size, axis=0)]
    gather x5 -> x4, local copies, waits for them, and re-layouts: 6.12 us -> 2.3 us  [shift_all(): jnp.take(jnp.stack(xs, axis=0), order, axis=0)]
  transfers between devices with their start and end apart: 33 -> 26, of which waited for: 17 -> 15; matrix products, arithmetic and copies ran while one was open for 30% -> 18% of each run, Pallas kernels for 0% -> 0%
where the time goes in v5:
time: 214 us; the launch traced here: 211 us
  waiting for transfers between devices  104 us (49%)
  matrix products  42.6 us (20%)
  starting transfers between devices  26.6 us (12%)
  other arithmetic  14.6 us (7%)
  between operations  14.5 us (7%)
  local copies, waits for them, and re-layouts  9.71 us (5%)
    ppermute x10, waiting for transfers between devices, exchange(): lax.ppermute(sent, axis, [(i, (i + s) % size) for i in range(size)])  44.6 us
    ppermute x12, waiting for transfers between devices, shift_all(): lax.ppermute(x, axis, [(i, (i + s) % size) for i in range(size)])  19 us
    ppermute x12, starting transfers between devices, shift_all(): lax.ppermute(x, axis, [(i, (i + s) % size) for i in range(size)])  18.3 us
    reduce_scatter x1, waiting for transfers between devices, body(): lax.psum_scatter(code_terms.astype(jnp.bfloat16), 'member', scatter_dimen...  15.3 us
    all_gather x1, waiting for transfers between devices, body(): lax.all_gather(jnp.stack([dz_query, dz_code], axis=0), 'member', axis=0)  12.5 us
    reduce_scatter x1, waiting for transfers between devices, body(): lax.psum_scatter(sent_proj, 'group', scatter_dimension=0, tiled=True)  12.1 us
    dot_general x2, matrix products, embed(): values = jnp.dot(features, projection, preferred_element_type=jnp.float32)  9.77 us
    ppermute x10, starting transfers between devices, exchange(): lax.ppermute(sent, axis, [(i, (i + s) % size) for i in range(size)])  8.07 us
  transfers between devices with their start and end apart: 26, of which 15 were waited for; matrix products, arithmetic and copies ran while one was open for 18% of the time, Pallas kernels for 0%

profile of v5, /device:TPU:3, one launch (start us, length us, event | category | flops | bytes accessed | tf_op | source)
XLA Modules:
  0.0 211.4 jit_solution(9135383020964955116)
XLA Ops:
  7.2 5.1 %multiply_reduce_fusion.1 = (f32[128]{0:T(128)S(1)}, f32[128,1024]{1,0:T(8,128)S(1)}) fusion(bf16[128,4096]{1,0:T(8,128)(2,1)} %param.14, bf16[4096,1024]{1,0:T(8,128)(2,1)} %param.15), kind=kOutput, calls=%fused_computation.38 | convolution fusion | flops 1074003840 | bytes 9961984 | tf_op jit(solution)/shard_map/dot_general | solution.py:14
  13.6 4.7 %multiply_reduce_fusion.2 = (f32[128]{0:T(128)S(1)}, f32[128,1024]{1,0:T(8,128)S(1)}) fusion(bf16[128,4096]{1,0:T(8,128)(2,1)S(1)} %copy-done.1, bf16[4096,1024]{1,0:T(8,128)(2,1)} %param.15), kind=kOutput, calls=%fused_computation.39 | convolution fusion | flops 1074003840 | bytes 9961984 | tf_op jit(solution)/shard_map/dot_general | solution.py:14
  18.4 3.4 %collective-permute-start.8 = (bf16[128,1024]{1,0:T(8,128)(2,1)S(1)}, bf16[128,1024]{1,0:T(8,128)(2,1)S(1)}, u32[]{:S(2)}, u32[]{:S(2)}) collective-permute-start(bf16[128,1024]{1,0:T(8,128)(2,1)S(1)} %multiply_convert_fusion.3), channel_id=1, source_target_pairs={{0,24},{8,0},{16,8},{24,16},{1,25},{9,1},{17,9},{25,17},{2,26},{10... | collective-permute-start | bytes 786440 | tf_op jit(solution)/shard_map/ppermute | solution.py:30
  22.3 2.8 %collective-permute-start.5 = (s32[16]{0:T(128)S(1)}, s32[16]{0:T(128)S(1)}, u32[]{:S(2)}, u32[]{:S(2)}) collective-permute-start(s32[16]{0:T(128)S(1)} %bitcast.165), channel_id=1, source_target_pairs={{0,24},{8,0},{16,8},{24,16},{1,25},{9,1},{17,9},{25,17},{2,26},{10... | collective-permute-start | bytes 200 | tf_op jit(solution)/shard_map/ppermute | solution.py:30
  26.8 11.4 %collective-permute-done.5 = s32[16]{0:T(128)S(1)} collective-permute-done((s32[16]{0:T(128)S(1)}, s32[16]{0:T(128)S(1)}, u32[]{:S(2)}, u32[]{:S(2)}) %collective-permute-start.5) | collective-permute-done | bytes 96 | tf_op jit(solution)/shard_map/ppermute | solution.py:30
  38.2 5.3 %collective-permute-start.3 = (s32[16]{0:T(128)S(1)}, s32[16]{0:T(128)S(1)}, u32[]{:S(2)}, u32[]{:S(2)}) collective-permute-start(s32[16]{0:T(128)S(1)} %bitcast.167), channel_id=1, source_target_pairs={{0,8},{8,16},{16,24},{24,0},{1,9},{9,17},{17,25},{25,1},{2,10},{10... | collective-permute-start | bytes 200 | tf_op jit(solution)/shard_map/ppermute | solution.py:30
  43.6 3.4 %collective-permute-start.2 = (f32[128]{0:T(128)S(1)}, f32[128]{0:T(128)S(1)}, u32[]{:S(2)}, u32[]{:S(2)}) collective-permute-start(f32[128]{0:T(128)S(1)} %copy-done.9), channel_id=1, source_target_pairs={{0,24},{8,0},{16,8},{24,16},{1,25},{9,1},{17,9},{25,17},{2,26},{10... | collective-permute-start | bytes 1544 | tf_op jit(solution)/shard_map/ppermute | solution.py:30
  54.7 3.3 %fusion.32 = (f32[4,128]{1,0:T(4,128)S(1)}, f32[4,128,1024]{2,1,0:T(8,128)S(1)}) fusion(bf16[4,128,1024]{2,1,0:T(8,128)(2,1)} %broadcast_select_fusion, bf16[1024,1024]{1,0:T(8,128)(2,1)} %all-gather.4.cloned.1.call-done, pred[4,1024]{1,0:T(4,128)(4,1)S(1)} %broadcast_in_dim.140), kind=kOutput, calls=%fused_computation.125 | convolution fusion | flops 1075314176 | bytes 5249024 | tf_op jit(solution)/shard_map/gqe,ke->gqk/dot_general | solution.py:78
  61.0 2.4 %collective-permute-done.10 = f32[2,4,128]{2,1,0:T(4,128)S(1)} collective-permute-done((f32[2,4,128]{2,1,0:T(4,128)S(1)}, f32[2,4,128]{2,1,0:T(4,128)S(1)}, u32[]{:S(2)}, u32[]{:S(2)}) %collective-permute-start.10) | collective-permute-done | bytes 4128 | tf_op jit(solution)/shard_map/ppermute | solution.py:30
  68.9 2.4 %add_convert_fusion = bf16[1024,1024]{1,0:T(8,128)(2,1)} fusion(f32[1024,1024]{1,0:T(8,128)S(1)} %fusion.17, f32[1024,1024]{1,0:T(8,128)S(1)} %fusion.18, f32[1024,1024]{1,0:T(8,128)S(1)} %fusion.19, pred[]{:T(512)S(6)} %eq.84, pred[]{:T(512)S(6)} %eq.83, pred[]{:T(512)S(6)} %eq.82, pred[]{:T(512)S(6)} %eq.81, bf16[4,128,1024]{2,1,0:T(8,128)(2,1)S(1)} %copy-done.5, ...), kind=kOutput, calls=%fused_computation.8 | convolution fusion | flops 285212672 | bytes 15204356 | tf_op jit(solution)/shard_map/dot_general | solution.py:108
  72.5 4.2 %fusion.33 = (bf16[4,128,1024]{2,1,0:T(8,128)(2,1)S(1)}, f32[4,128,1024]{2,1,0:T(8,128)}) fusion(bf16[4,128,1024]{2,1,0:T(8,128)(2,1)S(1)} %copy-done.4, bf16[1024,1024]{1,0:T(8,128)(2,1)} %all-gather.4.cloned.1.call-done), kind=kOutput, calls=%fused_computation.126 | convolution fusion | flops 1074266112 | bytes 6291456 | tf_op jit(solution)/shard_map/gqk,ke->gqe/dot_general | solution.py:101
  78.9 4.4 %collective-permute-done.14 = bf16[128,1024]{1,0:T(8,128)(2,1)S(1)} collective-permute-done((bf16[128,1024]{1,0:T(8,128)(2,1)S(1)}, bf16[128,1024]{1,0:T(8,128)(2,1)S(1)}, u32[]{:S(2)}, u32[]{:S(2)}) %collective-permute-start.14) | collective-permute-done | bytes 262176 | tf_op jit(solution)/shard_map/ppermute | solution.py:41
  83.3 13.5 %collective-permute-done.13 = bf16[128,1024]{1,0:T(8,128)(2,1)S(1)} collective-permute-done((bf16[128,1024]{1,0:T(8,128)(2,1)S(1)}, bf16[128,1024]{1,0:T(8,128)(2,1)S(1)}, u32[]{:S(2)}, u32[]{:S(2)}) %collective-permute-start.13) | collective-permute-done | bytes 262176 | tf_op jit(solution)/shard_map/ppermute | solution.py:41
  100.4 15.3 %reduce-scatter.3.cloned.1.call-done = bf16[128,1024]{1,0:T(8,128)(2,1)} async-done(((bf16[1024,1024]{1,0:T(8,128)(2,1)}), bf16[128,1024]{1,0:T(8,128)(2,1)}) %reduce-scatter.3.cloned.1.call-update) | async-done | bytes 262160 | tf_op jit(solution)/shard_map/reduce_scatter | solution.py:111
  122.5 2.0 collective-permute-start.15
  128.0 4.2 %collective-permute-done.15 = bf16[2,128,4,128]{3,1,2,0:T(8,128)(2,1)S(1)} collective-permute-done((bf16[2,128,4,128]{3,1,2,0:T(8,128)(2,1)S(1)}, bf16[2,128,4,128]{3,1,2,0:T(8,128)(2,1)S(1)}, u32[]{:S(2)}, u32[]{:S(2)}) %collective-permute-start.15) | collective-permute-done | bytes 262176 | tf_op jit(solution)/shard_map/ppermute | solution.py:41
  132.8 9.5 %collective-permute-done.16 = bf16[2,128,4,128]{3,1,2,0:T(8,128)(2,1)S(1)} collective-permute-done((bf16[2,128,4,128]{3,1,2,0:T(8,128)(2,1)S(1)}, bf16[2,128,4,128]{3,1,2,0:T(8,128)(2,1)S(1)}, u32[]{:S(2)}, u32[]{:S(2)}) %collective-permute-start.16) | collective-permute-done | bytes 262176 | tf_op jit(solution)/shard_map/ppermute | solution.py:41
  143.6 11.7 %collective-permute-done.19 = bf16[2,128,4,128]{3,1,2,0:T(8,128)(2,1)S(1)} collective-permute-done((bf16[2,128,4,128]{3,1,2,0:T(8,128)(2,1)S(1)}, bf16[2,128,4,128]{3,1,2,0:T(8,128)(2,1)S(1)}, u32[]{:S(2)}, u32[]{:S(2)}) %collective-permute-start.19) | collective-permute-done | bytes 262176 | tf_op jit(solution)/shard_map/ppermute | solution.py:41
  155.5 2.2 %gather_fusion.3 = bf16[8,2,128,4,128]{4,2,3,1,0:T(8,128)(2,1)} fusion(bf16[8,2,128,4,128]{4,2,3,1,0:T(8,128)(2,1)S(1)} %bitcast_dynamic-update-slice_fusion, s32[1024]{0:T(1024)S(1)} %pad_clamp_fusion), kind=kCustom, calls=%fused_computation.5 | custom fusion | bytes 4194336 | tf_op jit(solution)/shard_map/jit(_take)/gather | solution.py:43
  157.6 12.5 %all-gather.6.cloned.1.call-done = bf16[16,128,1024]{2,1,0:T(8,128)(2,1)} async-done(((bf16[2,128,1024]{2,1,0:T(8,128)(2,1)}), bf16[16,128,1024]{2,1,0:T(8,128)(2,1)}) %all-gather.6.cloned.1.call-update) | async-done | bytes 4194320 | tf_op jit(solution)/shard_map/all_gather | solution.py:124
  170.1 6.3 %select_convert_fusion = (bf16[4,128,1024]{2,1,0:T(8,128)(2,1)}, f32[4,128,1024]{2,1,0:T(8,128)S(1)}) fusion(pred[4]{0:T(512)(128)(4,1)S(1)} %iota_compare_fusion.1, bf16[8,2,128,1024,1]{3,2,4,1,0:T(8,128)(2,1)} %bitcast.175, bf16[8,2,128,4,128]{4,2,3,1,0:T(8,128)(2,1)} %gather_fusion.3, pred[8]{0:T(512)(128)(4,1)S(1)} %compare_and_fusion), kind=kOutput, calls=%fused_computation.14 | convolution fusion | flops 2149056512 | bytes 9437196 | tf_op jit(solution)/shard_map/mtqgr,mtqe->gre/dot_general | solution.py:125
  176.4 7.2 %convolution_convert_fusion.1 = bf16[128,4096]{1,0:T(8,128)(2,1)} fusion(bf16[128,1024]{1,0:T(8,128)(2,1)S(1)} %copy-done.7, bf16[4096,1024]{1,0:T(8,128)(2,1)} %param.15), kind=kOutput, calls=%fused_computation.7 | convolution fusion | flops 1074266112 | bytes 9699328 | tf_op jit(solution)/shard_map/qe,de->qd/dot_general | solution.py:117
  183.7 7.2 %convolution_convert_fusion = bf16[128,4096]{1,0:T(8,128)(2,1)} fusion(bf16[128,1024]{1,0:T(8,128)(2,1)S(1)} %fusion.15, bf16[4096,1024]{1,0:T(8,128)(2,1)} %param.15), kind=kOutput, calls=%fused_computation.6 | convolution fusion | flops 1074266112 | bytes 9699328 | tf_op jit(solution)/shard_map/qe,de->qd/dot_general | solution.py:120
  190.9 12.1 %reduce-scatter.5.cloned.1.call-done = bf16[1,128,1024]{2,1,0:T(8,128)(2,1)} async-done(((bf16[4,128,1024]{2,1,0:T(8,128)(2,1)}), bf16[1,128,1024]{2,1,0:T(8,128)(2,1)}) %reduce-scatter.5.cloned.1.call-update) | async-done | bytes 262160 | tf_op jit(solution)/shard_map/reduce_scatter | solution.py:130
  (127 shorter events, 40.4 us)
Async XLA Ops:
  7.2 47.5 %all-gather.4.cloned.1.call-start = ((), (), s32[]{:S(2)}) async-start(), calls=%async_computation.2 | async-start | bytes 2359296 | tf_op jit(solution)/shard_map/all_gather | solution.py:67
  13.1 102.6 %reduce-scatter.3.cloned.1.call-start = ((), (), s32[]{:S(2)}) async-start(), calls=%async_computation.3 | async-start | bytes 2359296 | tf_op jit(solution)/shard_map/reduce_scatter | solution.py:111
  18.4 34.3 %collective-permute-start.8 = (bf16[128,1024]{1,0:T(8,128)(2,1)S(1)}, bf16[128,1024]{1,0:T(8,128)(2,1)S(1)}, u32[]{:S(2)}, u32[]{:S(2)}) collective-permute-start(bf16[128,1024]{1,0:T(8,128)(2,1)S(1)} %multiply_convert_fusion.3), channel_id=1, source_target_pairs={{0,24},{8,0},{16,8},{24,16},{1,25},{9,1},{17,9},{25,17},{2,26},{10... | collective-permute-start | bytes 786440 | tf_op jit(solution)/shard_map/ppermute | solution.py:30
  21.8 31.0 %collective-permute-start.7 = (bf16[128,1024]{1,0:T(8,128)(2,1)S(1)}, bf16[128,1024]{1,0:T(8,128)(2,1)S(1)}, u32[]{:S(2)}, u32[]{:S(2)}) collective-permute-start(bf16[128,1024]{1,0:T(8,128)(2,1)S(1)} %multiply_convert_fusion.3), channel_id=1, source_target_pairs={{0,16},{8,24},{16,0},{24,8},{1,17},{9,25},{17,1},{25,9},{2,18},{10... | collective-permute-start | bytes 786440 | tf_op jit(solution)/shard_map/ppermute | solution.py:30
  21.8 31.0 %collective-permute-start.6 = (bf16[128,1024]{1,0:T(8,128)(2,1)S(1)}, bf16[128,1024]{1,0:T(8,128)(2,1)S(1)}, u32[]{:S(2)}, u32[]{:S(2)}) collective-permute-start(bf16[128,1024]{1,0:T(8,128)(2,1)S(1)} %multiply_convert_fusion.3), channel_id=1, source_target_pairs={{0,8},{8,16},{16,24},{24,0},{1,9},{9,17},{17,25},{25,1},{2,10},{10... | collective-permute-start | bytes 786440 | tf_op jit(solution)/shard_map/ppermute | solution.py:30
  22.3 15.9 %collective-permute-start.5 = (s32[16]{0:T(128)S(1)}, s32[16]{0:T(128)S(1)}, u32[]{:S(2)}, u32[]{:S(2)}) collective-permute-start(s32[16]{0:T(128)S(1)} %bitcast.165), channel_id=1, source_target_pairs={{0,24},{8,0},{16,8},{24,16},{1,25},{9,1},{17,9},{25,17},{2,26},{10... | collective-permute-start | bytes 200 | tf_op jit(solution)/shard_map/ppermute | solution.py:30
  25.1 18.5 %collective-permute-start.4 = (s32[16]{0:T(128)S(1)}, s32[16]{0:T(128)S(1)}, u32[]{:S(2)}, u32[]{:S(2)}) collective-permute-start(s32[16]{0:T(128)S(1)} %bitcast.166), channel_id=1, source_target_pairs={{0,16},{8,24},{16,0},{24,8},{1,17},{9,25},{17,1},{25,9},{2,18},{10... | collective-permute-start | bytes 200 | tf_op jit(solution)/shard_map/ppermute | solution.py:30
  38.2 8.8 %collective-permute-start.3 = (s32[16]{0:T(128)S(1)}, s32[16]{0:T(128)S(1)}, u32[]{:S(2)}, u32[]{:S(2)}) collective-permute-start(s32[16]{0:T(128)S(1)} %bitcast.167), channel_id=1, source_target_pairs={{0,8},{8,16},{16,24},{24,0},{1,9},{9,17},{17,25},{25,1},{2,10},{10... | collective-permute-start | bytes 200 | tf_op jit(solution)/shard_map/ppermute | solution.py:30
  43.6 4.2 %collective-permute-start.2 = (f32[128]{0:T(128)S(1)}, f32[128]{0:T(128)S(1)}, u32[]{:S(2)}, u32[]{:S(2)}) collective-permute-start(f32[128]{0:T(128)S(1)} %copy-done.9), channel_id=1, source_target_pairs={{0,24},{8,0},{16,8},{24,16},{1,25},{9,1},{17,9},{25,17},{2,26},{10... | collective-permute-start | bytes 1544 | tf_op jit(solution)/shard_map/ppermute | solution.py:30
  47.8 4.4 %collective-permute-start = (f32[128]{0:T(128)S(1)}, f32[128]{0:T(128)S(1)}, u32[]{:S(2)}, u32[]{:S(2)}) collective-permute-start(f32[128]{0:T(128)S(1)} %copy-done.9), channel_id=1, source_target_pairs={{0,8},{8,16},{16,24},{24,0},{1,9},{9,17},{17,25},{25,1},{2,10},{10... | collective-permute-start | bytes 1544 | tf_op jit(solution)/shard_map/ppermute | solution.py:30
  60.0 3.4 %collective-permute-start.10 = (f32[2,4,128]{2,1,0:T(4,128)S(1)}, f32[2,4,128]{2,1,0:T(4,128)S(1)}, u32[]{:S(2)}, u32[]{:S(2)}) collective-permute-start(f32[2,4,128]{2,1,0:T(4,128)S(1)} %get-tuple-element.53), channel_id=1, source_target_pairs={{0,16},{8,24},{16,0},{24,8},{1,17},{9,25},{17,1},{25,9},{2,18},{10... | collective-permute-start | bytes 12296 | tf_op jit(solution)/shard_map/ppermute | solution.py:30
  60.0 4.3 %collective-permute-start.9 = (f32[2,4,128]{2,1,0:T(4,128)S(1)}, f32[2,4,128]{2,1,0:T(4,128)S(1)}, u32[]{:S(2)}, u32[]{:S(2)}) collective-permute-start(f32[2,4,128]{2,1,0:T(4,128)S(1)} %get-tuple-element.53), channel_id=1, source_target_pairs={{0,8},{8,16},{16,24},{24,0},{1,9},{9,17},{17,25},{25,1},{2,10},{10... | collective-permute-start | bytes 12296 | tf_op jit(solution)/shard_map/ppermute | solution.py:30
  71.3 98.8 %all-gather.6.cloned.1.call-start = ((), (), s32[]{:S(2)}) async-start(), calls=%async_computation.5 | async-start | bytes 4718592 | tf_op jit(solution)/shard_map/all_gather | solution.py:124
  76.8 6.5 %collective-permute-start.14 = (bf16[128,1024]{1,0:T(8,128)(2,1)S(1)}, bf16[128,1024]{1,0:T(8,128)(2,1)S(1)}, u32[]{:S(2)}, u32[]{:S(2)}) collective-permute-start(bf16[128,1024]{1,0:T(8,128)(2,1)S(1)} %get-tuple-element.49), channel_id=1, source_target_pairs={{0,24},{8,0},{16,8},{24,16},{1,25},{9,1},{17,9},{25,17},{2,26},{10... | collective-permute-start | bytes 786440 | tf_op jit(solution)/shard_map/ppermute | solution.py:41
  77.1 19.7 %collective-permute-start.13 = (bf16[128,1024]{1,0:T(8,128)(2,1)S(1)}, bf16[128,1024]{1,0:T(8,128)(2,1)S(1)}, u32[]{:S(2)}, u32[]{:S(2)}) collective-permute-start(bf16[128,1024]{1,0:T(8,128)(2,1)S(1)} %get-tuple-element.50), channel_id=1, source_target_pairs={{0,16},{8,24},{16,0},{24,8},{1,17},{9,25},{17,1},{25,9},{2,18},{10... | collective-permute-start | bytes 786440 | tf_op jit(solution)/shard_map/ppermute | solution.py:41
  77.5 19.4 %collective-permute-start.12 = (bf16[128,1024]{1,0:T(8,128)(2,1)S(1)}, bf16[128,1024]{1,0:T(8,128)(2,1)S(1)}, u32[]{:S(2)}, u32[]{:S(2)}) collective-permute-start(bf16[128,1024]{1,0:T(8,128)(2,1)S(1)} %get-tuple-element.51), channel_id=1, source_target_pairs={{0,8},{8,16},{16,24},{24,0},{1,9},{9,17},{17,25},{25,1},{2,10},{10... | collective-permute-start | bytes 786440 | tf_op jit(solution)/shard_map/ppermute | solution.py:41
  118.9 84.2 %reduce-scatter.5.cloned.1.call-start = ((), (), s32[]{:S(2)}) async-start(), calls=%async_computation.4 | async-start | bytes 1310720 | tf_op jit(solution)/shard_map/reduce_scatter | solution.py:130
  122.5 9.7 %collective-permute-start.15 = (bf16[2,128,4,128]{3,1,2,0:T(8,128)(2,1)S(1)}, bf16[2,128,4,128]{3,1,2,0:T(8,128)(2,1)S(1)}, u32[]{:S(2)}, u32[]{:S(2)}) collective-permute-start(bf16[2,128,4,128]{3,1,2,0:T(8,128)(2,1)S(1)} %get-tuple-element.46), channel_id=1, source_target_pairs={{0,1},{1,2},{2,3},{3,4},{4,5},{5,6},{6,7},{7,0},{8,9},{9,10},{10,1... | collective-permute-start | bytes 786440 | tf_op jit(solution)/shard_map/ppermute | solution.py:41
  124.5 17.8 %collective-permute-start.16 = (bf16[2,128,4,128]{3,1,2,0:T(8,128)(2,1)S(1)}, bf16[2,128,4,128]{3,1,2,0:T(8,128)(2,1)S(1)}, u32[]{:S(2)}, u32[]{:S(2)}) collective-permute-start(bf16[2,128,4,128]{3,1,2,0:T(8,128)(2,1)S(1)} %get-tuple-element.45), channel_id=1, source_target_pairs={{0,2},{1,3},{2,4},{3,5},{4,6},{5,7},{6,0},{7,1},{8,10},{9,11},{10,... | collective-permute-start | bytes 786440 | tf_op jit(solution)/shard_map/ppermute | solution.py:41
  124.8 18.8 %collective-permute-start.17 = (bf16[2,128,4,128]{3,1,2,0:T(8,128)(2,1)S(1)}, bf16[2,128,4,128]{3,1,2,0:T(8,128)(2,1)S(1)}, u32[]{:S(2)}, u32[]{:S(2)}) collective-permute-start(bf16[2,128,4,128]{3,1,2,0:T(8,128)(2,1)S(1)} %get-tuple-element.44), channel_id=1, source_target_pairs={{0,3},{1,4},{2,5},{3,6},{4,7},{5,0},{6,1},{7,2},{8,11},{9,12},{10,... | collective-permute-start | bytes 786440 | tf_op jit(solution)/shard_map/ppermute | solution.py:41
  125.1 18.4 %collective-permute-start.18 = (bf16[2,128,4,128]{3,1,2,0:T(8,128)(2,1)S(1)}, bf16[2,128,4,128]{3,1,2,0:T(8,128)(2,1)S(1)}, u32[]{:S(2)}, u32[]{:S(2)}) collective-permute-start(bf16[2,128,4,128]{3,1,2,0:T(8,128)(2,1)S(1)} %get-tuple-element.43), channel_id=1, source_target_pairs={{0,4},{1,5},{2,6},{3,7},{4,0},{5,1},{6,2},{7,3},{8,12},{9,13},{10,... | collective-permute-start | bytes 786440 | tf_op jit(solution)/shard_map/ppermute | solution.py:41
  126.3 29.0 %collective-permute-start.19 = (bf16[2,128,4,128]{3,1,2,0:T(8,128)(2,1)S(1)}, bf16[2,128,4,128]{3,1,2,0:T(8,128)(2,1)S(1)}, u32[]{:S(2)}, u32[]{:S(2)}) collective-permute-start(bf16[2,128,4,128]{3,1,2,0:T(8,128)(2,1)S(1)} %get-tuple-element.42), channel_id=1, source_target_pairs={{0,5},{1,6},{2,7},{3,0},{4,1},{5,2},{6,3},{7,4},{8,13},{9,14},{10,... | collective-permute-start | bytes 786440 | tf_op jit(solution)/shard_map/ppermute | solution.py:41
  132.2 23.1 %collective-permute-start.20 = (bf16[2,128,4,128]{3,1,2,0:T(8,128)(2,1)S(1)}, bf16[2,128,4,128]{3,1,2,0:T(8,128)(2,1)S(1)}, u32[]{:S(2)}, u32[]{:S(2)}) collective-permute-start(bf16[2,128,4,128]{3,1,2,0:T(8,128)(2,1)S(1)} %get-tuple-element.41), channel_id=1, source_target_pairs={{0,6},{1,7},{2,0},{3,1},{4,2},{5,3},{6,4},{7,5},{8,14},{9,15},{10,... | collective-permute-start | bytes 786440 | tf_op jit(solution)/shard_map/ppermute | solution.py:41
  142.2 13.2 %collective-permute-start.21 = (bf16[2,128,4,128]{3,1,2,0:T(8,128)(2,1)S(1)}, bf16[2,128,4,128]{3,1,2,0:T(8,128)(2,1)S(1)}, u32[]{:S(2)}, u32[]{:S(2)}) collective-permute-start(bf16[2,128,4,128]{3,1,2,0:T(8,128)(2,1)S(1)} %get-tuple-element.40), channel_id=1, source_target_pairs={{0,7},{1,0},{2,1},{3,2},{4,3},{5,4},{6,5},{7,6},{8,15},{9,8},{10,9... | collective-permute-start | bytes 786440 | tf_op jit(solution)/shard_map/ppermute | solution.py:41
  (12 other events, 91.7 us)
Sparse Core Ops, SparseCore 0:
  13.2 29.3 all-gather.3
  71.4 44.2 reduce-scatter.2
  119.0 51.0 all-gather.5
  176.5 26.4 reduce-scatter.4

commit v6 on v5

--- a/solution.py
+++ b/solution.py
@@ -60,7 +60,7 @@
         2, queries_dev, groups, members, rows_dev
     )
     feats = jnp.transpose(feats, (3, 0, 1, 2, 4))
-    feat_cols = exchange(feats, "member")
+    feat_cols = lax.all_to_all(feats, "member", split_axis=0, concat_axis=0, tiled=True)
 
     q_unit, q_inv, q_emb = embed(query_feat, projection)
     c_unit, c_inv, c_emb = embed(code_feat, projection)

time: 214 us -> 212 us (level)
  blocking collectives: 0 us -> 34.2 us
  waiting for transfers between devices: 104 us -> 77.6 us
  starting transfers between devices: 26.6 us -> 20.6 us
  local copies, waits for them, and re-layouts: 9.71 us -> 6.2 us
    all_to_all x0 -> x1, blocking collectives: none -> 34.2 us  [body(): lax.all_to_all(feats, 'member', split_axis=0, concat_axis=0, tiled=True)]
    ppermute x10 -> x3, waiting for transfers between devices: 44.6 us -> 18 us  [exchange(): lax.ppermute(sent, axis, [(i, (i + s) % size) for i in range(size)])]
    ppermute x10 -> x3, starting transfers between devices: 8.07 us -> 2.09 us  [exchange(): lax.ppermute(sent, axis, [(i, (i + s) % size) for i in range(size)])]
    gather x2 -> x1, local copies, waits for them, and re-layouts: 2.78 us -> 0.61 us  [exchange(): return jnp.take(stacked, (index - jnp.arange(size)) % size, axis=0)]
  transfers between devices with their start and end apart: 26 -> 19, of which waited for: 15 -> 11; matrix products, arithmetic and copies ran while one was open for 18% -> 16% of each run, Pallas kernels for 0% -> 0%
where the time goes in v6:
time: 212 us; the launch traced here: 209 us
  waiting for transfers between devices  77.6 us (37%)
  matrix products  42.5 us (20%)
  blocking collectives  34.2 us (16%)
  starting transfers between devices  20.6 us (10%)
  other arithmetic  14.2 us (7%)
  between operations  14.2 us (7%)
  local copies, waits for them, and re-layouts  6.2 us (3%)
    all_to_all x1, blocking collectives, body(): lax.all_to_all(feats, 'member', split_axis=0, concat_axis=0, tiled=True)  34.2 us
    ppermute x12, waiting for transfers between devices, shift_all(): lax.ppermute(x, axis, [(i, (i + s) % size) for i in range(size)])  19 us
    ppermute x12, starting transfers between devices, shift_all(): lax.ppermute(x, axis, [(i, (i + s) % size) for i in range(size)])  18.3 us
    ppermute x3, waiting for transfers between devices, exchange(): lax.ppermute(sent, axis, [(i, (i + s) % size) for i in range(size)])  18 us
    reduce_scatter x1, waiting for transfers between devices, body(): lax.psum_scatter(code_terms.astype(jnp.bfloat16), 'member', scatter_dimen...  15.3 us
    all_gather x1, waiting for transfers between devices, body(): lax.all_gather(jnp.stack([dz_query, dz_code], axis=0), 'member', axis=0)  13.2 us
    reduce_scatter x1, waiting for transfers between devices, body(): lax.psum_scatter(sent_proj, 'group', scatter_dimension=0, tiled=True)  12.1 us
    dot_general x2, matrix products, embed(): values = jnp.dot(features, projection, preferred_element_type=jnp.float32)  9.77 us
  transfers between devices with their start and end apart: 19, of which 11 were waited for; matrix products, arithmetic and copies ran while one was open for 16% of the time, Pallas kernels for 0%

profile of v6, /device:TPU:3, one launch (start us, length us, event | category | flops | bytes accessed | tf_op | source)
XLA Modules:
  0.0 209.4 jit_solution(18369732459536630811)
XLA Ops:
  7.2 5.1 %multiply_reduce_fusion.1 = (f32[128]{0:T(128)S(1)}, f32[128,1024]{1,0:T(8,128)S(1)}) fusion(bf16[128,4096]{1,0:T(8,128)(2,1)} %param.12, bf16[4096,1024]{1,0:T(8,128)(2,1)} %param.13), kind=kOutput, calls=%fused_computation.33 | convolution fusion | flops 1074003840 | bytes 9961984 | tf_op jit(solution)/shard_map/dot_general | solution.py:14
  13.6 4.7 %multiply_reduce_fusion.2 = (f32[128]{0:T(128)S(1)}, f32[128,1024]{1,0:T(8,128)S(1)}) fusion(bf16[128,4096]{1,0:T(8,128)(2,1)S(1)} %copy-done.1, bf16[4096,1024]{1,0:T(8,128)(2,1)} %param.13), kind=kOutput, calls=%fused_computation.34 | convolution fusion | flops 1074003840 | bytes 9961984 | tf_op jit(solution)/shard_map/dot_general | solution.py:14
  18.4 3.4 %collective-permute-start.8 = (bf16[128,1024]{1,0:T(8,128)(2,1)S(1)}, bf16[128,1024]{1,0:T(8,128)(2,1)S(1)}, u32[]{:S(2)}, u32[]{:S(2)}) collective-permute-start(bf16[128,1024]{1,0:T(8,128)(2,1)S(1)} %multiply_convert_fusion.3), channel_id=1, source_target_pairs={{0,24},{8,0},{16,8},{24,16},{1,25},{9,1},{17,9},{25,17},{2,26},{10... | collective-permute-start | bytes 786440 | tf_op jit(solution)/shard_map/ppermute | solution.py:30
  22.3 2.8 %collective-permute-start.5 = (s32[16]{0:T(128)S(1)}, s32[16]{0:T(128)S(1)}, u32[]{:S(2)}, u32[]{:S(2)}) collective-permute-start(s32[16]{0:T(128)S(1)} %bitcast.135), channel_id=1, source_target_pairs={{0,24},{8,0},{16,8},{24,16},{1,25},{9,1},{17,9},{25,17},{2,26},{10... | collective-permute-start | bytes 200 | tf_op jit(solution)/shard_map/ppermute | solution.py:30
  26.8 11.4 %collective-permute-done.5 = s32[16]{0:T(128)S(1)} collective-permute-done((s32[16]{0:T(128)S(1)}, s32[16]{0:T(128)S(1)}, u32[]{:S(2)}, u32[]{:S(2)}) %collective-permute-start.5) | collective-permute-done | bytes 96 | tf_op jit(solution)/shard_map/ppermute | solution.py:30
  38.2 5.3 %collective-permute-start.3 = (s32[16]{0:T(128)S(1)}, s32[16]{0:T(128)S(1)}, u32[]{:S(2)}, u32[]{:S(2)}) collective-permute-start(s32[16]{0:T(128)S(1)} %bitcast.137), channel_id=1, source_target_pairs={{0,8},{8,16},{16,24},{24,0},{1,9},{9,17},{17,25},{25,1},{2,10},{10... | collective-permute-start | bytes 200 | tf_op jit(solution)/shard_map/ppermute | solution.py:30
  43.6 3.4 %collective-permute-start.2 = (f32[128]{0:T(128)S(1)}, f32[128]{0:T(128)S(1)}, u32[]{:S(2)}, u32[]{:S(2)}) collective-permute-start(f32[128]{0:T(128)S(1)} %copy-done.9), channel_id=1, source_target_pairs={{0,24},{8,0},{16,8},{24,16},{1,25},{9,1},{17,9},{25,17},{2,26},{10... | collective-permute-start | bytes 1544 | tf_op jit(solution)/shard_map/ppermute | solution.py:30
  48.4 1.9 collective-permute-done.1
  50.3 1.9 collective-permute-done
  54.7 3.3 %fusion.21 = (f32[4,128]{1,0:T(4,128)S(1)}, f32[4,128,1024]{2,1,0:T(8,128)S(1)}) fusion(bf16[4,128,1024]{2,1,0:T(8,128)(2,1)} %broadcast_select_fusion, bf16[1024,1024]{1,0:T(8,128)(2,1)} %all-gather.4.cloned.1.call-done, pred[4,1024]{1,0:T(4,128)(4,1)S(1)} %broadcast_in_dim.121), kind=kOutput, calls=%fused_computation.91 | convolution fusion | flops 1075314176 | bytes 5249024 | tf_op jit(solution)/shard_map/gqe,ke->gqk/dot_general | solution.py:78
  61.0 2.4 %collective-permute-done.10 = f32[2,4,128]{2,1,0:T(4,128)S(1)} collective-permute-done((f32[2,4,128]{2,1,0:T(4,128)S(1)}, f32[2,4,128]{2,1,0:T(4,128)S(1)}, u32[]{:S(2)}, u32[]{:S(2)}) %collective-permute-start.10) | collective-permute-done | bytes 4128 | tf_op jit(solution)/shard_map/ppermute | solution.py:30
  65.0 1.7 multiply_convert_fusion
  68.9 2.4 %add_convert_fusion = bf16[1024,1024]{1,0:T(8,128)(2,1)} fusion(f32[1024,1024]{1,0:T(8,128)S(1)} %fusion.10, f32[1024,1024]{1,0:T(8,128)S(1)} %fusion.11, f32[1024,1024]{1,0:T(8,128)S(1)} %fusion.12, pred[]{:T(512)S(6)} %eq.75, pred[]{:T(512)S(6)} %eq.74, pred[]{:T(512)S(6)} %eq.73, pred[]{:T(512)S(6)} %eq.72, bf16[4,128,1024]{2,1,0:T(8,128)(2,1)S(1)} %copy-done.5, ...), kind=kOutput, calls=%fused_computation.7 | convolution fusion | flops 285212672 | bytes 15204356 | tf_op jit(solution)/shard_map/dot_general | solution.py:108
  72.5 4.2 %fusion.22 = (bf16[4,128,1024]{2,1,0:T(8,128)(2,1)S(1)}, f32[4,128,1024]{2,1,0:T(8,128)}) fusion(bf16[4,128,1024]{2,1,0:T(8,128)(2,1)S(1)} %copy-done.4, bf16[1024,1024]{1,0:T(8,128)(2,1)} %all-gather.4.cloned.1.call-done), kind=kOutput, calls=%fused_computation.92 | convolution fusion | flops 1074266112 | bytes 6291456 | tf_op jit(solution)/shard_map/gqk,ke->gqe/dot_general | solution.py:101
  78.8 4.4 %collective-permute-done.14 = bf16[128,1024]{1,0:T(8,128)(2,1)S(1)} collective-permute-done((bf16[128,1024]{1,0:T(8,128)(2,1)S(1)}, bf16[128,1024]{1,0:T(8,128)(2,1)S(1)}, u32[]{:S(2)}, u32[]{:S(2)}) %collective-permute-start.14) | collective-permute-done | bytes 262176 | tf_op jit(solution)/shard_map/ppermute | solution.py:41
  83.2 13.5 %collective-permute-done.13 = bf16[128,1024]{1,0:T(8,128)(2,1)S(1)} collective-permute-done((bf16[128,1024]{1,0:T(8,128)(2,1)S(1)}, bf16[128,1024]{1,0:T(8,128)(2,1)S(1)}, u32[]{:S(2)}, u32[]{:S(2)}) %collective-permute-start.13) | collective-permute-done | bytes 262176 | tf_op jit(solution)/shard_map/ppermute | solution.py:41
  100.4 15.3 %reduce-scatter.3.cloned.1.call-done = bf16[128,1024]{1,0:T(8,128)(2,1)} async-done(((bf16[1024,1024]{1,0:T(8,128)(2,1)}), bf16[128,1024]{1,0:T(8,128)(2,1)}) %reduce-scatter.3.cloned.1.call-update) | async-done | bytes 262160 | tf_op jit(solution)/shard_map/reduce_scatter | solution.py:111
  120.7 34.2 %all_to_all.5 = bf16[8,2,128,4,128]{2,4,1,3,0:T(8,128)(2,1)S(1)} all-to-all(bf16[8,2,128,4,128]{2,4,1,3,0:T(8,128)(2,1)S(1)} %copy.20), channel_id=1, replica_groups=mesh['group'=4,'member'=8] {'member'}, dimensions={0} | all-to-all | bytes 4194304 | tf_op jit(solution)/shard_map/all_to_all | solution.py:63
  154.9 13.2 %all-gather.6.cloned.1.call-done = bf16[16,128,1024]{2,1,0:T(8,128)(2,1)} async-done(((bf16[2,128,1024]{2,1,0:T(8,128)(2,1)}), bf16[16,128,1024]{2,1,0:T(8,128)(2,1)}) %all-gather.6.cloned.1.call-update) | async-done | bytes 4194320 | tf_op jit(solution)/shard_map/all_gather | solution.py:124
  168.1 6.2 %select_convert_fusion = (bf16[4,128,1024]{2,1,0:T(8,128)(2,1)}, f32[4,128,1024]{2,1,0:T(8,128)}) fusion(pred[4]{0:T(512)(128)(4,1)S(1)} %iota_compare_fusion.1, bf16[8,2,128,4,128]{2,4,1,3,0:T(8,128)(2,1)S(1)} %all_to_all.5, bf16[8,2,128,1024,1]{3,2,1,4,0:T(8,128)(2,1)} %bitcast.145), kind=kOutput, calls=%fused_computation.13 | convolution fusion | flops 2148007936 | bytes 9437188 | tf_op jit(solution)/shard_map/mtqgr,mtqe->gre/dot_general | solution.py:125
  174.3 7.2 %convolution_convert_fusion.1 = bf16[128,4096]{1,0:T(8,128)(2,1)} fusion(bf16[128,1024]{1,0:T(8,128)(2,1)S(1)} %copy-done.7, bf16[4096,1024]{1,0:T(8,128)(2,1)} %param.13), kind=kOutput, calls=%fused_computation.6 | convolution fusion | flops 1074266112 | bytes 9699328 | tf_op jit(solution)/shard_map/qe,de->qd/dot_general | solution.py:117
  181.6 7.2 %convolution_convert_fusion = bf16[128,4096]{1,0:T(8,128)(2,1)} fusion(bf16[128,1024]{1,0:T(8,128)(2,1)S(1)} %fusion.8, bf16[4096,1024]{1,0:T(8,128)(2,1)} %param.13), kind=kOutput, calls=%fused_computation.5 | convolution fusion | flops 1074266112 | bytes 9699328 | tf_op jit(solution)/shard_map/qe,de->qd/dot_general | solution.py:120
  188.8 12.1 %reduce-scatter.5.cloned.1.call-done = bf16[1,128,1024]{2,1,0:T(8,128)(2,1)} async-done(((bf16[4,128,1024]{2,1,0:T(8,128)(2,1)}), bf16[1,128,1024]{2,1,0:T(8,128)(2,1)}) %reduce-scatter.5.cloned.1.call-update) | async-done | bytes 262160 | tf_op jit(solution)/shard_map/reduce_scatter | solution.py:130
  200.9 2.0 convert_add_fusion
  (101 shorter events, 26.0 us)
Async XLA Ops:
  7.2 47.5 %all-gather.4.cloned.1.call-start = ((), (), s32[]{:S(2)}) async-start(), calls=%async_computation.3 | async-start | bytes 2359296 | tf_op jit(solution)/shard_map/all_gather | solution.py:67
  13.1 9.1 %copy-start.8 = (s32[1,16]{1,0:T(1,128)S(1)}, s32[1,16]{1,0:T(1,128)}, u32[]{:S(2)}) copy-start(s32[1,16]{1,0:T(1,128)} %param.14) | copy-start | bytes 196
  13.1 102.6 %reduce-scatter.3.cloned.1.call-start = ((), (), s32[]{:S(2)}) async-start(), calls=%async_computation.4 | async-start | bytes 2359296 | tf_op jit(solution)/shard_map/reduce_scatter | solution.py:111
  18.3 25.3 %copy-start.9 = (f32[128]{0:T(128)S(1)}, f32[128]{0:T(128)}, u32[]{:S(2)}) copy-start(f32[128]{0:T(128)} %param.15) | copy-start | bytes 1540
  18.4 34.3 %collective-permute-start.8 = (bf16[128,1024]{1,0:T(8,128)(2,1)S(1)}, bf16[128,1024]{1,0:T(8,128)(2,1)S(1)}, u32[]{:S(2)}, u32[]{:S(2)}) collective-permute-start(bf16[128,1024]{1,0:T(8,128)(2,1)S(1)} %multiply_convert_fusion.3), channel_id=1, source_target_pairs={{0,24},{8,0},{16,8},{24,16},{1,25},{9,1},{17,9},{25,17},{2,26},{10... | collective-permute-start | bytes 786440 | tf_op jit(solution)/shard_map/ppermute | solution.py:30
  21.8 31.0 %collective-permute-start.7 = (bf16[128,1024]{1,0:T(8,128)(2,1)S(1)}, bf16[128,1024]{1,0:T(8,128)(2,1)S(1)}, u32[]{:S(2)}, u32[]{:S(2)}) collective-permute-start(bf16[128,1024]{1,0:T(8,128)(2,1)S(1)} %multiply_convert_fusion.3), channel_id=1, source_target_pairs={{0,16},{8,24},{16,0},{24,8},{1,17},{9,25},{17,1},{25,9},{2,18},{10... | collective-permute-start | bytes 786440 | tf_op jit(solution)/shard_map/ppermute | solution.py:30
  21.8 31.0 %collective-permute-start.6 = (bf16[128,1024]{1,0:T(8,128)(2,1)S(1)}, bf16[128,1024]{1,0:T(8,128)(2,1)S(1)}, u32[]{:S(2)}, u32[]{:S(2)}) collective-permute-start(bf16[128,1024]{1,0:T(8,128)(2,1)S(1)} %multiply_convert_fusion.3), channel_id=1, source_target_pairs={{0,8},{8,16},{16,24},{24,0},{1,9},{9,17},{17,25},{25,1},{2,10},{10... | collective-permute-start | bytes 786440 | tf_op jit(solution)/shard_map/ppermute | solution.py:30
  22.3 15.9 %collective-permute-start.5 = (s32[16]{0:T(128)S(1)}, s32[16]{0:T(128)S(1)}, u32[]{:S(2)}, u32[]{:S(2)}) collective-permute-start(s32[16]{0:T(128)S(1)} %bitcast.135), channel_id=1, source_target_pairs={{0,24},{8,0},{16,8},{24,16},{1,25},{9,1},{17,9},{25,17},{2,26},{10... | collective-permute-start | bytes 200 | tf_op jit(solution)/shard_map/ppermute | solution.py:30
  25.1 18.5 %collective-permute-start.4 = (s32[16]{0:T(128)S(1)}, s32[16]{0:T(128)S(1)}, u32[]{:S(2)}, u32[]{:S(2)}) collective-permute-start(s32[16]{0:T(128)S(1)} %bitcast.136), channel_id=1, source_target_pairs={{0,16},{8,24},{16,0},{24,8},{1,17},{9,25},{17,1},{25,9},{2,18},{10... | collective-permute-start | bytes 200 | tf_op jit(solution)/shard_map/ppermute | solution.py:30
  38.2 8.8 %collective-permute-start.3 = (s32[16]{0:T(128)S(1)}, s32[16]{0:T(128)S(1)}, u32[]{:S(2)}, u32[]{:S(2)}) collective-permute-start(s32[16]{0:T(128)S(1)} %bitcast.137), channel_id=1, source_target_pairs={{0,8},{8,16},{16,24},{24,0},{1,9},{9,17},{17,25},{25,1},{2,10},{10... | collective-permute-start | bytes 200 | tf_op jit(solution)/shard_map/ppermute | solution.py:30
  43.6 4.2 %collective-permute-start.2 = (f32[128]{0:T(128)S(1)}, f32[128]{0:T(128)S(1)}, u32[]{:S(2)}, u32[]{:S(2)}) collective-permute-start(f32[128]{0:T(128)S(1)} %copy-done.9), channel_id=1, source_target_pairs={{0,24},{8,0},{16,8},{24,16},{1,25},{9,1},{17,9},{25,17},{2,26},{10... | collective-permute-start | bytes 1544 | tf_op jit(solution)/shard_map/ppermute | solution.py:30
  47.0 3.3 %collective-permute-start.1 = (f32[128]{0:T(128)S(1)}, f32[128]{0:T(128)S(1)}, u32[]{:S(2)}, u32[]{:S(2)}) collective-permute-start(f32[128]{0:T(128)S(1)} %copy-done.9), channel_id=1, source_target_pairs={{0,16},{8,24},{16,0},{24,8},{1,17},{9,25},{17,1},{25,9},{2,18},{10... | collective-permute-start | bytes 1544 | tf_op jit(solution)/shard_map/ppermute | solution.py:30
  47.8 4.4 %collective-permute-start = (f32[128]{0:T(128)S(1)}, f32[128]{0:T(128)S(1)}, u32[]{:S(2)}, u32[]{:S(2)}) collective-permute-start(f32[128]{0:T(128)S(1)} %copy-done.9), channel_id=1, source_target_pairs={{0,8},{8,16},{16,24},{24,0},{1,9},{9,17},{17,25},{25,1},{2,10},{10... | collective-permute-start | bytes 1544 | tf_op jit(solution)/shard_map/ppermute | solution.py:30
  58.5 2.5 %collective-permute-start.11 = (f32[2,4,128]{2,1,0:T(4,128)S(1)}, f32[2,4,128]{2,1,0:T(4,128)S(1)}, u32[]{:S(2)}, u32[]{:S(2)}) collective-permute-start(f32[2,4,128]{2,1,0:T(4,128)S(1)} %get-tuple-element.33), channel_id=1, source_target_pairs={{0,24},{8,0},{16,8},{24,16},{1,25},{9,1},{17,9},{25,17},{2,26},{10... | collective-permute-start | bytes 12296 | tf_op jit(solution)/shard_map/ppermute | solution.py:30
  60.0 3.4 %collective-permute-start.10 = (f32[2,4,128]{2,1,0:T(4,128)S(1)}, f32[2,4,128]{2,1,0:T(4,128)S(1)}, u32[]{:S(2)}, u32[]{:S(2)}) collective-permute-start(f32[2,4,128]{2,1,0:T(4,128)S(1)} %get-tuple-element.33), channel_id=1, source_target_pairs={{0,16},{8,24},{16,0},{24,8},{1,17},{9,25},{17,1},{25,9},{2,18},{10... | collective-permute-start | bytes 12296 | tf_op jit(solution)/shard_map/ppermute | solution.py:30
  60.0 4.3 %collective-permute-start.9 = (f32[2,4,128]{2,1,0:T(4,128)S(1)}, f32[2,4,128]{2,1,0:T(4,128)S(1)}, u32[]{:S(2)}, u32[]{:S(2)}) collective-permute-start(f32[2,4,128]{2,1,0:T(4,128)S(1)} %get-tuple-element.33), channel_id=1, source_target_pairs={{0,8},{8,16},{16,24},{24,0},{1,9},{9,17},{17,25},{25,1},{2,10},{10... | collective-permute-start | bytes 12296 | tf_op jit(solution)/shard_map/ppermute | solution.py:30
  71.3 96.8 %all-gather.6.cloned.1.call-start = ((), (), s32[]{:S(2)}) async-start(), calls=%async_computation.6 | async-start | bytes 4718592 | tf_op jit(solution)/shard_map/all_gather | solution.py:124
  76.7 6.5 %collective-permute-start.14 = (bf16[128,1024]{1,0:T(8,128)(2,1)S(1)}, bf16[128,1024]{1,0:T(8,128)(2,1)S(1)}, u32[]{:S(2)}, u32[]{:S(2)}) collective-permute-start(bf16[128,1024]{1,0:T(8,128)(2,1)S(1)} %get-tuple-element.29), channel_id=1, source_target_pairs={{0,24},{8,0},{16,8},{24,16},{1,25},{9,1},{17,9},{25,17},{2,26},{10... | collective-permute-start | bytes 786440 | tf_op jit(solution)/shard_map/ppermute | solution.py:41
  77.1 19.7 %collective-permute-start.13 = (bf16[128,1024]{1,0:T(8,128)(2,1)S(1)}, bf16[128,1024]{1,0:T(8,128)(2,1)S(1)}, u32[]{:S(2)}, u32[]{:S(2)}) collective-permute-start(bf16[128,1024]{1,0:T(8,128)(2,1)S(1)} %get-tuple-element.30), channel_id=1, source_target_pairs={{0,16},{8,24},{16,0},{24,8},{1,17},{9,25},{17,1},{25,9},{2,18},{10... | collective-permute-start | bytes 786440 | tf_op jit(solution)/shard_map/ppermute | solution.py:41
  77.4 19.4 %collective-permute-start.12 = (bf16[128,1024]{1,0:T(8,128)(2,1)S(1)}, bf16[128,1024]{1,0:T(8,128)(2,1)S(1)}, u32[]{:S(2)}, u32[]{:S(2)}) collective-permute-start(bf16[128,1024]{1,0:T(8,128)(2,1)S(1)} %get-tuple-element.31), channel_id=1, source_target_pairs={{0,8},{8,16},{16,24},{24,0},{1,9},{9,17},{17,25},{25,1},{2,10},{10... | collective-permute-start | bytes 786440 | tf_op jit(solution)/shard_map/ppermute | solution.py:41
  100.4 18.5 %copy-start.6 = (bf16[128,1024]{1,0:T(8,128)(2,1)}, bf16[128,1024]{1,0:T(8,128)(2,1)S(1)}, u32[]{:S(2)}) copy-start(bf16[128,1024]{1,0:T(8,128)(2,1)S(1)} %multiply_convert_fusion.1) | copy-start | bytes 786436
  100.4 18.5 %copy-start = (bf16[128,4096]{1,0:T(8,128)(2,1)S(1)}, bf16[128,4096]{1,0:T(8,128)(2,1)}, u32[]{:S(2)}) copy-start(bf16[128,4096]{1,0:T(8,128)(2,1)} %param.12) | copy-start | bytes 3145732
  118.9 82.1 %reduce-scatter.5.cloned.1.call-start = ((), (), s32[]{:S(2)}) async-start(), calls=%async_computation.5 | async-start | bytes 1310720 | tf_op jit(solution)/shard_map/reduce_scatter | solution.py:130
  168.1 6.3 %copy-start.7 = (bf16[128,1024]{1,0:T(8,128)(2,1)S(1)}, bf16[128,1024]{1,0:T(8,128)(2,1)}, u32[]{:S(2)}) copy-start(bf16[128,1024]{1,0:T(8,128)(2,1)} %copy-done.6) | copy-start | bytes 786436
  (5 other events, 8.2 us)
Sparse Core Ops, SparseCore 0:
  13.2 29.3 all-gather.3
  71.4 44.2 reduce-scatter.2
  119.0 49.0 all-gather.5
  174.4 26.4 reduce-scatter.4

commit v7 on v6

--- a/solution.py
+++ b/solution.py
@@ -108,9 +108,20 @@
         term = jnp.dot(grad[g].T, q_all[g], preferred_element_type=jnp.float32)
         term = jnp.where(g == group_index, term, term.astype(jnp.bfloat16).astype(jnp.float32))
         code_terms = term if code_terms is None else code_terms + term
-    code_delta = lax.psum_scatter(
-        code_terms.astype(jnp.bfloat16), "member", scatter_dimension=0, tiled=True
+    halves = code_terms.astype(jnp.bfloat16).reshape(members, 2, queries_dev // 2, emb_width)
+    first_half = lax.psum_scatter(
+        halves[:, 0].reshape(members * queries_dev // 2, emb_width),
+        "member",
+        scatter_dimension=0,
+        tiled=True,
     ).astype(jnp.float32)
+    second_half = jnp.sum(
+        lax.all_to_all(halves[:, 1], "member", split_axis=0, concat_axis=0, tiled=True).astype(
+            jnp.float32
+        ),
+        axis=0,
+    )
+    code_delta = jnp.concatenate([first_half, second_half], axis=0)
 
     dz_query = norm_back(query_delta, q_unit, q_inv)
     dz_code = norm_back(code_delta, c_unit, c_inv)

time: 212 us -> 209 us (0.986)
  waiting for transfers between devices: 77.6 us -> 62.9 us
  starting transfers between devices: 20.6 us -> 30.8 us
    all_to_all x0 -> x1, starting transfers between devices: none -> 10.2 us  [body(): lax.all_to_all(halves[:, 1], 'member', split_axis=0, concat_axis=0, tiled...]
    ppermute x3, waiting for transfers between devices: 18 us -> 8.02 us  [exchange(): lax.ppermute(sent, axis, [(i, (i + s) % size) for i in range(size)])]
    reduce_scatter x1, waiting for transfers between devices: 15.3 us -> 8.94 us  [body(): lax.psum_scatter(halves[:, 0].reshape(members * queries_dev // 2, emb_wid...]
  transfers between devices with their start and end apart: 19 -> 20, of which waited for: 11 -> 11; matrix products, arithmetic and copies ran while one was open for 16% -> 18% of each run, Pallas kernels for 0% -> 0%
where the time goes in v7:
time: 209 us; the launch traced here: 207 us
  waiting for transfers between devices  62.9 us (30%)
  matrix products  41.2 us (20%)
  blocking collectives  34.4 us (16%)
  starting transfers between devices  30.8 us (15%)
  other arithmetic  15.7 us (8%)
  between operations  14.1 us (7%)
  local copies, waits for them, and re-layouts  7.63 us (4%)
    all_to_all x1, blocking collectives, body(): lax.all_to_all(feats, 'member', split_axis=0, concat_axis=0, tiled=True)  34.4 us
    ppermute x12, waiting for transfers between devices, shift_all(): lax.ppermute(x, axis, [(i, (i + s) % size) for i in range(size)])  19 us
    ppermute x12, starting transfers between devices, shift_all(): lax.ppermute(x, axis, [(i, (i + s) % size) for i in range(size)])  18.3 us
    all_gather x1, waiting for transfers between devices, body(): lax.all_gather(jnp.stack([dz_query, dz_code], axis=0), 'member', axis=0)  13.2 us
    reduce_scatter x1, waiting for transfers between devices, body(): lax.psum_scatter(sent_proj, 'group', scatter_dimension=0, tiled=True)  12.1 us
    all_to_all x1, starting transfers between devices, body(): lax.all_to_all(halves[:, 1], 'member', split_axis=0, concat_axis=0, tiled...  10.2 us
    dot_general x2, matrix products, embed(): values = jnp.dot(features, projection, preferred_element_type=jnp.float32)  9.77 us
    reduce_scatter x1, waiting for transfers between devices, body(): lax.psum_scatter(halves[:, 0].reshape(members * queries_dev // 2, emb_wid...  8.94 us
  transfers between devices with their start and end apart: 20, of which 11 were waited for; matrix products, arithmetic and copies ran while one was open for 18% of the time, Pallas kernels for 0%

profile of v7, /device:TPU:3, one launch (start us, length us, event | category | flops | bytes accessed | tf_op | source)
XLA Modules:
  0.0 206.6 jit_solution(17163878826239197533)
XLA Ops:
  7.2 5.1 %multiply_reduce_fusion.2 = (f32[128]{0:T(128)S(1)}, f32[128,1024]{1,0:T(8,128)S(1)}) fusion(bf16[128,4096]{1,0:T(8,128)(2,1)} %param.12, bf16[4096,1024]{1,0:T(8,128)(2,1)} %param.13), kind=kOutput, calls=%fused_computation.33 | convolution fusion | flops 1074003840 | bytes 9961984 | tf_op jit(solution)/shard_map/dot_general | solution.py:14
  13.6 4.7 %multiply_reduce_fusion.3 = (f32[128]{0:T(128)S(1)}, f32[128,1024]{1,0:T(8,128)S(1)}) fusion(bf16[128,4096]{1,0:T(8,128)(2,1)S(1)} %copy-done.1, bf16[4096,1024]{1,0:T(8,128)(2,1)} %param.13), kind=kOutput, calls=%fused_computation.34 | convolution fusion | flops 1074003840 | bytes 9961984 | tf_op jit(solution)/shard_map/dot_general | solution.py:14
  18.4 3.4 %collective-permute-start.8 = (bf16[128,1024]{1,0:T(8,128)(2,1)S(1)}, bf16[128,1024]{1,0:T(8,128)(2,1)S(1)}, u32[]{:S(2)}, u32[]{:S(2)}) collective-permute-start(bf16[128,1024]{1,0:T(8,128)(2,1)S(1)} %multiply_convert_fusion.4), channel_id=1, source_target_pairs={{0,24},{8,0},{16,8},{24,16},{1,25},{9,1},{17,9},{25,17},{2,26},{10... | collective-permute-start | bytes 786440 | tf_op jit(solution)/shard_map/ppermute | solution.py:30
  22.3 2.8 %collective-permute-start.5 = (s32[16]{0:T(128)S(1)}, s32[16]{0:T(128)S(1)}, u32[]{:S(2)}, u32[]{:S(2)}) collective-permute-start(s32[16]{0:T(128)S(1)} %bitcast.141), channel_id=1, source_target_pairs={{0,24},{8,0},{16,8},{24,16},{1,25},{9,1},{17,9},{25,17},{2,26},{10... | collective-permute-start | bytes 200 | tf_op jit(solution)/shard_map/ppermute | solution.py:30
  26.8 11.4 %collective-permute-done.5 = s32[16]{0:T(128)S(1)} collective-permute-done((s32[16]{0:T(128)S(1)}, s32[16]{0:T(128)S(1)}, u32[]{:S(2)}, u32[]{:S(2)}) %collective-permute-start.5) | collective-permute-done | bytes 96 | tf_op jit(solution)/shard_map/ppermute | solution.py:30
  38.2 5.3 %collective-permute-start.3 = (s32[16]{0:T(128)S(1)}, s32[16]{0:T(128)S(1)}, u32[]{:S(2)}, u32[]{:S(2)}) collective-permute-start(s32[16]{0:T(128)S(1)} %bitcast.143), channel_id=1, source_target_pairs={{0,8},{8,16},{16,24},{24,0},{1,9},{9,17},{17,25},{25,1},{2,10},{10... | collective-permute-start | bytes 200 | tf_op jit(solution)/shard_map/ppermute | solution.py:30
  43.6 3.4 %collective-permute-start.2 = (f32[128]{0:T(128)S(1)}, f32[128]{0:T(128)S(1)}, u32[]{:S(2)}, u32[]{:S(2)}) collective-permute-start(f32[128]{0:T(128)S(1)} %copy-done.10), channel_id=1, source_target_pairs={{0,24},{8,0},{16,8},{24,16},{1,25},{9,1},{17,9},{25,17},{2,26},{10... | collective-permute-start | bytes 1544 | tf_op jit(solution)/shard_map/ppermute | solution.py:30
  48.4 1.9 collective-permute-done.1
  50.3 1.9 collective-permute-done
  54.7 3.3 %fusion.19 = (f32[4,128]{1,0:T(4,128)S(1)}, f32[4,128,1024]{2,1,0:T(8,128)S(1)}) fusion(bf16[4,128,1024]{2,1,0:T(8,128)(2,1)} %broadcast_select_fusion, bf16[1024,1024]{1,0:T(8,128)(2,1)} %all-gather.4.cloned.1.call-done, pred[4,1024]{1,0:T(4,128)(4,1)S(1)} %broadcast_in_dim.121), kind=kOutput, calls=%fused_computation.92 | convolution fusion | flops 1075314176 | bytes 5249024 | tf_op jit(solution)/shard_map/gqe,ke->gqk/dot_general | solution.py:78
  61.0 2.4 %collective-permute-done.10 = f32[2,4,128]{2,1,0:T(4,128)S(1)} collective-permute-done((f32[2,4,128]{2,1,0:T(4,128)S(1)}, f32[2,4,128]{2,1,0:T(4,128)S(1)}, u32[]{:S(2)}, u32[]{:S(2)}) %collective-permute-start.10) | collective-permute-done | bytes 4128 | tf_op jit(solution)/shard_map/ppermute | solution.py:30
  65.0 1.7 multiply_convert_fusion
  71.5 4.2 %fusion.20 = (bf16[4,128,1024]{2,1,0:T(8,128)(2,1)S(1)}, f32[4,128,1024]{2,1,0:T(8,128)}) fusion(bf16[4,128,1024]{2,1,0:T(8,128)(2,1)S(1)} %copy-done.4, bf16[1024,1024]{1,0:T(8,128)(2,1)} %all-gather.4.cloned.1.call-done), kind=kOutput, calls=%fused_computation.93 | convolution fusion | flops 1074266112 | bytes 6291456 | tf_op jit(solution)/shard_map/gqk,ke->gqe/dot_general | solution.py:101
  77.8 10.2 %all-to-all-start = ((bf16[8,64,1024]{2,1,0:T(8,128)(2,1)}), bf16[8,64,1024]{2,1,0:T(8,128)(2,1)S(1)}, u32[]{:S(2)}, u32[]{:S(2)}) async-start(bf16[8,64,1024]{2,1,0:T(8,128)(2,1)} %get-tuple-element.29), calls=%async_computation.1 | async-start | bytes 2097152 | tf_op jit(solution)/shard_map/all_to_all | solution.py:119
  88.1 8.0 %collective-permute-done.13 = bf16[128,1024]{1,0:T(8,128)(2,1)} collective-permute-done((bf16[128,1024]{1,0:T(8,128)(2,1)S(1)}, bf16[128,1024]{1,0:T(8,128)(2,1)}, u32[]{:S(2)}, u32[]{:S(2)}) %collective-permute-start.13) | collective-permute-done | bytes 262176 | tf_op jit(solution)/shard_map/ppermute | solution.py:41
  98.9 1.6 select_reduce_fusion
  104.8 8.9 %reduce-scatter.3.cloned.1.call-done = bf16[64,1024]{1,0:T(8,128)(2,1)} async-done(((bf16[512,1024]{1,0:T(8,128)(2,1)}), bf16[64,1024]{1,0:T(8,128)(2,1)}) %reduce-scatter.3.cloned.1.call-update) | async-done | bytes 131088 | tf_op jit(solution)/shard_map/reduce_scatter | solution.py:112
  117.8 34.4 %all_to_all.10 = bf16[8,2,128,4,128]{2,4,1,3,0:T(8,128)(2,1)S(1)} all-to-all(bf16[8,2,128,4,128]{2,4,1,3,0:T(8,128)(2,1)S(1)} %copy.24), channel_id=1, replica_groups=mesh['group'=4,'member'=8] {'member'}, dimensions={0} | all-to-all | bytes 4194304 | tf_op jit(solution)/shard_map/all_to_all | solution.py:63
  152.1 13.2 %all-gather.6.cloned.1.call-done = bf16[16,128,1024]{2,1,0:T(8,128)(2,1)} async-done(((bf16[2,128,1024]{2,1,0:T(8,128)(2,1)}), bf16[16,128,1024]{2,1,0:T(8,128)(2,1)}) %all-gather.6.cloned.1.call-update) | async-done | bytes 4194320 | tf_op jit(solution)/shard_map/all_gather | solution.py:135
  165.3 6.2 %select_convert_fusion = (bf16[4,128,1024]{2,1,0:T(8,128)(2,1)}, f32[4,128,1024]{2,1,0:T(8,128)}) fusion(pred[4]{0:T(512)(128)(4,1)S(1)} %iota_compare_fusion.1, bf16[8,2,128,4,128]{2,4,1,3,0:T(8,128)(2,1)S(1)} %all_to_all.10, bf16[8,2,128,1024,1]{3,2,1,4,0:T(8,128)(2,1)} %bitcast.151), kind=kOutput, calls=%fused_computation.13 | convolution fusion | flops 2148007936 | bytes 9437188 | tf_op jit(solution)/shard_map/mtqgr,mtqe->gre/dot_general | solution.py:136
  171.5 7.3 %convolution_convert_fusion.1 = bf16[128,4096]{1,0:T(8,128)(2,1)} fusion(bf16[128,1024]{1,0:T(8,128)(2,1)S(1)} %multiply_convert_fusion.2, bf16[4096,1024]{1,0:T(8,128)(2,1)} %param.13), kind=kOutput, calls=%fused_computation.6 | convolution fusion | flops 1074266112 | bytes 9699328 | tf_op jit(solution)/shard_map/qe,de->qd/dot_general | solution.py:128
  178.8 7.2 %convolution_convert_fusion = bf16[128,4096]{1,0:T(8,128)(2,1)} fusion(bf16[128,1024]{1,0:T(8,128)(2,1)S(1)} %copy-done.7, bf16[4096,1024]{1,0:T(8,128)(2,1)} %param.13), kind=kOutput, calls=%fused_computation.5 | convolution fusion | flops 1074266112 | bytes 9699328 | tf_op jit(solution)/shard_map/qe,de->qd/dot_general | solution.py:131
  186.0 12.1 %reduce-scatter.5.cloned.1.call-done = bf16[1,128,1024]{2,1,0:T(8,128)(2,1)} async-done(((bf16[4,128,1024]{2,1,0:T(8,128)(2,1)}), bf16[1,128,1024]{2,1,0:T(8,128)(2,1)}) %reduce-scatter.5.cloned.1.call-update) | async-done | bytes 262160 | tf_op jit(solution)/shard_map/reduce_scatter | solution.py:141
  198.1 2.0 convert_add_fusion
  (108 shorter events, 29.9 us)
Async XLA Ops:
  7.2 47.5 %all-gather.4.cloned.1.call-start = ((), (), s32[]{:S(2)}) async-start(), calls=%async_computation.4 | async-start | bytes 2359296 | tf_op jit(solution)/shard_map/all_gather | solution.py:67
  13.1 9.1 %copy-start.9 = (s32[1,16]{1,0:T(1,128)S(1)}, s32[1,16]{1,0:T(1,128)}, u32[]{:S(2)}) copy-start(s32[1,16]{1,0:T(1,128)} %param.14) | copy-start | bytes 196
  13.1 100.6 %reduce-scatter.3.cloned.1.call-start = ((), (), s32[]{:S(2)}) async-start(), calls=%async_computation.5 | async-start | bytes 1179648 | tf_op jit(solution)/shard_map/reduce_scatter | solution.py:112
  18.3 25.3 %copy-start.10 = (f32[128]{0:T(128)S(1)}, f32[128]{0:T(128)}, u32[]{:S(2)}) copy-start(f32[128]{0:T(128)} %param.15) | copy-start | bytes 1540
  18.4 34.3 %collective-permute-start.8 = (bf16[128,1024]{1,0:T(8,128)(2,1)S(1)}, bf16[128,1024]{1,0:T(8,128)(2,1)S(1)}, u32[]{:S(2)}, u32[]{:S(2)}) collective-permute-start(bf16[128,1024]{1,0:T(8,128)(2,1)S(1)} %multiply_convert_fusion.4), channel_id=1, source_target_pairs={{0,24},{8,0},{16,8},{24,16},{1,25},{9,1},{17,9},{25,17},{2,26},{10... | collective-permute-start | bytes 786440 | tf_op jit(solution)/shard_map/ppermute | solution.py:30
  21.8 31.0 %collective-permute-start.7 = (bf16[128,1024]{1,0:T(8,128)(2,1)S(1)}, bf16[128,1024]{1,0:T(8,128)(2,1)S(1)}, u32[]{:S(2)}, u32[]{:S(2)}) collective-permute-start(bf16[128,1024]{1,0:T(8,128)(2,1)S(1)} %multiply_convert_fusion.4), channel_id=1, source_target_pairs={{0,16},{8,24},{16,0},{24,8},{1,17},{9,25},{17,1},{25,9},{2,18},{10... | collective-permute-start | bytes 786440 | tf_op jit(solution)/shard_map/ppermute | solution.py:30
  21.8 31.0 %collective-permute-start.6 = (bf16[128,1024]{1,0:T(8,128)(2,1)S(1)}, bf16[128,1024]{1,0:T(8,128)(2,1)S(1)}, u32[]{:S(2)}, u32[]{:S(2)}) collective-permute-start(bf16[128,1024]{1,0:T(8,128)(2,1)S(1)} %multiply_convert_fusion.4), channel_id=1, source_target_pairs={{0,8},{8,16},{16,24},{24,0},{1,9},{9,17},{17,25},{25,1},{2,10},{10... | collective-permute-start | bytes 786440 | tf_op jit(solution)/shard_map/ppermute | solution.py:30
  22.3 15.9 %collective-permute-start.5 = (s32[16]{0:T(128)S(1)}, s32[16]{0:T(128)S(1)}, u32[]{:S(2)}, u32[]{:S(2)}) collective-permute-start(s32[16]{0:T(128)S(1)} %bitcast.141), channel_id=1, source_target_pairs={{0,24},{8,0},{16,8},{24,16},{1,25},{9,1},{17,9},{25,17},{2,26},{10... | collective-permute-start | bytes 200 | tf_op jit(solution)/shard_map/ppermute | solution.py:30
  25.1 18.5 %collective-permute-start.4 = (s32[16]{0:T(128)S(1)}, s32[16]{0:T(128)S(1)}, u32[]{:S(2)}, u32[]{:S(2)}) collective-permute-start(s32[16]{0:T(128)S(1)} %bitcast.142), channel_id=1, source_target_pairs={{0,16},{8,24},{16,0},{24,8},{1,17},{9,25},{17,1},{25,9},{2,18},{10... | collective-permute-start | bytes 200 | tf_op jit(solution)/shard_map/ppermute | solution.py:30
  38.2 8.8 %collective-permute-start.3 = (s32[16]{0:T(128)S(1)}, s32[16]{0:T(128)S(1)}, u32[]{:S(2)}, u32[]{:S(2)}) collective-permute-start(s32[16]{0:T(128)S(1)} %bitcast.143), channel_id=1, source_target_pairs={{0,8},{8,16},{16,24},{24,0},{1,9},{9,17},{17,25},{25,1},{2,10},{10... | collective-permute-start | bytes 200 | tf_op jit(solution)/shard_map/ppermute | solution.py:30
  43.6 4.2 %collective-permute-start.2 = (f32[128]{0:T(128)S(1)}, f32[128]{0:T(128)S(1)}, u32[]{:S(2)}, u32[]{:S(2)}) collective-permute-start(f32[128]{0:T(128)S(1)} %copy-done.10), channel_id=1, source_target_pairs={{0,24},{8,0},{16,8},{24,16},{1,25},{9,1},{17,9},{25,17},{2,26},{10... | collective-permute-start | bytes 1544 | tf_op jit(solution)/shard_map/ppermute | solution.py:30
  47.0 3.3 %collective-permute-start.1 = (f32[128]{0:T(128)S(1)}, f32[128]{0:T(128)S(1)}, u32[]{:S(2)}, u32[]{:S(2)}) collective-permute-start(f32[128]{0:T(128)S(1)} %copy-done.10), channel_id=1, source_target_pairs={{0,16},{8,24},{16,0},{24,8},{1,17},{9,25},{17,1},{25,9},{2,18},{10... | collective-permute-start | bytes 1544 | tf_op jit(solution)/shard_map/ppermute | solution.py:30
  47.8 4.4 %collective-permute-start = (f32[128]{0:T(128)S(1)}, f32[128]{0:T(128)S(1)}, u32[]{:S(2)}, u32[]{:S(2)}) collective-permute-start(f32[128]{0:T(128)S(1)} %copy-done.10), channel_id=1, source_target_pairs={{0,8},{8,16},{16,24},{24,0},{1,9},{9,17},{17,25},{25,1},{2,10},{10... | collective-permute-start | bytes 1544 | tf_op jit(solution)/shard_map/ppermute | solution.py:30
  58.5 2.5 %collective-permute-start.11 = (f32[2,4,128]{2,1,0:T(4,128)S(1)}, f32[2,4,128]{2,1,0:T(4,128)S(1)}, u32[]{:S(2)}, u32[]{:S(2)}) collective-permute-start(f32[2,4,128]{2,1,0:T(4,128)S(1)} %get-tuple-element.35), channel_id=1, source_target_pairs={{0,24},{8,0},{16,8},{24,16},{1,25},{9,1},{17,9},{25,17},{2,26},{10... | collective-permute-start | bytes 12296 | tf_op jit(solution)/shard_map/ppermute | solution.py:30
  60.0 3.4 %collective-permute-start.10 = (f32[2,4,128]{2,1,0:T(4,128)S(1)}, f32[2,4,128]{2,1,0:T(4,128)S(1)}, u32[]{:S(2)}, u32[]{:S(2)}) collective-permute-start(f32[2,4,128]{2,1,0:T(4,128)S(1)} %get-tuple-element.35), channel_id=1, source_target_pairs={{0,16},{8,24},{16,0},{24,8},{1,17},{9,25},{17,1},{25,9},{2,18},{10... | collective-permute-start | bytes 12296 | tf_op jit(solution)/shard_map/ppermute | solution.py:30
  60.0 4.3 %collective-permute-start.9 = (f32[2,4,128]{2,1,0:T(4,128)S(1)}, f32[2,4,128]{2,1,0:T(4,128)S(1)}, u32[]{:S(2)}, u32[]{:S(2)}) collective-permute-start(f32[2,4,128]{2,1,0:T(4,128)S(1)} %get-tuple-element.35), channel_id=1, source_target_pairs={{0,8},{8,16},{16,24},{24,0},{1,9},{9,17},{17,25},{25,1},{2,10},{10... | collective-permute-start | bytes 12296 | tf_op jit(solution)/shard_map/ppermute | solution.py:30
  75.8 12.3 %collective-permute-start.14 = (bf16[128,1024]{1,0:T(8,128)(2,1)S(1)}, bf16[128,1024]{1,0:T(8,128)(2,1)S(1)}, u32[]{:S(2)}, u32[]{:S(2)}) collective-permute-start(bf16[128,1024]{1,0:T(8,128)(2,1)S(1)} %get-tuple-element.31), channel_id=1, source_target_pairs={{0,24},{8,0},{16,8},{24,16},{1,25},{9,1},{17,9},{25,17},{2,26},{10... | collective-permute-start | bytes 786440 | tf_op jit(solution)/shard_map/ppermute | solution.py:41
  76.1 20.0 %collective-permute-start.13 = (bf16[128,1024]{1,0:T(8,128)(2,1)S(1)}, bf16[128,1024]{1,0:T(8,128)(2,1)}, u32[]{:S(2)}, u32[]{:S(2)}) collective-permute-start(bf16[128,1024]{1,0:T(8,128)(2,1)S(1)} %get-tuple-element.32), channel_id=1, source_target_pairs={{0,16},{8,24},{16,0},{24,8},{1,17},{9,25},{17,1},{25,9},{2,18},{10... | collective-permute-start | bytes 786440 | tf_op jit(solution)/shard_map/ppermute | solution.py:41
  76.5 19.6 %collective-permute-start.12 = (bf16[128,1024]{1,0:T(8,128)(2,1)S(1)}, bf16[128,1024]{1,0:T(8,128)(2,1)}, u32[]{:S(2)}, u32[]{:S(2)}) collective-permute-start(bf16[128,1024]{1,0:T(8,128)(2,1)S(1)} %get-tuple-element.33), channel_id=1, source_target_pairs={{0,8},{8,16},{16,24},{24,0},{1,9},{9,17},{17,25},{25,1},{2,10},{10... | collective-permute-start | bytes 786440 | tf_op jit(solution)/shard_map/ppermute | solution.py:41
  77.8 26.7 %all-to-all-start = ((bf16[8,64,1024]{2,1,0:T(8,128)(2,1)}), bf16[8,64,1024]{2,1,0:T(8,128)(2,1)S(1)}, u32[]{:S(2)}, u32[]{:S(2)}) async-start(bf16[8,64,1024]{2,1,0:T(8,128)(2,1)} %get-tuple-element.29), calls=%async_computation.1 | async-start | bytes 2097152 | tf_op jit(solution)/shard_map/all_to_all | solution.py:119
  88.1 77.2 %all-gather.6.cloned.1.call-start = ((), (), s32[]{:S(2)}) async-start(), calls=%async_computation.7 | async-start | bytes 4718592 | tf_op jit(solution)/shard_map/all_gather | solution.py:135
  88.1 8.0 %copy-start.8 = (bf16[128,1024]{1,0:T(8,128)(2,1)}, bf16[128,1024]{1,0:T(8,128)(2,1)S(1)}, u32[]{:S(2)}) copy-start(bf16[128,1024]{1,0:T(8,128)(2,1)S(1)} %collective-permute-done.14) | copy-start | bytes 786436
  104.8 11.2 %copy-start = (bf16[128,4096]{1,0:T(8,128)(2,1)S(1)}, bf16[128,4096]{1,0:T(8,128)(2,1)}, u32[]{:S(2)}) copy-start(bf16[128,4096]{1,0:T(8,128)(2,1)} %param.12) | copy-start | bytes 3145732
  115.9 82.2 %reduce-scatter.5.cloned.1.call-start = ((), (), s32[]{:S(2)}) async-start(), calls=%async_computation.6 | async-start | bytes 1310720 | tf_op jit(solution)/shard_map/reduce_scatter | solution.py:141
  (7 other events, 16.7 us)
Sparse Core Ops, SparseCore 0:
  13.2 29.3 all-gather.3
  71.6 42.0 reduce-scatter.2
  116.2 49.0 all-gather.5
  171.6 26.4 reduce-scatter.4

commit v8 on v4

--- a/solution.py
+++ b/solution.py
@@ -60,7 +60,7 @@
         2, queries_dev, groups, members, rows_dev
     )
     feats = jnp.transpose(feats, (3, 0, 1, 2, 4))
-    feat_cols = exchange(feats, "member")
+    feat_cols = lax.all_to_all(feats, "member", split_axis=0, concat_axis=0, tiled=True)
 
     q_unit, q_inv, q_emb = embed(query_feat, projection)
     c_unit, c_inv, c_emb = embed(code_feat, projection)
@@ -108,9 +108,16 @@
         term = jnp.dot(grad[g].T, q_all[g], preferred_element_type=jnp.float32)
         term = jnp.where(g == group_index, term, term.astype(jnp.bfloat16).astype(jnp.float32))
         code_terms = term if code_terms is None else code_terms + term
-    code_delta = lax.psum_scatter(
-        code_terms.astype(jnp.bfloat16), "member", scatter_dimension=0, tiled=True
-    ).astype(jnp.float32)
+    code_delta = jnp.sum(
+        lax.all_to_all(
+            code_terms.astype(jnp.bfloat16).reshape(members, queries_dev, emb_width),
+            "member",
+            split_axis=0,
+            concat_axis=0,
+            tiled=True,
+        ).astype(jnp.float32),
+        axis=0,
+    )
 
     dz_query = norm_back(query_delta, q_unit, q_inv)
     dz_code = norm_back(code_delta, c_unit, c_inv)
@@ -121,7 +128,13 @@
         "qe,de->qd", dz_code, projection, preferred_element_type=jnp.float32
     ).astype(jnp.bfloat16)
 
-    dzq_all = shift_all(dz_query, "member")
+    dzq_all = lax.all_to_all(
+        jnp.broadcast_to(dz_query[None], (members, queries_dev, emb_width)),
+        "member",
+        split_axis=0,
+        concat_axis=0,
+        tiled=True,
+    )
     dzc_all = lax.all_gather(dz_code, "member", axis=0)
     proj_parts = jnp.einsum(
         "mqgr,mqe->gre", feat_cols[:, 0], dzq_all, preferred_element_type=jnp.float32

time: 250 us -> 221 us (0.88)
  local copies, waits for them, and re-layouts: 36.1 us -> 14 us
  other arithmetic: 23.3 us -> 13.9 us
    all_to_all x0 -> x3, waiting for transfers between devices: none -> 39.6 us  [the longest x1 22.3 us: body(): lax.all_to_all(jnp.broadcast_to(dz_query[None], (members, queries_dev, em...]
    all_to_all x0 -> x3, starting transfers between devices: none -> 19.7 us  [the longest x1 9.11 us: body(): lax.all_to_all(code_terms.astype(jnp.bfloat16).reshape(members, queries_d...]
    ppermute x19 -> x12, waiting for transfers between devices: 37 us -> 19 us  [shift_all(): lax.ppermute(x, axis, [(i, (i + s) % size) for i in range(size)])]
    reduce_scatter x1 -> x0, waiting for transfers between devices: 17.4 us -> none  [body(): lax.psum_scatter(code_terms.astype(jnp.bfloat16), 'member', scatter_dimen...]
    unnamed x40 -> x16, local copies, waits for them, and re-layouts: 17.2 us -> 5.12 us
    ppermute x10 -> x3, starting transfers between devices: 13.7 us -> 2.36 us  [exchange(): lax.ppermute(sent, axis, [(i, (i + s) % size) for i in range(size)])]
    gather x3 -> x1, local copies, waits for them, and re-layouts: 7.98 us -> 0.61 us  [exchange(): return jnp.take(stacked, (index - jnp.arange(size)) % size, axis=0)]
    ppermute x19 -> x12, starting transfers between devices: 25.3 us -> 18.3 us  [shift_all(): lax.ppermute(x, axis, [(i, (i + s) % size) for i in range(size)])]
  transfers between devices with their start and end apart: 33 -> 21, of which waited for: 17 -> 11; matrix products, arithmetic and copies ran while one was open for 30% -> 22% of each run, Pallas kernels for 0% -> 0%
where the time goes in v8:
time: 221 us; the launch traced here: 219 us
  waiting for transfers between devices  91.6 us (41%)
  matrix products  44.6 us (20%)
  starting transfers between devices  40.4 us (18%)
  local copies, waits for them, and re-layouts  14 us (6%)
  between operations  14 us (6%)
  other arithmetic  13.9 us (6%)
    all_to_all x1, waiting for transfers between devices, body(): lax.all_to_all(jnp.broadcast_to(dz_query[None], (members, queries_dev, em...  22.3 us
    ppermute x3, waiting for transfers between devices, exchange(): lax.ppermute(sent, axis, [(i, (i + s) % size) for i in range(size)])  21.7 us
    ppermute x12, waiting for transfers between devices, shift_all(): lax.ppermute(x, axis, [(i, (i + s) % size) for i in range(size)])  19 us
    ppermute x12, starting transfers between devices, shift_all(): lax.ppermute(x, axis, [(i, (i + s) % size) for i in range(size)])  18.3 us
    all_to_all x1, waiting for transfers between devices, body(): lax.all_to_all(code_terms.astype(jnp.bfloat16).reshape(members, queries_d...  17.3 us
    reduce_scatter x1, waiting for transfers between devices, body(): lax.psum_scatter(sent_proj, 'group', scatter_dimension=0, tiled=True)  11.2 us
    dot_general x2, matrix products, embed(): values = jnp.dot(features, projection, preferred_element_type=jnp.float32)  9.78 us
    all_to_all x1, starting transfers between devices, body(): lax.all_to_all(code_terms.astype(jnp.bfloat16).reshape(members, queries_d...  9.11 us
  transfers between devices with their start and end apart: 21, of which 11 were waited for; matrix products, arithmetic and copies ran while one was open for 22% of the time, Pallas kernels for 0%

profile of v8, /device:TPU:3, one launch (start us, length us, event | category | flops | bytes accessed | tf_op | source)
XLA Modules:
  0.0 218.5 jit_solution(3696653065767086520)
XLA Ops:
  7.2 5.1 %multiply_reduce_fusion.2 = (f32[128]{0:T(128)S(1)}, f32[128,1024]{1,0:T(8,128)S(1)}) fusion(bf16[128,4096]{1,0:T(8,128)(2,1)} %param.12, bf16[4096,1024]{1,0:T(8,128)(2,1)} %param.13), kind=kOutput, calls=%fused_computation.34 | convolution fusion | flops 1074003840 | bytes 9961984 | tf_op jit(solution)/shard_map/dot_general | solution.py:14
  13.6 4.7 %multiply_reduce_fusion.3 = (f32[128]{0:T(128)S(1)}, f32[128,1024]{1,0:T(8,128)S(1)}) fusion(bf16[128,4096]{1,0:T(8,128)(2,1)S(1)} %copy-done, bf16[4096,1024]{1,0:T(8,128)(2,1)} %param.13), kind=kOutput, calls=%fused_computation.35 | convolution fusion | flops 1074003840 | bytes 9961984 | tf_op jit(solution)/shard_map/dot_general | solution.py:14
  18.4 3.4 %collective-permute-start.8 = (bf16[128,1024]{1,0:T(8,128)(2,1)S(1)}, bf16[128,1024]{1,0:T(8,128)(2,1)S(1)}, u32[]{:S(2)}, u32[]{:S(2)}) collective-permute-start(bf16[128,1024]{1,0:T(8,128)(2,1)S(1)} %multiply_convert_fusion.4), channel_id=1, source_target_pairs={{0,24},{8,0},{16,8},{24,16},{1,25},{9,1},{17,9},{25,17},{2,26},{10... | collective-permute-start | bytes 786440 | tf_op jit(solution)/shard_map/ppermute | solution.py:30
  22.3 2.8 %collective-permute-start.5 = (s32[16]{0:T(128)S(1)}, s32[16]{0:T(128)S(1)}, u32[]{:S(2)}, u32[]{:S(2)}) collective-permute-start(s32[16]{0:T(128)S(1)} %bitcast.144), channel_id=1, source_target_pairs={{0,24},{8,0},{16,8},{24,16},{1,25},{9,1},{17,9},{25,17},{2,26},{10... | collective-permute-start | bytes 200 | tf_op jit(solution)/shard_map/ppermute | solution.py:30
  26.8 11.4 %collective-permute-done.5 = s32[16]{0:T(128)S(1)} collective-permute-done((s32[16]{0:T(128)S(1)}, s32[16]{0:T(128)S(1)}, u32[]{:S(2)}, u32[]{:S(2)}) %collective-permute-start.5) | collective-permute-done | bytes 96 | tf_op jit(solution)/shard_map/ppermute | solution.py:30
  38.2 5.4 %collective-permute-start.3 = (s32[16]{0:T(128)S(1)}, s32[16]{0:T(128)S(1)}, u32[]{:S(2)}, u32[]{:S(2)}) collective-permute-start(s32[16]{0:T(128)S(1)} %bitcast.146), channel_id=1, source_target_pairs={{0,8},{8,16},{16,24},{24,0},{1,9},{9,17},{17,25},{25,1},{2,10},{10... | collective-permute-start | bytes 200 | tf_op jit(solution)/shard_map/ppermute | solution.py:30
  43.6 3.4 %collective-permute-start.2 = (f32[128]{0:T(128)S(1)}, f32[128]{0:T(128)S(1)}, u32[]{:S(2)}, u32[]{:S(2)}) collective-permute-start(f32[128]{0:T(128)S(1)} %copy-done.6), channel_id=1, source_target_pairs={{0,24},{8,0},{16,8},{24,16},{1,25},{9,1},{17,9},{25,17},{2,26},{10... | collective-permute-start | bytes 1544 | tf_op jit(solution)/shard_map/ppermute | solution.py:30
  54.7 3.3 %fusion.21 = (f32[4,128]{1,0:T(4,128)S(1)}, f32[4,128,1024]{2,1,0:T(8,128)S(1)}) fusion(bf16[4,128,1024]{2,1,0:T(8,128)(2,1)} %broadcast_select_fusion, bf16[1024,1024]{1,0:T(8,128)(2,1)} %all-gather.4.cloned.1.call-done, pred[4,1024]{1,0:T(4,128)(4,1)S(1)} %broadcast_in_dim.127), kind=kOutput, calls=%fused_computation.93 | convolution fusion | flops 1075314176 | bytes 5249024 | tf_op jit(solution)/shard_map/gqe,ke->gqk/dot_general | solution.py:78
  61.0 2.4 %collective-permute-done.10 = f32[2,4,128]{2,1,0:T(4,128)S(1)} collective-permute-done((f32[2,4,128]{2,1,0:T(4,128)S(1)}, f32[2,4,128]{2,1,0:T(4,128)S(1)}, u32[]{:S(2)}, u32[]{:S(2)}) %collective-permute-start.10) | collective-permute-done | bytes 4128 | tf_op jit(solution)/shard_map/ppermute | solution.py:30
  68.9 2.4 %add_convert_fusion = bf16[1024,1024]{1,0:T(8,128)(2,1)} fusion(f32[1024,1024]{1,0:T(8,128)S(1)} %fusion.9, f32[1024,1024]{1,0:T(8,128)S(1)} %fusion.10, f32[1024,1024]{1,0:T(8,128)S(1)} %fusion.11, pred[]{:T(512)S(6)} %eq.75, pred[]{:T(512)S(6)} %eq.74, pred[]{:T(512)S(6)} %eq.73, pred[]{:T(512)S(6)} %eq.72, bf16[4,128,1024]{2,1,0:T(8,128)(2,1)S(1)} %copy-done.3, ...), kind=kOutput, calls=%fused_computation.8 | convolution fusion | flops 285212672 | bytes 15204356 | tf_op jit(solution)/shard_map/dot_general | solution.py:108
  71.3 9.1 %all-to-all-start = ((bf16[8,128,1024]{2,1,0:T(8,128)(2,1)}), bf16[8,128,1024]{2,1,0:T(8,128)(2,1)S(1)}, u32[]{:S(2)}, u32[]{:S(2)}) async-start(bf16[8,128,1024]{2,1,0:T(8,128)(2,1)} %bitcast.129), calls=%async_computation | async-start | bytes 4194304 | tf_op jit(solution)/shard_map/all_to_all | solution.py:112
  88.1 17.3 %all-to-all-done = bf16[8,128,1024]{2,1,0:T(8,128)(2,1)S(1)} async-done(((bf16[8,128,1024]{2,1,0:T(8,128)(2,1)}), bf16[8,128,1024]{2,1,0:T(8,128)(2,1)S(1)}, u32[]{:S(2)}, u32[]{:S(2)}) %all-to-all-start) | async-done | bytes 2097184 | tf_op jit(solution)/shard_map/all_to_all | solution.py:112
  105.4 5.8 %all-to-all-start.1 = ((bf16[8,2,128,4,128]{2,4,3,1,0:T(8,128)(2,1)}), bf16[8,2,128,4,128]{2,4,3,1,0:T(8,128)(2,1)}, u32[]{:S(2)}, u32[]{:S(2)}) async-start(bf16[8,2,128,4,128]{2,4,3,1,0:T(8,128)(2,1)} %copy.23), calls=%async_computation.1 | async-start | bytes 4194304 | tf_op jit(solution)/shard_map/all_to_all | solution.py:63
  112.8 4.2 %fusion.22 = (bf16[4,128,1024]{2,1,0:T(8,128)(2,1)S(1)}, f32[4,128,1024]{2,1,0:T(8,128)}) fusion(bf16[4,128,1024]{2,1,0:T(8,128)(2,1)S(1)} %copy-done.2, bf16[1024,1024]{1,0:T(8,128)(2,1)} %all-gather.4.cloned.1.call-done), kind=kOutput, calls=%fused_computation.94 | convolution fusion | flops 1074266112 | bytes 6291456 | tf_op jit(solution)/shard_map/gqk,ke->gqe/dot_general | solution.py:101
  119.5 5.6 %collective-permute-done.14 = bf16[128,1024]{1,0:T(8,128)(2,1)S(1)} collective-permute-done((bf16[128,1024]{1,0:T(8,128)(2,1)S(1)}, bf16[128,1024]{1,0:T(8,128)(2,1)S(1)}, u32[]{:S(2)}, u32[]{:S(2)}) %collective-permute-start.14) | collective-permute-done | bytes 262176 | tf_op jit(solution)/shard_map/ppermute | solution.py:41
  125.1 16.1 %collective-permute-done.13 = bf16[128,1024]{1,0:T(8,128)(2,1)S(1)} collective-permute-done((bf16[128,1024]{1,0:T(8,128)(2,1)S(1)}, bf16[128,1024]{1,0:T(8,128)(2,1)S(1)}, u32[]{:S(2)}, u32[]{:S(2)}) %collective-permute-start.13) | collective-permute-done | bytes 262176 | tf_op jit(solution)/shard_map/ppermute | solution.py:41
  146.3 4.8 %all-to-all-start.2 = ((bf16[8,128,1024]{2,1,0:T(8,128)(2,1)}), bf16[8,128,1024]{2,1,0:T(8,128)(2,1)S(1)}, u32[]{:S(2)}, u32[]{:S(2)}) async-start(bf16[8,128,1024]{2,1,0:T(8,128)(2,1)} %broadcast_in_dim.135), calls=%async_computation.2 | async-start | bytes 4194304 | tf_op jit(solution)/shard_map/all_to_all | solution.py:131
  151.1 2.8 %fusion.20 = (bf16[8,1,128,4,128]{2,4,3,1,0:T(8,128)(2,1)S(1)}, bf16[8,1,128,4,128]{2,4,3,1,0:T(8,128)(2,1)}) fusion(bf16[8,2,128,4,128]{2,4,3,1,0:T(8,128)(2,1)} %all-to-all-done.1), kind=kLoop, calls=%fused_computation.92 | loop fusion | bytes 4194304 | tf_op jit(solution)/shard_map/slice | solution.py:141
  153.9 22.3 %all-to-all-done.2 = bf16[8,128,1024]{2,1,0:T(8,128)(2,1)S(1)} async-done(((bf16[8,128,1024]{2,1,0:T(8,128)(2,1)}), bf16[8,128,1024]{2,1,0:T(8,128)(2,1)S(1)}, u32[]{:S(2)}, u32[]{:S(2)}) %all-to-all-start.2) | async-done | bytes 2097184 | tf_op jit(solution)/shard_map/all_to_all | solution.py:131
  176.2 3.8 %fusion = f32[4,128,1024,1]{2,1,3,0:T(8,128)} fusion(bf16[8,128,1024]{2,1,0:T(8,128)(2,1)S(1)} %all-to-all-done.2, bf16[8,1,128,4,128]{2,4,3,1,0:T(8,128)(2,1)} %get-tuple-element.29), kind=kOutput, calls=%fused_computation.11 | convolution fusion | flops 1073741824 | bytes 5242880 | tf_op jit(solution)/shard_map/mqgr,mqe->gre/dot_general | solution.py:139
  180.0 4.4 %select_convert_fusion = (bf16[4,128,1024]{2,1,0:T(8,128)(2,1)}, f32[4,128,1024]{2,1,0:T(8,128)S(1)}) fusion(pred[4]{0:T(512)(128)(4,1)S(1)} %iota_compare_fusion.1, bf16[8,128,1024,1]{2,1,0,3:T(8,128)(2,1)} %bitcast.132, bf16[8,1,128,4,128]{2,4,3,1,0:T(8,128)(2,1)S(1)} %get-tuple-element.28, f32[4,128,1024,1]{2,1,3,0:T(8,128)} %fusion), kind=kOutput, calls=%fused_computation.17 | convolution fusion | flops 1074790400 | bytes 8388612 | tf_op jit(solution)/shard_map/mqgr,mqe->gre/dot_general | solution.py:141
  184.4 7.3 %convolution_convert_fusion.1 = bf16[128,4096]{1,0:T(8,128)(2,1)} fusion(bf16[128,1024]{1,0:T(8,128)(2,1)S(1)} %multiply_convert_fusion.2, bf16[4096,1024]{1,0:T(8,128)(2,1)} %param.13), kind=kOutput, calls=%fused_computation.6 | convolution fusion | flops 1074266112 | bytes 9699328 | tf_op jit(solution)/shard_map/qe,de->qd/dot_general | solution.py:124
  191.7 7.2 %convolution_convert_fusion = bf16[128,4096]{1,0:T(8,128)(2,1)} fusion(bf16[128,1024]{1,0:T(8,128)(2,1)S(1)} %copy-done.4, bf16[4096,1024]{1,0:T(8,128)(2,1)} %param.13), kind=kOutput, calls=%fused_computation.5 | convolution fusion | flops 1074266112 | bytes 9699328 | tf_op jit(solution)/shard_map/qe,de->qd/dot_general | solution.py:127
  199.0 11.2 %reduce-scatter.2.cloned.1.call-done = bf16[1,128,1024]{2,1,0:T(8,128)(2,1)} async-done(((bf16[4,128,1024]{2,1,0:T(8,128)(2,1)}), bf16[1,128,1024]{2,1,0:T(8,128)(2,1)}) %reduce-scatter.2.cloned.1.call-update) | async-done | bytes 262160 | tf_op jit(solution)/shard_map/reduce_scatter | solution.py:144
  (100 shorter events, 38.3 us)
Async XLA Ops:
  7.2 47.5 %all-gather.4.cloned.1.call-start = ((), (), s32[]{:S(2)}) async-start(), calls=%async_computation.4 | async-start | bytes 2359296 | tf_op jit(solution)/shard_map/all_gather | solution.py:67
  13.6 8.7 %copy-start.5 = (s32[1,16]{1,0:T(1,128)S(1)}, s32[1,16]{1,0:T(1,128)}, u32[]{:S(2)}) copy-start(s32[1,16]{1,0:T(1,128)} %param.14) | copy-start | bytes 196
  18.3 25.3 %copy-start.6 = (f32[128]{0:T(128)S(1)}, f32[128]{0:T(128)}, u32[]{:S(2)}) copy-start(f32[128]{0:T(128)} %param.15) | copy-start | bytes 1540
  18.4 34.3 %collective-permute-start.8 = (bf16[128,1024]{1,0:T(8,128)(2,1)S(1)}, bf16[128,1024]{1,0:T(8,128)(2,1)S(1)}, u32[]{:S(2)}, u32[]{:S(2)}) collective-permute-start(bf16[128,1024]{1,0:T(8,128)(2,1)S(1)} %multiply_convert_fusion.4), channel_id=1, source_target_pairs={{0,24},{8,0},{16,8},{24,16},{1,25},{9,1},{17,9},{25,17},{2,26},{10... | collective-permute-start | bytes 786440 | tf_op jit(solution)/shard_map/ppermute | solution.py:30
  21.8 31.0 %collective-permute-start.7 = (bf16[128,1024]{1,0:T(8,128)(2,1)S(1)}, bf16[128,1024]{1,0:T(8,128)(2,1)S(1)}, u32[]{:S(2)}, u32[]{:S(2)}) collective-permute-start(bf16[128,1024]{1,0:T(8,128)(2,1)S(1)} %multiply_convert_fusion.4), channel_id=1, source_target_pairs={{0,16},{8,24},{16,0},{24,8},{1,17},{9,25},{17,1},{25,9},{2,18},{10... | collective-permute-start | bytes 786440 | tf_op jit(solution)/shard_map/ppermute | solution.py:30
  21.8 31.0 %collective-permute-start.6 = (bf16[128,1024]{1,0:T(8,128)(2,1)S(1)}, bf16[128,1024]{1,0:T(8,128)(2,1)S(1)}, u32[]{:S(2)}, u32[]{:S(2)}) collective-permute-start(bf16[128,1024]{1,0:T(8,128)(2,1)S(1)} %multiply_convert_fusion.4), channel_id=1, source_target_pairs={{0,8},{8,16},{16,24},{24,0},{1,9},{9,17},{17,25},{25,1},{2,10},{10... | collective-permute-start | bytes 786440 | tf_op jit(solution)/shard_map/ppermute | solution.py:30
  22.3 15.9 %collective-permute-start.5 = (s32[16]{0:T(128)S(1)}, s32[16]{0:T(128)S(1)}, u32[]{:S(2)}, u32[]{:S(2)}) collective-permute-start(s32[16]{0:T(128)S(1)} %bitcast.144), channel_id=1, source_target_pairs={{0,24},{8,0},{16,8},{24,16},{1,25},{9,1},{17,9},{25,17},{2,26},{10... | collective-permute-start | bytes 200 | tf_op jit(solution)/shard_map/ppermute | solution.py:30
  25.1 18.5 %collective-permute-start.4 = (s32[16]{0:T(128)S(1)}, s32[16]{0:T(128)S(1)}, u32[]{:S(2)}, u32[]{:S(2)}) collective-permute-start(s32[16]{0:T(128)S(1)} %bitcast.145), channel_id=1, source_target_pairs={{0,16},{8,24},{16,0},{24,8},{1,17},{9,25},{17,1},{25,9},{2,18},{10... | collective-permute-start | bytes 200 | tf_op jit(solution)/shard_map/ppermute | solution.py:30
  38.2 8.8 %collective-permute-start.3 = (s32[16]{0:T(128)S(1)}, s32[16]{0:T(128)S(1)}, u32[]{:S(2)}, u32[]{:S(2)}) collective-permute-start(s32[16]{0:T(128)S(1)} %bitcast.146), channel_id=1, source_target_pairs={{0,8},{8,16},{16,24},{24,0},{1,9},{9,17},{17,25},{25,1},{2,10},{10... | collective-permute-start | bytes 200 | tf_op jit(solution)/shard_map/ppermute | solution.py:30
  43.6 4.2 %collective-permute-start.2 = (f32[128]{0:T(128)S(1)}, f32[128]{0:T(128)S(1)}, u32[]{:S(2)}, u32[]{:S(2)}) collective-permute-start(f32[128]{0:T(128)S(1)} %copy-done.6), channel_id=1, source_target_pairs={{0,24},{8,0},{16,8},{24,16},{1,25},{9,1},{17,9},{25,17},{2,26},{10... | collective-permute-start | bytes 1544 | tf_op jit(solution)/shard_map/ppermute | solution.py:30
  47.0 3.3 %collective-permute-start.1 = (f32[128]{0:T(128)S(1)}, f32[128]{0:T(128)S(1)}, u32[]{:S(2)}, u32[]{:S(2)}) collective-permute-start(f32[128]{0:T(128)S(1)} %copy-done.6), channel_id=1, source_target_pairs={{0,16},{8,24},{16,0},{24,8},{1,17},{9,25},{17,1},{25,9},{2,18},{10... | collective-permute-start | bytes 1544 | tf_op jit(solution)/shard_map/ppermute | solution.py:30
  47.8 4.4 %collective-permute-start = (f32[128]{0:T(128)S(1)}, f32[128]{0:T(128)S(1)}, u32[]{:S(2)}, u32[]{:S(2)}) collective-permute-start(f32[128]{0:T(128)S(1)} %copy-done.6), channel_id=1, source_target_pairs={{0,8},{8,16},{16,24},{24,0},{1,9},{9,17},{17,25},{25,1},{2,10},{10... | collective-permute-start | bytes 1544 | tf_op jit(solution)/shard_map/ppermute | solution.py:30
  58.5 2.5 %collective-permute-start.11 = (f32[2,4,128]{2,1,0:T(4,128)S(1)}, f32[2,4,128]{2,1,0:T(4,128)S(1)}, u32[]{:S(2)}, u32[]{:S(2)}) collective-permute-start(f32[2,4,128]{2,1,0:T(4,128)S(1)} %get-tuple-element.35), channel_id=1, source_target_pairs={{0,24},{8,0},{16,8},{24,16},{1,25},{9,1},{17,9},{25,17},{2,26},{10... | collective-permute-start | bytes 12296 | tf_op jit(solution)/shard_map/ppermute | solution.py:30
  60.0 3.4 %collective-permute-start.10 = (f32[2,4,128]{2,1,0:T(4,128)S(1)}, f32[2,4,128]{2,1,0:T(4,128)S(1)}, u32[]{:S(2)}, u32[]{:S(2)}) collective-permute-start(f32[2,4,128]{2,1,0:T(4,128)S(1)} %get-tuple-element.35), channel_id=1, source_target_pairs={{0,16},{8,24},{16,0},{24,8},{1,17},{9,25},{17,1},{25,9},{2,18},{10... | collective-permute-start | bytes 12296 | tf_op jit(solution)/shard_map/ppermute | solution.py:30
  60.0 4.3 %collective-permute-start.9 = (f32[2,4,128]{2,1,0:T(4,128)S(1)}, f32[2,4,128]{2,1,0:T(4,128)S(1)}, u32[]{:S(2)}, u32[]{:S(2)}) collective-permute-start(f32[2,4,128]{2,1,0:T(4,128)S(1)} %get-tuple-element.35), channel_id=1, source_target_pairs={{0,8},{8,16},{16,24},{24,0},{1,9},{9,17},{17,25},{25,1},{2,10},{10... | collective-permute-start | bytes 12296 | tf_op jit(solution)/shard_map/ppermute | solution.py:30
  71.3 34.2 %all-to-all-start = ((bf16[8,128,1024]{2,1,0:T(8,128)(2,1)}), bf16[8,128,1024]{2,1,0:T(8,128)(2,1)S(1)}, u32[]{:S(2)}, u32[]{:S(2)}) async-start(bf16[8,128,1024]{2,1,0:T(8,128)(2,1)} %bitcast.129), calls=%async_computation | async-start | bytes 4194304 | tf_op jit(solution)/shard_map/all_to_all | solution.py:112
  105.4 39.3 %all-to-all-start.1 = ((bf16[8,2,128,4,128]{2,4,3,1,0:T(8,128)(2,1)}), bf16[8,2,128,4,128]{2,4,3,1,0:T(8,128)(2,1)}, u32[]{:S(2)}, u32[]{:S(2)}) async-start(bf16[8,2,128,4,128]{2,4,3,1,0:T(8,128)(2,1)} %copy.23), calls=%async_computation.1 | async-start | bytes 4194304 | tf_op jit(solution)/shard_map/all_to_all | solution.py:63
  111.2 68.8 %all-gather.6.cloned.1.call-start = ((), (), s32[]{:S(2)}) async-start(), calls=%async_computation.6 | async-start | bytes 2359296 | tf_op jit(solution)/shard_map/all_gather | solution.py:138
  117.1 8.0 %collective-permute-start.14 = (bf16[128,1024]{1,0:T(8,128)(2,1)S(1)}, bf16[128,1024]{1,0:T(8,128)(2,1)S(1)}, u32[]{:S(2)}, u32[]{:S(2)}) collective-permute-start(bf16[128,1024]{1,0:T(8,128)(2,1)S(1)} %get-tuple-element.31), channel_id=1, source_target_pairs={{0,24},{8,0},{16,8},{24,16},{1,25},{9,1},{17,9},{25,17},{2,26},{10... | collective-permute-start | bytes 786440 | tf_op jit(solution)/shard_map/ppermute | solution.py:41
  117.4 23.7 %collective-permute-start.13 = (bf16[128,1024]{1,0:T(8,128)(2,1)S(1)}, bf16[128,1024]{1,0:T(8,128)(2,1)S(1)}, u32[]{:S(2)}, u32[]{:S(2)}) collective-permute-start(bf16[128,1024]{1,0:T(8,128)(2,1)S(1)} %get-tuple-element.32), channel_id=1, source_target_pairs={{0,16},{8,24},{16,0},{24,8},{1,17},{9,25},{17,1},{25,9},{2,18},{10... | collective-permute-start | bytes 786440 | tf_op jit(solution)/shard_map/ppermute | solution.py:41
  118.1 23.1 %collective-permute-start.12 = (bf16[128,1024]{1,0:T(8,128)(2,1)S(1)}, bf16[128,1024]{1,0:T(8,128)(2,1)S(1)}, u32[]{:S(2)}, u32[]{:S(2)}) collective-permute-start(bf16[128,1024]{1,0:T(8,128)(2,1)S(1)} %get-tuple-element.33), channel_id=1, source_target_pairs={{0,8},{8,16},{16,24},{24,0},{1,9},{9,17},{17,25},{25,1},{2,10},{10... | collective-permute-start | bytes 786440 | tf_op jit(solution)/shard_map/ppermute | solution.py:41
  146.3 29.8 %all-to-all-start.2 = ((bf16[8,128,1024]{2,1,0:T(8,128)(2,1)}), bf16[8,128,1024]{2,1,0:T(8,128)(2,1)S(1)}, u32[]{:S(2)}, u32[]{:S(2)}) async-start(bf16[8,128,1024]{2,1,0:T(8,128)(2,1)} %broadcast_in_dim.135), calls=%async_computation.2 | async-start | bytes 4194304 | tf_op jit(solution)/shard_map/all_to_all | solution.py:131
  151.1 59.1 %reduce-scatter.2.cloned.1.call-start = ((), (), s32[]{:S(2)}) async-start(), calls=%async_computation.5 | async-start | bytes 1310720 | tf_op jit(solution)/shard_map/reduce_scatter | solution.py:144
  184.4 7.3 %copy-start.4 = (bf16[128,1024]{1,0:T(8,128)(2,1)S(1)}, bf16[128,1024]{1,0:T(8,128)(2,1)}, u32[]{:S(2)}) copy-start(bf16[128,1024]{1,0:T(8,128)(2,1)} %multiply_convert_fusion.1) | copy-start | bytes 786436
  (4 other events, 6.6 us)
Sparse Core Ops, SparseCore 0:
  13.2 29.3 all-gather.3
  114.5 34.1 all-gather.5
  184.6 25.5 reduce-scatter.1

commit v9 on v7

--- a/solution.py
+++ b/solution.py
@@ -65,7 +65,14 @@
     q_unit, q_inv, q_emb = embed(query_feat, projection)
     c_unit, c_inv, c_emb = embed(code_feat, projection)
     group_codes = lax.all_gather(c_emb, "member", axis=0, tiled=True)
-    q_all, ids_all, w_all = shift_all((q_emb, hard_ids[0], loss_weight), "group")
+    q_all = lax.all_to_all(
+        jnp.broadcast_to(q_emb[None], (groups, queries_dev, emb_width)),
+        "group",
+        split_axis=0,
+        concat_axis=0,
+        tiled=True,
+    )
+    ids_all = shift_all(hard_ids[0], "group")
 
     block_ids = group_index * per_group + jnp.arange(per_group, dtype=jnp.int32)
     asked = jnp.any(ids_all[:, :, None] == block_ids[None, None, :], axis=1)
@@ -82,7 +89,9 @@
     part_max = jnp.max(scores, axis=2)
     safe_max = jnp.where(part_max > -jnp.inf, part_max, 0.0)
     part_sum = jnp.sum(jnp.exp(scores - safe_max[:, :, None]), axis=2)
-    stats = shift_all(jnp.stack([part_max, part_sum], axis=0), "group")
+    weights_row = jnp.broadcast_to(loss_weight[None], (groups, queries_dev))
+    stats = shift_all(jnp.stack([part_max, part_sum, weights_row], axis=0), "group")
+    w_all = stats[:, 2, 0]
     row_max = jnp.max(stats[:, 0], axis=0)
     row_sum = jnp.sum(stats[:, 1] * jnp.exp(stats[:, 0] - row_max[None]), axis=0)
     log_total = row_max + jnp.log(row_sum)

time: 209 us -> 205 us (0.981)
  starting transfers between devices: 30.8 us -> 20.2 us
  waiting for transfers between devices: 62.9 us -> 70.4 us
    all_to_all x0 -> x1, waiting for transfers between devices: none -> 23.3 us  [body(): lax.all_to_all(jnp.broadcast_to(q_emb[None], (groups, queries_dev, emb_wi...]
    ppermute x12 -> x6, waiting for transfers between devices: 19 us -> 3.3 us  [shift_all(): lax.ppermute(x, axis, [(i, (i + s) % size) for i in range(size)])]
    ppermute x12 -> x6, starting transfers between devices: 18.3 us -> 5.34 us  [shift_all(): lax.ppermute(x, axis, [(i, (i + s) % size) for i in range(size)])]
    all_to_all x0 -> x1, starting transfers between devices: none -> 4.08 us  [body(): lax.all_to_all(jnp.broadcast_to(q_emb[None], (groups, queries_dev, emb_wi...]
    ppermute x3, waiting for transfers between devices: 8.02 us -> 10.9 us  [exchange(): lax.ppermute(sent, axis, [(i, (i + s) % size) for i in range(size)])]
  transfers between devices with their start and end apart: 20 -> 15, of which waited for: 11 -> 8; matrix products, arithmetic and copies ran while one was open for 18% -> 18% of each run, Pallas kernels for 0% -> 0%
where the time goes in v9:
time: 205 us; the launch traced here: 203 us
  waiting for transfers between devices  70.4 us (34%)
  matrix products  41.2 us (20%)
  blocking collectives  34.4 us (17%)
  starting transfers between devices  20.2 us (10%)
  other arithmetic  14.3 us (7%)
  between operations  14.1 us (7%)
  local copies, waits for them, and re-layouts  8.29 us (4%)
    all_to_all x1, blocking collectives, body(): lax.all_to_all(feats, 'member', split_axis=0, concat_axis=0, tiled=True)  34.4 us
    all_to_all x1, waiting for transfers between devices, body(): lax.all_to_all(jnp.broadcast_to(q_emb[None], (groups, queries_dev, emb_wi...  23.3 us
    all_gather x1, waiting for transfers between devices, body(): lax.all_gather(jnp.stack([dz_query, dz_code], axis=0), 'member', axis=0)  13.2 us
    reduce_scatter x1, waiting for transfers between devices, body(): lax.psum_scatter(sent_proj, 'group', scatter_dimension=0, tiled=True)  12.1 us
    ppermute x3, waiting for transfers between devices, exchange(): lax.ppermute(sent, axis, [(i, (i + s) % size) for i in range(size)])  10.9 us
    dot_general x2, matrix products, embed(): values = jnp.dot(features, projection, preferred_element_type=jnp.float32)  9.77 us
    all_to_all x1, starting transfers between devices, body(): lax.all_to_all(halves[:, 1], 'member', split_axis=0, concat_axis=0, tiled...  8.65 us
    reduce_scatter x1, waiting for transfers between devices, body(): lax.psum_scatter(halves[:, 0].reshape(members * queries_dev // 2, emb_wid...  7.59 us
  transfers between devices with their start and end apart: 15, of which 8 were waited for; matrix products, arithmetic and copies ran while one was open for 18% of the time, Pallas kernels for 0%

profile of v9, /device:TPU:3, one launch (start us, length us, event | category | flops | bytes accessed | tf_op | source)
XLA Modules:
  0.0 202.9 jit_solution(5095705230341626002)
XLA Ops:
  7.2 5.1 %multiply_reduce_fusion.2 = (f32[128]{0:T(128)S(1)}, f32[128,1024]{1,0:T(8,128)S(1)}) fusion(bf16[128,4096]{1,0:T(8,128)(2,1)} %param.10, bf16[4096,1024]{1,0:T(8,128)(2,1)} %param.11), kind=kOutput, calls=%fused_computation.29 | convolution fusion | flops 1074003840 | bytes 9961984 | tf_op jit(solution)/shard_map/dot_general | solution.py:14
  13.1 3.4 %collective-permute-start.2 = (s32[16]{0:T(128)S(1)}, s32[16]{0:T(128)S(1)}, u32[]{:S(2)}, u32[]{:S(2)}) collective-permute-start(s32[16]{0:T(128)S(1)} %bitcast.131), channel_id=1, source_target_pairs={{0,24},{8,0},{16,8},{24,16},{1,25},{9,1},{17,9},{25,17},{2,26},{10... | collective-permute-start | bytes 200 | tf_op jit(solution)/shard_map/ppermute | solution.py:30
  17.0 4.7 %multiply_reduce_fusion.3 = (f32[128]{0:T(128)S(1)}, f32[128,1024]{1,0:T(8,128)S(1)}) fusion(bf16[128,4096]{1,0:T(8,128)(2,1)S(1)} %copy-done.1, bf16[4096,1024]{1,0:T(8,128)(2,1)} %param.11), kind=kOutput, calls=%fused_computation.30 | convolution fusion | flops 1074003840 | bytes 9961984 | tf_op jit(solution)/shard_map/dot_general | solution.py:14
  22.9 4.1 %all-to-all-start = ((bf16[4,128,1024]{2,1,0:T(8,128)(2,1)}), bf16[4,128,1024]{2,1,0:T(8,128)(2,1)S(1)}, u32[]{:S(2)}, u32[]{:S(2)}) async-start(bf16[4,128,1024]{2,1,0:T(8,128)(2,1)} %broadcast_in_dim.120), calls=%async_computation | async-start | bytes 2097152 | tf_op jit(solution)/shard_map/all_to_all | solution.py:68
  29.0 23.3 %all-to-all-done = bf16[4,128,1024]{2,1,0:T(8,128)(2,1)S(1)} async-done(((bf16[4,128,1024]{2,1,0:T(8,128)(2,1)}), bf16[4,128,1024]{2,1,0:T(8,128)(2,1)S(1)}, u32[]{:S(2)}, u32[]{:S(2)}) %all-to-all-start) | async-done | bytes 1048608 | tf_op jit(solution)/shard_map/all_to_all | solution.py:68
  53.2 3.3 %fusion.19 = (f32[4,128]{1,0:T(4,128)S(1)}, f32[4,128,1024]{2,1,0:T(8,128)S(1)}) fusion(bf16[4,128,1024]{2,1,0:T(8,128)(2,1)} %copy-done.5, bf16[1024,1024]{1,0:T(8,128)(2,1)} %all-gather.4.cloned.1.call-done, pred[4,1024]{1,0:T(4,128)(4,1)S(1)} %broadcast_in_dim.118), kind=kOutput, calls=%fused_computation.86 | convolution fusion | flops 1075314176 | bytes 5249024 | tf_op jit(solution)/shard_map/gqe,ke->gqk/dot_general | solution.py:85
  59.7 1.4 collective-permute-done.4
  62.7 1.6 multiply_convert_fusion
  67.7 1.5 fusion.18
  69.3 4.2 %fusion.20 = (bf16[4,128,1024]{2,1,0:T(8,128)(2,1)S(1)}, f32[4,128,1024]{2,1,0:T(8,128)}) fusion(bf16[4,128,1024]{2,1,0:T(8,128)(2,1)S(1)} %copy-done.4, bf16[1024,1024]{1,0:T(8,128)(2,1)} %all-gather.4.cloned.1.call-done), kind=kOutput, calls=%fused_computation.87 | convolution fusion | flops 1074266112 | bytes 6291456 | tf_op jit(solution)/shard_map/gqk,ke->gqe/dot_general | solution.py:110
  73.6 1.3 collective-permute-start.8
  75.6 8.6 %all-to-all-start.1 = ((bf16[8,64,1024]{2,1,0:T(8,128)(2,1)}), bf16[8,64,1024]{2,1,0:T(8,128)(2,1)S(1)}, u32[]{:S(2)}, u32[]{:S(2)}) async-start(bf16[8,64,1024]{2,1,0:T(8,128)(2,1)} %get-tuple-element.28), calls=%async_computation.2 | async-start | bytes 2097152 | tf_op jit(solution)/shard_map/all_to_all | solution.py:128
  84.3 10.9 %collective-permute-done.7 = bf16[128,1024]{1,0:T(8,128)(2,1)} collective-permute-done((bf16[128,1024]{1,0:T(8,128)(2,1)S(1)}, bf16[128,1024]{1,0:T(8,128)(2,1)}, u32[]{:S(2)}, u32[]{:S(2)}) %collective-permute-start.7) | collective-permute-done | bytes 262176 | tf_op jit(solution)/shard_map/ppermute | solution.py:41
  96.5 1.6 gather_fusion.2
  98.0 1.6 select_reduce_fusion
  99.7 1.2 multiply_reduce_fusion.1
  102.3 7.6 %reduce-scatter.3.cloned.1.call-done = bf16[64,1024]{1,0:T(8,128)(2,1)} async-done(((bf16[512,1024]{1,0:T(8,128)(2,1)}), bf16[64,1024]{1,0:T(8,128)(2,1)}) %reduce-scatter.3.cloned.1.call-update) | async-done | bytes 131088 | tf_op jit(solution)/shard_map/reduce_scatter | solution.py:121
  114.0 34.4 %all_to_all.15 = bf16[8,2,128,4,128]{2,4,1,3,0:T(8,128)(2,1)S(1)} all-to-all(bf16[8,2,128,4,128]{2,4,1,3,0:T(8,128)(2,1)S(1)} %copy.26), channel_id=1, replica_groups=mesh['group'=4,'member'=8] {'member'}, dimensions={0} | all-to-all | bytes 4194304 | tf_op jit(solution)/shard_map/all_to_all | solution.py:63
  148.4 13.2 %all-gather.6.cloned.1.call-done = bf16[16,128,1024]{2,1,0:T(8,128)(2,1)} async-done(((bf16[2,128,1024]{2,1,0:T(8,128)(2,1)}), bf16[16,128,1024]{2,1,0:T(8,128)(2,1)}) %all-gather.6.cloned.1.call-update) | async-done | bytes 4194320 | tf_op jit(solution)/shard_map/all_gather | solution.py:144
  161.5 6.2 %select_convert_fusion = (bf16[4,128,1024]{2,1,0:T(8,128)(2,1)}, f32[4,128,1024]{2,1,0:T(8,128)}) fusion(pred[4]{0:T(512)(128)(4,1)S(1)} %iota_compare_fusion.1, bf16[8,2,128,4,128]{2,4,1,3,0:T(8,128)(2,1)S(1)} %all_to_all.15, bf16[8,2,128,1024,1]{3,2,1,4,0:T(8,128)(2,1)} %bitcast.137), kind=kOutput, calls=%fused_computation.11 | convolution fusion | flops 2148007936 | bytes 9437188 | tf_op jit(solution)/shard_map/mtqgr,mtqe->gre/dot_general | solution.py:145
  167.8 7.3 %convolution_convert_fusion.1 = bf16[128,4096]{1,0:T(8,128)(2,1)} fusion(bf16[128,1024]{1,0:T(8,128)(2,1)S(1)} %multiply_convert_fusion.2, bf16[4096,1024]{1,0:T(8,128)(2,1)} %param.11), kind=kOutput, calls=%fused_computation.4 | convolution fusion | flops 1074266112 | bytes 9699328 | tf_op jit(solution)/shard_map/qe,de->qd/dot_general | solution.py:137
  175.1 7.2 %convolution_convert_fusion = bf16[128,4096]{1,0:T(8,128)(2,1)} fusion(bf16[128,1024]{1,0:T(8,128)(2,1)S(1)} %copy-done.8, bf16[4096,1024]{1,0:T(8,128)(2,1)} %param.11), kind=kOutput, calls=%fused_computation.3 | convolution fusion | flops 1074266112 | bytes 9699328 | tf_op jit(solution)/shard_map/qe,de->qd/dot_general | solution.py:140
  182.3 12.1 %reduce-scatter.5.cloned.1.call-done = bf16[1,128,1024]{2,1,0:T(8,128)(2,1)} async-done(((bf16[4,128,1024]{2,1,0:T(8,128)(2,1)}), bf16[1,128,1024]{2,1,0:T(8,128)(2,1)}) %reduce-scatter.5.cloned.1.call-update) | async-done | bytes 262160 | tf_op jit(solution)/shard_map/reduce_scatter | solution.py:150
  194.4 2.0 convert_add_fusion
  (95 shorter events, 21.0 us)
Async XLA Ops:
  7.2 6.0 %copy-start.11 = (s32[1,16]{1,0:T(1,128)S(1)}, s32[1,16]{1,0:T(1,128)}, u32[]{:S(2)}) copy-start(s32[1,16]{1,0:T(1,128)} %param.12) | copy-start | bytes 196
  7.2 46.1 %all-gather.4.cloned.1.call-start = ((), (), s32[]{:S(2)}) async-start(), calls=%async_computation.5 | async-start | bytes 2359296 | tf_op jit(solution)/shard_map/all_gather | solution.py:67
  12.3 4.7 %copy-start.1 = (bf16[128,4096]{1,0:T(8,128)(2,1)S(1)}, bf16[128,4096]{1,0:T(8,128)(2,1)}, u32[]{:S(2)}) copy-start(bf16[128,4096]{1,0:T(8,128)(2,1)} %param.9) | copy-start | bytes 3145732
  13.1 14.8 %collective-permute-start.2 = (s32[16]{0:T(128)S(1)}, s32[16]{0:T(128)S(1)}, u32[]{:S(2)}, u32[]{:S(2)}) collective-permute-start(s32[16]{0:T(128)S(1)} %bitcast.131), channel_id=1, source_target_pairs={{0,24},{8,0},{16,8},{24,16},{1,25},{9,1},{17,9},{25,17},{2,26},{10... | collective-permute-start | bytes 200 | tf_op jit(solution)/shard_map/ppermute | solution.py:30
  16.5 11.5 %collective-permute-start.1 = (s32[16]{0:T(128)S(1)}, s32[16]{0:T(128)S(1)}, u32[]{:S(2)}, u32[]{:S(2)}) collective-permute-start(s32[16]{0:T(128)S(1)} %bitcast.132), channel_id=1, source_target_pairs={{0,16},{8,24},{16,0},{24,8},{1,17},{9,25},{17,1},{25,9},{2,18},{10... | collective-permute-start | bytes 200 | tf_op jit(solution)/shard_map/ppermute | solution.py:30
  16.5 11.5 %collective-permute-start = (s32[16]{0:T(128)S(1)}, s32[16]{0:T(128)S(1)}, u32[]{:S(2)}, u32[]{:S(2)}) collective-permute-start(s32[16]{0:T(128)S(1)} %bitcast.133), channel_id=1, source_target_pairs={{0,8},{8,16},{16,24},{24,0},{1,9},{9,17},{17,25},{25,1},{2,10},{10... | collective-permute-start | bytes 200 | tf_op jit(solution)/shard_map/ppermute | solution.py:30
  22.9 29.4 %all-to-all-start = ((bf16[4,128,1024]{2,1,0:T(8,128)(2,1)}), bf16[4,128,1024]{2,1,0:T(8,128)(2,1)S(1)}, u32[]{:S(2)}, u32[]{:S(2)}) async-start(bf16[4,128,1024]{2,1,0:T(8,128)(2,1)} %broadcast_in_dim.120), calls=%async_computation | async-start | bytes 2097152 | tf_op jit(solution)/shard_map/all_to_all | solution.py:68
  27.0 82.9 %reduce-scatter.3.cloned.1.call-start = ((), (), s32[]{:S(2)}) async-start(), calls=%async_computation.6 | async-start | bytes 1179648 | tf_op jit(solution)/shard_map/reduce_scatter | solution.py:121
  57.2 2.5 %collective-permute-start.5 = (f32[3,4,128]{2,1,0:T(4,128)S(1)}, f32[3,4,128]{2,1,0:T(4,128)S(1)}, u32[]{:S(2)}, u32[]{:S(2)}) collective-permute-start(f32[3,4,128]{2,1,0:T(4,128)S(1)} %get-tuple-element.34), channel_id=1, source_target_pairs={{0,24},{8,0},{16,8},{24,16},{1,25},{9,1},{17,9},{25,17},{2,26},{10... | collective-permute-start | bytes 18440 | tf_op jit(solution)/shard_map/ppermute | solution.py:30
  57.7 3.4 %collective-permute-start.4 = (f32[3,4,128]{2,1,0:T(4,128)S(1)}, f32[3,4,128]{2,1,0:T(4,128)S(1)}, u32[]{:S(2)}, u32[]{:S(2)}) collective-permute-start(f32[3,4,128]{2,1,0:T(4,128)S(1)} %get-tuple-element.34), channel_id=1, source_target_pairs={{0,16},{8,24},{16,0},{24,8},{1,17},{9,25},{17,1},{25,9},{2,18},{10... | collective-permute-start | bytes 18440 | tf_op jit(solution)/shard_map/ppermute | solution.py:30
  57.7 4.3 %collective-permute-start.3 = (f32[3,4,128]{2,1,0:T(4,128)S(1)}, f32[3,4,128]{2,1,0:T(4,128)S(1)}, u32[]{:S(2)}, u32[]{:S(2)}) collective-permute-start(f32[3,4,128]{2,1,0:T(4,128)S(1)} %get-tuple-element.34), channel_id=1, source_target_pairs={{0,8},{8,16},{16,24},{24,0},{1,9},{9,17},{17,25},{25,1},{2,10},{10... | collective-permute-start | bytes 18440 | tf_op jit(solution)/shard_map/ppermute | solution.py:30
  62.6 1.8 copy-start.6
  64.4 2.2 %copy-start.3 = (bf16[4,128,1024]{2,1,0:T(8,128)(2,1)}, bf16[4,128,1024]{2,1,0:T(8,128)(2,1)S(1)}, u32[]{:S(2)}) copy-start(bf16[4,128,1024]{2,1,0:T(8,128)(2,1)S(1)} %multiply_convert_fusion) | copy-start | bytes 3145732
  67.7 1.6 copy-start.4
  73.6 10.7 %collective-permute-start.8 = (bf16[128,1024]{1,0:T(8,128)(2,1)S(1)}, bf16[128,1024]{1,0:T(8,128)(2,1)S(1)}, u32[]{:S(2)}, u32[]{:S(2)}) collective-permute-start(bf16[128,1024]{1,0:T(8,128)(2,1)S(1)} %get-tuple-element.30), channel_id=1, source_target_pairs={{0,24},{8,0},{16,8},{24,16},{1,25},{9,1},{17,9},{25,17},{2,26},{10... | collective-permute-start | bytes 786440 | tf_op jit(solution)/shard_map/ppermute | solution.py:41
  74.9 20.3 %collective-permute-start.7 = (bf16[128,1024]{1,0:T(8,128)(2,1)S(1)}, bf16[128,1024]{1,0:T(8,128)(2,1)}, u32[]{:S(2)}, u32[]{:S(2)}) collective-permute-start(bf16[128,1024]{1,0:T(8,128)(2,1)S(1)} %get-tuple-element.31), channel_id=1, source_target_pairs={{0,16},{8,24},{16,0},{24,8},{1,17},{9,25},{17,1},{25,9},{2,18},{10... | collective-permute-start | bytes 786440 | tf_op jit(solution)/shard_map/ppermute | solution.py:41
  74.9 20.3 %collective-permute-start.6 = (bf16[128,1024]{1,0:T(8,128)(2,1)S(1)}, bf16[128,1024]{1,0:T(8,128)(2,1)}, u32[]{:S(2)}, u32[]{:S(2)}) collective-permute-start(bf16[128,1024]{1,0:T(8,128)(2,1)S(1)} %get-tuple-element.32), channel_id=1, source_target_pairs={{0,8},{8,16},{16,24},{24,0},{1,9},{9,17},{17,25},{25,1},{2,10},{10... | collective-permute-start | bytes 786440 | tf_op jit(solution)/shard_map/ppermute | solution.py:41
  75.6 26.5 %all-to-all-start.1 = ((bf16[8,64,1024]{2,1,0:T(8,128)(2,1)}), bf16[8,64,1024]{2,1,0:T(8,128)(2,1)S(1)}, u32[]{:S(2)}, u32[]{:S(2)}) async-start(bf16[8,64,1024]{2,1,0:T(8,128)(2,1)} %get-tuple-element.28), calls=%async_computation.2 | async-start | bytes 2097152 | tf_op jit(solution)/shard_map/all_to_all | solution.py:128
  84.3 77.3 %all-gather.6.cloned.1.call-start = ((), (), s32[]{:S(2)}) async-start(), calls=%async_computation.8 | async-start | bytes 4718592 | tf_op jit(solution)/shard_map/all_gather | solution.py:144
  84.3 10.9 %copy-start.9 = (bf16[128,1024]{1,0:T(8,128)(2,1)}, bf16[128,1024]{1,0:T(8,128)(2,1)S(1)}, u32[]{:S(2)}) copy-start(bf16[128,1024]{1,0:T(8,128)(2,1)S(1)} %collective-permute-done.8) | copy-start | bytes 786436
  102.3 9.9 %copy-start = (bf16[128,4096]{1,0:T(8,128)(2,1)S(1)}, bf16[128,4096]{1,0:T(8,128)(2,1)}, u32[]{:S(2)}) copy-start(bf16[128,4096]{1,0:T(8,128)(2,1)} %param.10) | copy-start | bytes 3145732
  111.2 1.6 copy-start.2
  112.1 82.3 %reduce-scatter.5.cloned.1.call-start = ((), (), s32[]{:S(2)}) async-start(), calls=%async_computation.7 | async-start | bytes 1310720 | tf_op jit(solution)/shard_map/reduce_scatter | solution.py:150
  167.8 7.3 %copy-start.8 = (bf16[128,1024]{1,0:T(8,128)(2,1)S(1)}, bf16[128,1024]{1,0:T(8,128)(2,1)}, u32[]{:S(2)}) copy-start(bf16[128,1024]{1,0:T(8,128)(2,1)} %copy-done.7) | copy-start | bytes 786436
  (3 other events, 2.5 us)
Sparse Core Ops, SparseCore 0:
  13.2 29.3 all-gather.3
  69.4 40.5 reduce-scatter.2
  112.4 49.0 all-gather.5
  167.9 26.4 reduce-scatter.4

commit v10 on v8

--- a/solution.py
+++ b/solution.py
@@ -63,9 +63,23 @@
     feat_cols = lax.all_to_all(feats, "member", split_axis=0, concat_axis=0, tiled=True)
 
     q_unit, q_inv, q_emb = embed(query_feat, projection)
-    c_unit, c_inv, c_emb = embed(code_feat, projection)
-    group_codes = lax.all_gather(c_emb, "member", axis=0, tiled=True)
-    q_all, ids_all, w_all = shift_all((q_emb, hard_ids[0], loss_weight), "group")
+    code_values = lax.all_gather(
+        jnp.dot(code_feat, projection, preferred_element_type=jnp.float32),
+        "member",
+        axis=0,
+        tiled=True,
+    )
+    c_inv = lax.rsqrt(jnp.sum(code_values * code_values, axis=1) + epsilon)
+    c_unit = code_values * c_inv[:, None]
+    group_codes = c_unit.astype(jnp.bfloat16)
+    q_all = lax.all_to_all(
+        jnp.broadcast_to(q_emb[None], (groups, queries_dev, emb_width)),
+        "group",
+        split_axis=0,
+        concat_axis=0,
+        tiled=True,
+    )
+    ids_all = shift_all(hard_ids[0], "group")
 
     block_ids = group_index * per_group + jnp.arange(per_group, dtype=jnp.int32)
     asked = jnp.any(ids_all[:, :, None] == block_ids[None, None, :], axis=1)
@@ -82,7 +96,9 @@
     part_max = jnp.max(scores, axis=2)
     safe_max = jnp.where(part_max > -jnp.inf, part_max, 0.0)
     part_sum = jnp.sum(jnp.exp(scores - safe_max[:, :, None]), axis=2)
-    stats = shift_all(jnp.stack([part_max, part_sum], axis=0), "group")
+    weights_row = jnp.broadcast_to(loss_weight[None], (groups, queries_dev))
+    stats = shift_all(jnp.stack([part_max, part_sum, weights_row], axis=0), "group")
+    w_all = stats[:, 2, 0]
     row_max = jnp.max(stats[:, 0], axis=0)
     row_sum = jnp.sum(stats[:, 1] * jnp.exp(stats[:, 0] - row_max[None]), axis=0)
     log_total = row_max + jnp.log(row_sum)
@@ -108,19 +124,11 @@
         term = jnp.dot(grad[g].T, q_all[g], preferred_element_type=jnp.float32)
         term = jnp.where(g == group_index, term, term.astype(jnp.bfloat16).astype(jnp.float32))
         code_terms = term if code_terms is None else code_terms + term
-    code_delta = jnp.sum(
-        lax.all_to_all(
-            code_terms.astype(jnp.bfloat16).reshape(members, queries_dev, emb_width),
-            "member",
-            split_axis=0,
-            concat_axis=0,
-            tiled=True,
-        ).astype(jnp.float32),
-        axis=0,
-    )
+    code_delta = lax.psum(code_terms.astype(jnp.bfloat16), "member").astype(jnp.float32)
 
     dz_query = norm_back(query_delta, q_unit, q_inv)
-    dz_code = norm_back(code_delta, c_unit, c_inv)
+    dz_code_all = norm_back(code_delta, c_unit, c_inv)
+    dz_code = lax.dynamic_slice_in_dim(dz_code_all, member_index * queries_dev, queries_dev, 0)
     query_grad = jnp.einsum(
         "qe,de->qd", dz_query, projection, preferred_element_type=jnp.float32
     ).astype(jnp.bfloat16)
@@ -135,7 +143,7 @@
         concat_axis=0,
         tiled=True,
     )
-    dzc_all = lax.all_gather(dz_code, "member", axis=0)
+    dzc_all = dz_code_all.reshape(members, queries_dev, emb_width)
     proj_parts = jnp.einsum(
         "mqgr,mqe->gre", feat_cols[:, 0], dzq_all, preferred_element_type=jnp.float32
     ) + jnp.einsum("mqgr,mqe->gre", feat_cols[:, 1], dzc_all, preferred_element_type=jnp.float32)

time: 221 us -> 208 us (0.941)
  starting transfers between devices: 40.4 us -> 26.6 us
  other arithmetic: 13.9 us -> 19.1 us
  waiting for transfers between devices: 91.6 us -> 87.6 us
    psum x0 -> x1, waiting for transfers between devices: none -> 41.7 us  [body(): lax.psum(code_terms.astype(jnp.bfloat16), 'member').astype(jnp.float32)]
    all_to_all x1, waiting for transfers between devices: 22.3 us -> 0.01 us  [body(): lax.all_to_all(jnp.broadcast_to(dz_query[None], (members, queries_dev, em...]
    all_to_all x1, waiting for transfers between devices: 17.3 us -> 0.01 us  [body(): lax.all_to_all(jnp.broadcast_to(q_emb[None], (groups, queries_dev, emb_wi...]
    all_gather x2 -> x1, waiting for transfers between devices: 0.01 us -> 16.5 us  [body(): lax.all_gather(jnp.dot(code_feat, projection, preferred_element_type=jnp....]
    ppermute x12 -> x6, waiting for transfers between devices: 19 us -> 3.97 us  [shift_all(): lax.ppermute(x, axis, [(i, (i + s) % size) for i in range(size)])]
    ppermute x12 -> x6, starting transfers between devices: 18.3 us -> 8.38 us  [shift_all(): lax.ppermute(x, axis, [(i, (i + s) % size) for i in range(size)])]
    ppermute x3, waiting for transfers between devices: 21.7 us -> 12 us  [exchange(): lax.ppermute(sent, axis, [(i, (i + s) % size) for i in range(size)])]
    dot_general x0 -> x1, matrix products: none -> 5.85 us  [body(): jnp.dot(code_feat, projection, preferred_element_type=jnp.float32)]
  transfers between devices with their start and end apart: 21 -> 15, of which waited for: 11 -> 7; matrix products, arithmetic and copies ran while one was open for 22% -> 30% of each run, Pallas kernels for 0% -> 0%
where the time goes in v10:
time: 208 us; the launch traced here: 205 us
  waiting for transfers between devices  87.6 us (42%)
  matrix products  42.9 us (21%)
  starting transfers between devices  26.6 us (13%)
  other arithmetic  19.1 us (9%)
  local copies, waits for them, and re-layouts  15 us (7%)
  between operations  14 us (7%)
    psum x1, waiting for transfers between devices, body(): lax.psum(code_terms.astype(jnp.bfloat16), 'member').astype(jnp.float32)  41.7 us
    all_gather x1, waiting for transfers between devices, body(): lax.all_gather(jnp.dot(code_feat, projection, preferred_element_type=jnp....  16.5 us
    reduce_scatter x1, waiting for transfers between devices, body(): lax.psum_scatter(sent_proj, 'group', scatter_dimension=0, tiled=True)  13.4 us
    ppermute x3, waiting for transfers between devices, exchange(): lax.ppermute(sent, axis, [(i, (i + s) % size) for i in range(size)])  12 us
    ppermute x6, starting transfers between devices, shift_all(): lax.ppermute(x, axis, [(i, (i + s) % size) for i in range(size)])  8.38 us
    dot_general x1, matrix products, body(): jnp.einsum('qe,de->qd', dz_code, projection, preferred_element_type=jnp.f...  7.3 us
    dot_general x1, matrix products, body(): jnp.einsum('qe,de->qd', dz_query, projection, preferred_element_type=jnp....  7.24 us
    all_to_all x1, starting transfers between devices, body(): lax.all_to_all(jnp.broadcast_to(dz_query[None], (members, queries_dev, em...  6.61 us
  transfers between devices with their start and end apart: 15, of which 7 were waited for; matrix products, arithmetic and copies ran while one was open for 30% of the time, Pallas kernels for 0%

profile of v10, /device:TPU:3, one launch (start us, length us, event | category | flops | bytes accessed | tf_op | source)
XLA Modules:
  0.0 205.2 jit_solution(14061619593128823379)
XLA Ops:
  7.2 5.8 %fusion.26 = f32[128,1024]{1,0:T(8,128)} fusion(bf16[128,4096]{1,0:T(8,128)(2,1)} %param.10, bf16[4096,1024]{1,0:T(8,128)(2,1)} %param.11), kind=kOutput, calls=%fused_computation.91 | convolution fusion | flops 1073741824 | bytes 9961472 | tf_op jit(solution)/shard_map/dot_general | solution.py:67
  14.5 2.3 %collective-permute-start.1 = (s32[16]{0:T(128)S(1)}, s32[16]{0:T(128)S(1)}, u32[]{:S(2)}, u32[]{:S(2)}) collective-permute-start(s32[16]{0:T(128)S(1)} %bitcast.126), channel_id=1, source_target_pairs={{0,16},{8,24},{16,0},{24,8},{1,17},{9,25},{17,1},{25,9},{2,18},{10... | collective-permute-start | bytes 200 | tf_op jit(solution)/shard_map/ppermute | solution.py:30
  17.8 4.7 %multiply_reduce_fusion.2 = (f32[128]{0:T(128)S(1)}, f32[128,1024]{1,0:T(8,128)S(1)}) fusion(bf16[128,4096]{1,0:T(8,128)(2,1)S(1)} %copy-done.4, bf16[4096,1024]{1,0:T(8,128)(2,1)} %param.11), kind=kOutput, calls=%fused_computation.31 | convolution fusion | flops 1074003840 | bytes 9961984 | tf_op jit(solution)/shard_map/dot_general | solution.py:14
  23.8 3.6 %all-to-all-start = ((bf16[4,128,1024]{2,1,0:T(8,128)(2,1)}), bf16[4,128,1024]{2,1,0:T(8,128)(2,1)S(1)}, u32[]{:S(2)}, u32[]{:S(2)}) async-start(bf16[4,128,1024]{2,1,0:T(8,128)(2,1)} %broadcast_in_dim.126), calls=%async_computation | async-start | bytes 2097152 | tf_op jit(solution)/shard_map/all_to_all | solution.py:75
  35.0 16.5 %all-gather.2.cloned.1.call-done = f32[1024,1024]{1,0:T(8,128)} async-done(((f32[128,1024]{1,0:T(8,128)}), f32[1024,1024]{1,0:T(8,128)}) %all-gather.2.cloned.1.call-update) | async-done | bytes 4194320 | tf_op jit(solution)/shard_map/all_gather | solution.py:66
  51.5 2.5 %multiply_reduce_fusion = f32[1024]{0:T(1024)S(1)} fusion(f32[1024,1024]{1,0:T(8,128)} %all-gather.2.cloned.1.call-done), kind=kLoop, calls=%fused_computation.11 | loop fusion | flops 2096128 | bytes 4198400 | tf_op jit(solution)/shard_map/reduce_sum | solution.py:72
  54.0 4.7 %all-to-all-start.1 = ((bf16[8,2,128,4,128]{2,4,3,1,0:T(8,128)(2,1)}), bf16[8,2,128,4,128]{2,4,3,1,0:T(8,128)(2,1)}, u32[]{:S(2)}, u32[]{:S(2)}) async-start(bf16[8,2,128,4,128]{2,4,3,1,0:T(8,128)(2,1)} %copy.25), calls=%async_computation.1 | async-start | bytes 4194304 | tf_op jit(solution)/shard_map/all_to_all | solution.py:63
  58.7 3.6 %fusion.24 = (f32[4,128]{1,0:T(4,128)S(1)}, f32[4,128,1024]{2,1,0:T(8,128)S(1)}) fusion(bf16[4,128,1024]{2,1,0:T(8,128)(2,1)S(1)} %all-to-all-done, f32[1024,1024]{1,0:T(8,128)} %all-gather.2.cloned.1.call-done, f32[1024]{0:T(1024)S(1)} %add_rsqrt_fusion, pred[4,1024]{1,0:T(4,128)(4,1)S(1)} %broadcast_in_dim.124), kind=kOutput, calls=%fused_computation.89 | convolution fusion | flops 1077411328 | bytes 7350272 | tf_op jit(solution)/shard_map/gqe,ke->gqk/dot_general | solution.py:92
  68.1 2.6 %collective-permute-done.3 = f32[3,4,128]{2,1,0:T(4,128)S(1)} collective-permute-done((f32[3,4,128]{2,1,0:T(4,128)S(1)}, f32[3,4,128]{2,1,0:T(4,128)S(1)}, u32[]{:S(2)}, u32[]{:S(2)}) %collective-permute-start.3) | collective-permute-done | bytes 6176 | tf_op jit(solution)/shard_map/ppermute | solution.py:30
  72.9 3.5 %fusion.25 = (bf16[4,128,1024]{2,1,0:T(8,128)(2,1)S(1)}, f32[4,128,1024]{2,1,0:T(8,128)S(1)}) fusion(bf16[4,128,1024]{2,1,0:T(8,128)(2,1)S(1)} %multiply_convert_fusion.1, f32[1024,1024]{1,0:T(8,128)} %all-gather.2.cloned.1.call-done, f32[1024]{0:T(1024)S(1)} %add_rsqrt_fusion), kind=kOutput, calls=%fused_computation.90 | convolution fusion | flops 1076363264 | bytes 8392704 | tf_op jit(solution)/shard_map/gqk,ke->gqe/dot_general | solution.py:117
  77.7 3.0 %collective-permute-start.8 = (bf16[128,1024]{1,0:T(8,128)(2,1)}, bf16[128,1024]{1,0:T(8,128)(2,1)}, u32[]{:S(2)}, u32[]{:S(2)}) collective-permute-start(bf16[128,1024]{1,0:T(8,128)(2,1)} %get-tuple-element.30), channel_id=1, source_target_pairs={{0,24},{8,0},{16,8},{24,16},{1,25},{9,1},{17,9},{25,17},{2,26},{10... | collective-permute-start | bytes 786440 | tf_op jit(solution)/shard_map/ppermute | solution.py:41
  82.9 2.4 %add_convert_fusion = bf16[1024,1024]{1,0:T(8,128)(2,1)} fusion(f32[1024,1024]{1,0:T(8,128)S(1)} %fusion.10, f32[1024,1024]{1,0:T(8,128)S(1)} %fusion.11, f32[1024,1024]{1,0:T(8,128)S(1)} %fusion.12, pred[]{:T(512)S(6)} %eq.75, pred[]{:T(512)S(6)} %eq.74, pred[]{:T(512)S(6)} %eq.73, pred[]{:T(512)S(6)} %eq.72, bf16[4,128,1024]{2,1,0:T(8,128)(2,1)S(1)} %all-to-all-done, ...), kind=kOutput, calls=%fused_computation.10 | convolution fusion | flops 285212672 | bytes 15204356 | tf_op jit(solution)/shard_map/dot_general | solution.py:124
  85.4 11.8 %collective-permute-done.7 = bf16[128,1024]{1,0:T(8,128)(2,1)} collective-permute-done((bf16[128,1024]{1,0:T(8,128)(2,1)}, bf16[128,1024]{1,0:T(8,128)(2,1)}, u32[]{:S(2)}, u32[]{:S(2)}) %collective-permute-start.7) | collective-permute-done | bytes 262176 | tf_op jit(solution)/shard_map/ppermute | solution.py:41
  97.2 2.2 %pad_maximum_fusion = bf16[4,128,1024]{2,1,0:T(8,128)(2,1)} fusion(bf16[1,128,1024]{2,1,0:T(8,128)(2,1)} %bitcast.22, bf16[1,128,1024]{2,1,0:T(8,128)(2,1)} %bitcast.20, bf16[1,128,1024]{2,1,0:T(8,128)(2,1)} %bitcast.18, bf16[1,128,1024]{2,1,0:T(8,128)(2,1)S(1)} %get-tuple-element.29), kind=kLoop, calls=%fused_computation.23 | loop fusion | flops 1572864 | bytes 2097152 | tf_op jit(solution)/shard_map/stack | solution.py:42
  99.5 2.9 %gather_fusion.2 = bf16[4,128,1024]{2,1,0:T(8,128)(2,1)} fusion(bf16[4,128,1024]{2,1,0:T(8,128)(2,1)} %pad_maximum_fusion, s32[1024]{0:T(1024)S(1)} %pad_clamp_fusion), kind=kCustom, calls=%fused_computation.2 | custom fusion | bytes 2097168 | tf_op jit(solution)/shard_map/jit(_take)/gather | solution.py:43
  106.0 6.6 %all-to-all-start.2 = ((bf16[8,128,1024]{2,1,0:T(8,128)(2,1)}), bf16[8,128,1024]{2,1,0:T(8,128)(2,1)}, u32[]{:S(2)}, u32[]{:S(2)}) async-start(bf16[8,128,1024]{2,1,0:T(8,128)(2,1)} %broadcast_in_dim.134), calls=%async_computation.2 | async-start | bytes 4194304 | tf_op jit(solution)/shard_map/all_to_all | solution.py:139
  112.6 2.8 %fusion.23 = (bf16[8,1,128,4,128]{2,4,3,1,0:T(8,128)(2,1)S(1)}, bf16[8,1,128,4,128]{2,4,3,1,0:T(8,128)(2,1)}) fusion(bf16[8,2,128,4,128]{2,4,3,1,0:T(8,128)(2,1)} %all-to-all-done.1), kind=kLoop, calls=%fused_computation.88 | loop fusion | bytes 4194304 | tf_op jit(solution)/shard_map/slice | solution.py:149
  115.4 41.7 %all-reduce.2.cloned.1.call-done = bf16[1024,1024]{1,0:T(8,128)(2,1)} async-done(((bf16[1024,1024]{1,0:T(8,128)(2,1)}), bf16[1024,1024]{1,0:T(8,128)(2,1)}) %all-reduce.2.cloned.1.call-update) | async-done | bytes 2097168 | tf_op jit(solution)/shard_map/psum | solution.py:127
  157.1 3.7 %fusion = f32[1024]{0:T(1024)S(1)} fusion(bf16[1024,1024]{1,0:T(8,128)(2,1)} %all-reduce.2.cloned.1.call-done, f32[1024,1024]{1,0:T(8,128)} %all-gather.2.cloned.1.call-done, f32[1024]{0:T(1024)S(1)} %add_rsqrt_fusion), kind=kLoop, calls=%fused_computation.7 | loop fusion | flops 4193280 | bytes 6299648 | tf_op jit(solution)/shard_map/reduce_sum | solution.py:21
  162.6 3.2 %fusion.4 = f32[4,128,1024,1]{2,1,3,0:T(8,128)S(1)} fusion(bf16[8,128,1024]{2,1,0:T(8,128)(2,1)} %all-to-all-done.2, bf16[8,1,128,4,128]{2,4,3,1,0:T(8,128)(2,1)} %get-tuple-element.28), kind=kOutput, calls=%fused_computation.16 | convolution fusion | flops 1073741824 | bytes 5242880 | tf_op jit(solution)/shard_map/mqgr,mqe->gre/dot_general | solution.py:147
  165.8 2.9 %select_convert_fusion = (bf16[4,128,1024]{2,1,0:T(8,128)(2,1)}, f32[4,128,1024]{2,1,0:T(8,128)}) fusion(pred[4]{0:T(512)(128)(4,1)S(1)} %iota_compare_fusion.1, bf16[8,128,1024,1]{2,1,0,3:T(8,128)(2,1)S(1)} %bitcast.116, bf16[8,1,128,4,128]{2,4,3,1,0:T(8,128)(2,1)S(1)} %get-tuple-element.27, f32[4,128,1024,1]{2,1,3,0:T(8,128)S(1)} %fusion.4), kind=kOutput, calls=%fused_computation.18 | convolution fusion | flops 1074790400 | bytes 8388612 | tf_op jit(solution)/shard_map/mqgr,mqe->gre/dot_general | solution.py:149
  168.7 7.2 %convolution_convert_fusion.1 = bf16[128,4096]{1,0:T(8,128)(2,1)} fusion(bf16[128,1024]{1,0:T(8,128)(2,1)S(1)} %multiply_convert_fusion.2, bf16[4096,1024]{1,0:T(8,128)(2,1)} %param.11), kind=kOutput, calls=%fused_computation.6 | convolution fusion | flops 1074266112 | bytes 9699328 | tf_op jit(solution)/shard_map/qe,de->qd/dot_general | solution.py:132
  176.0 7.3 %convolution_convert_fusion = bf16[128,4096]{1,0:T(8,128)(2,1)} fusion(bf16[4096,1024]{1,0:T(8,128)(2,1)} %param.11, bf16[1024,1024]{1,0:T(8,128)(2,1)S(1)} %fusion.2, s32[]{:T(128)S(6)} %select_n.153), kind=kOutput, calls=%fused_computation.5 | convolution fusion | flops 1074266112 | bytes 9699332 | tf_op jit(solution)/shard_map/qe,de->qd/dot_general | solution.py:135
  183.3 13.4 %reduce-scatter.2.cloned.1.call-done = bf16[1,128,1024]{2,1,0:T(8,128)(2,1)} async-done(((bf16[4,128,1024]{2,1,0:T(8,128)(2,1)}), bf16[1,128,1024]{2,1,0:T(8,128)(2,1)}) %reduce-scatter.2.cloned.1.call-update) | async-done | bytes 262160 | tf_op jit(solution)/shard_map/reduce_scatter | solution.py:152
  (86 shorter events, 30.2 us)
Async XLA Ops:
  7.2 5.9 %copy-start.8 = (s32[1,16]{1,0:T(1,128)S(1)}, s32[1,16]{1,0:T(1,128)}, u32[]{:S(2)}) copy-start(s32[1,16]{1,0:T(1,128)} %param.12) | copy-start | bytes 196
  7.2 10.7 %copy-start.4 = (bf16[128,4096]{1,0:T(8,128)(2,1)S(1)}, bf16[128,4096]{1,0:T(8,128)(2,1)}, u32[]{:S(2)}) copy-start(bf16[128,4096]{1,0:T(8,128)(2,1)} %param.9) | copy-start | bytes 3145732
  7.2 44.3 %all-gather.2.cloned.1.call-start = ((), (), s32[]{:S(2)}) async-start(), calls=%async_computation.4 | async-start | bytes 4718592 | tf_op jit(solution)/shard_map/all_gather | solution.py:66
  13.1 20.9 %collective-permute-start = (s32[16]{0:T(128)S(1)}, s32[16]{0:T(128)S(1)}, u32[]{:S(2)}, u32[]{:S(2)}) collective-permute-start(s32[16]{0:T(128)S(1)} %bitcast.125), channel_id=1, source_target_pairs={{0,8},{8,16},{16,24},{24,0},{1,9},{9,17},{17,25},{25,1},{2,10},{10... | collective-permute-start | bytes 200 | tf_op jit(solution)/shard_map/ppermute | solution.py:30
  14.5 19.5 %collective-permute-start.1 = (s32[16]{0:T(128)S(1)}, s32[16]{0:T(128)S(1)}, u32[]{:S(2)}, u32[]{:S(2)}) collective-permute-start(s32[16]{0:T(128)S(1)} %bitcast.126), channel_id=1, source_target_pairs={{0,16},{8,24},{16,0},{24,8},{1,17},{9,25},{17,1},{25,9},{2,18},{10... | collective-permute-start | bytes 200 | tf_op jit(solution)/shard_map/ppermute | solution.py:30
  16.8 17.2 %collective-permute-start.2 = (s32[16]{0:T(128)S(1)}, s32[16]{0:T(128)S(1)}, u32[]{:S(2)}, u32[]{:S(2)}) collective-permute-start(s32[16]{0:T(128)S(1)} %bitcast.127), channel_id=1, source_target_pairs={{0,24},{8,0},{16,8},{24,16},{1,25},{9,1},{17,9},{25,17},{2,26},{10... | collective-permute-start | bytes 200 | tf_op jit(solution)/shard_map/ppermute | solution.py:30
  22.6 1.2 copy-start.2
  23.8 5.1 %copy-start.5 = (bf16[128,4096]{1,0:T(8,128)(2,1)S(1)}, bf16[128,4096]{1,0:T(8,128)(2,1)}, u32[]{:S(2)}) copy-start(bf16[128,4096]{1,0:T(8,128)(2,1)} %param.10) | copy-start | bytes 3145732
  23.8 30.2 %all-to-all-start = ((bf16[4,128,1024]{2,1,0:T(8,128)(2,1)}), bf16[4,128,1024]{2,1,0:T(8,128)(2,1)S(1)}, u32[]{:S(2)}, u32[]{:S(2)}) async-start(bf16[4,128,1024]{2,1,0:T(8,128)(2,1)} %broadcast_in_dim.126), calls=%async_computation | async-start | bytes 2097152 | tf_op jit(solution)/shard_map/all_to_all | solution.py:75
  28.9 1.3 copy-start.6
  54.0 50.4 %all-to-all-start.1 = ((bf16[8,2,128,4,128]{2,4,3,1,0:T(8,128)(2,1)}), bf16[8,2,128,4,128]{2,4,3,1,0:T(8,128)(2,1)}, u32[]{:S(2)}, u32[]{:S(2)}) async-start(bf16[8,2,128,4,128]{2,4,3,1,0:T(8,128)(2,1)} %copy.25), calls=%async_computation.1 | async-start | bytes 4194304 | tf_op jit(solution)/shard_map/all_to_all | solution.py:63
  58.7 98.4 %all-reduce.2.cloned.1.call-start = ((), (), s32[]{:S(2)}) async-start(), calls=%async_computation.5 | async-start | bytes 4194304 | tf_op jit(solution)/shard_map/psum | solution.py:127
  62.3 0.7 copy-start.7
  63.0 3.7 %collective-permute-start.4 = (f32[3,4,128]{2,1,0:T(4,128)S(1)}, f32[3,4,128]{2,1,0:T(4,128)S(1)}, u32[]{:S(2)}, u32[]{:S(2)}) collective-permute-start(f32[3,4,128]{2,1,0:T(4,128)S(1)} %get-tuple-element.34), channel_id=1, source_target_pairs={{0,16},{8,24},{16,0},{24,8},{1,17},{9,25},{17,1},{25,9},{2,18},{10... | collective-permute-start | bytes 18440 | tf_op jit(solution)/shard_map/ppermute | solution.py:30
  65.2 2.9 %collective-permute-start.5 = (f32[3,4,128]{2,1,0:T(4,128)S(1)}, f32[3,4,128]{2,1,0:T(4,128)S(1)}, u32[]{:S(2)}, u32[]{:S(2)}) collective-permute-start(f32[3,4,128]{2,1,0:T(4,128)S(1)} %get-tuple-element.34), channel_id=1, source_target_pairs={{0,24},{8,0},{16,8},{24,16},{1,25},{9,1},{17,9},{25,17},{2,26},{10... | collective-permute-start | bytes 18440 | tf_op jit(solution)/shard_map/ppermute | solution.py:30
  66.4 4.3 %collective-permute-start.3 = (f32[3,4,128]{2,1,0:T(4,128)S(1)}, f32[3,4,128]{2,1,0:T(4,128)S(1)}, u32[]{:S(2)}, u32[]{:S(2)}) collective-permute-start(f32[3,4,128]{2,1,0:T(4,128)S(1)} %get-tuple-element.34), channel_id=1, source_target_pairs={{0,8},{8,16},{16,24},{24,0},{1,9},{9,17},{17,25},{25,1},{2,10},{10... | collective-permute-start | bytes 18440 | tf_op jit(solution)/shard_map/ppermute | solution.py:30
  77.4 8.0 %collective-permute-start.6 = (bf16[128,1024]{1,0:T(8,128)(2,1)}, bf16[128,1024]{1,0:T(8,128)(2,1)}, u32[]{:S(2)}, u32[]{:S(2)}) collective-permute-start(bf16[128,1024]{1,0:T(8,128)(2,1)} %get-tuple-element.32), channel_id=1, source_target_pairs={{0,8},{8,16},{16,24},{24,0},{1,9},{9,17},{17,25},{25,1},{2,10},{10... | collective-permute-start | bytes 786440 | tf_op jit(solution)/shard_map/ppermute | solution.py:41
  77.4 19.8 %collective-permute-start.7 = (bf16[128,1024]{1,0:T(8,128)(2,1)}, bf16[128,1024]{1,0:T(8,128)(2,1)}, u32[]{:S(2)}, u32[]{:S(2)}) collective-permute-start(bf16[128,1024]{1,0:T(8,128)(2,1)} %get-tuple-element.31), channel_id=1, source_target_pairs={{0,16},{8,24},{16,0},{24,8},{1,17},{9,25},{17,1},{25,9},{2,18},{10... | collective-permute-start | bytes 786440 | tf_op jit(solution)/shard_map/ppermute | solution.py:41
  77.7 19.5 %collective-permute-start.8 = (bf16[128,1024]{1,0:T(8,128)(2,1)}, bf16[128,1024]{1,0:T(8,128)(2,1)}, u32[]{:S(2)}, u32[]{:S(2)}) collective-permute-start(bf16[128,1024]{1,0:T(8,128)(2,1)} %get-tuple-element.30), channel_id=1, source_target_pairs={{0,24},{8,0},{16,8},{24,16},{1,25},{9,1},{17,9},{25,17},{2,26},{10... | collective-permute-start | bytes 786440 | tf_op jit(solution)/shard_map/ppermute | solution.py:41
  99.5 4.6 %copy-start.3 = (f32[128,1024]{1,0:T(8,128)S(1)}, f32[128,1024]{1,0:T(8,128)}, u32[]{:S(2)}) copy-start(f32[128,1024]{1,0:T(8,128)} %copy-done.2) | copy-start | bytes 1572868
  106.0 56.6 %all-to-all-start.2 = ((bf16[8,128,1024]{2,1,0:T(8,128)(2,1)}), bf16[8,128,1024]{2,1,0:T(8,128)(2,1)}, u32[]{:S(2)}, u32[]{:S(2)}) async-start(bf16[8,128,1024]{2,1,0:T(8,128)(2,1)} %broadcast_in_dim.134), calls=%async_computation.2 | async-start | bytes 4194304 | tf_op jit(solution)/shard_map/all_to_all | solution.py:139
  112.6 84.1 %reduce-scatter.2.cloned.1.call-start = ((), (), s32[]{:S(2)}) async-start(), calls=%async_computation.6 | async-start | bytes 1310720 | tf_op jit(solution)/shard_map/reduce_scatter | solution.py:152
  157.1 4.0 %copy-start = (f32[1024,1024]{1,0:T(8,128)S(1)}, f32[1024,1024]{1,0:T(8,128)}, u32[]{:S(2)}) copy-start(f32[1024,1024]{1,0:T(8,128)} %all-gather.2.cloned.1.call-done) | copy-start | bytes 12582916
  157.1 4.7 %copy-start.1 = (bf16[1024,1024]{1,0:T(8,128)(2,1)S(1)}, bf16[1024,1024]{1,0:T(8,128)(2,1)}, u32[]{:S(2)}) copy-start(bf16[1024,1024]{1,0:T(8,128)(2,1)} %all-reduce.2.cloned.1.call-done) | copy-start | bytes 6291460
Sparse Core Ops, SparseCore 0:
  13.2 38.2 all-gather.1
  85.4 71.6 all-reduce.1
  168.9 27.8 reduce-scatter.1

commit v11 on v10

--- a/solution.py
+++ b/solution.py
@@ -60,7 +60,6 @@
         2, queries_dev, groups, members, rows_dev
     )
     feats = jnp.transpose(feats, (3, 0, 1, 2, 4))
-    feat_cols = lax.all_to_all(feats, "member", split_axis=0, concat_axis=0, tiled=True)
 
     q_unit, q_inv, q_emb = embed(query_feat, projection)
     code_values = lax.all_gather(
@@ -116,6 +115,8 @@
 
     delta_parts = jnp.einsum("gqk,ke->gqe", grad, group_codes, preferred_element_type=jnp.float32)
     returned = exchange(delta_parts.astype(jnp.bfloat16), "group").astype(jnp.float32)
+    feats, returned = lax.optimization_barrier((feats, returned))
+    feat_cols = lax.all_to_all(feats, "member", split_axis=0, concat_axis=0, tiled=True)
     own_part = jnp.take(delta_parts, group_index, axis=0)
     query_delta = own_part + jnp.sum(jnp.where(own[:, None, None], 0.0, returned), axis=0)
 

time: 208 us -> 247 us (1.19)
  waiting for transfers between devices: 87.6 us -> 117 us
  starting transfers between devices: 26.6 us -> 30.9 us
  matrix products: 42.9 us -> 46.7 us
  local copies, waits for them, and re-layouts: 15 us -> 17.8 us
    all_to_all x1, waiting for transfers between devices: 0.01 us -> 21.7 us  [body(): lax.all_to_all(feats, 'member', split_axis=0, concat_axis=0, tiled=True)]
    psum x1, waiting for transfers between devices: 41.7 us -> 47.6 us  [body(): lax.psum(code_terms.astype(jnp.bfloat16), 'member').astype(jnp.float32)]
    unnamed x20 -> x32, local copies, waits for them, and re-layouts: 3.84 us -> 8.96 us
  transfers between devices with their start and end apart: 15 -> 15, of which waited for: 7 -> 8; matrix products, arithmetic and copies ran while one was open for 30% -> 19% of each run, Pallas kernels for 0% -> 0%
where the time goes in v11:
time: 247 us; the launch traced here: 244 us
  waiting for transfers between devices  117 us (47%)
  matrix products  46.7 us (19%)
  starting transfers between devices  30.9 us (13%)
  local copies, waits for them, and re-layouts  17.8 us (7%)
  other arithmetic  17.7 us (7%)
  between operations  14 us (6%)
    psum x1, waiting for transfers between devices, body(): lax.psum(code_terms.astype(jnp.bfloat16), 'member').astype(jnp.float32)  47.6 us
    all_to_all x1, waiting for transfers between devices, body(): lax.all_to_all(feats, 'member', split_axis=0, concat_axis=0, tiled=True)  21.7 us
    all_gather x1, waiting for transfers between devices, body(): lax.all_gather(jnp.dot(code_feat, projection, preferred_element_type=jnp....  16.6 us
    ppermute x3, waiting for transfers between devices, exchange(): lax.ppermute(sent, axis, [(i, (i + s) % size) for i in range(size)])  13.7 us
    reduce_scatter x1, waiting for transfers between devices, body(): lax.psum_scatter(sent_proj, 'group', scatter_dimension=0, tiled=True)  13.4 us
    unnamed x32, local copies, waits for them, and re-layouts  8.96 us
    all_to_all x1, starting transfers between devices, body(): lax.all_to_all(jnp.broadcast_to(dz_query[None], (members, queries_dev, em...  8.7 us
    ppermute x6, starting transfers between devices, shift_all(): lax.ppermute(x, axis, [(i, (i + s) % size) for i in range(size)])  8.38 us
  transfers between devices with their start and end apart: 15, of which 8 were waited for; matrix products, arithmetic and copies ran while one was open for 19% of the time, Pallas kernels for 0%

profile of v11, /device:TPU:3, one launch (start us, length us, event | category | flops | bytes accessed | tf_op | source)
XLA Modules:
  0.0 244.1 jit_solution(3258198172399512789)
XLA Ops:
  7.2 5.9 %fusion.26 = f32[128,1024]{1,0:T(8,128)} fusion(bf16[128,4096]{1,0:T(8,128)(2,1)} %param.10, bf16[4096,1024]{1,0:T(8,128)(2,1)} %param.11), kind=kOutput, calls=%fused_computation.92 | convolution fusion | flops 1073741824 | bytes 9961472 | tf_op jit(solution)/shard_map/dot_general | solution.py:66
  17.9 4.7 %multiply_reduce_fusion.2 = (f32[128]{0:T(128)S(1)}, f32[128,1024]{1,0:T(8,128)S(1)}) fusion(bf16[128,4096]{1,0:T(8,128)(2,1)S(1)} %copy-done.9, bf16[4096,1024]{1,0:T(8,128)(2,1)} %param.11), kind=kOutput, calls=%fused_computation.32 | convolution fusion | flops 1074003840 | bytes 9961984 | tf_op jit(solution)/shard_map/dot_general | solution.py:14
  23.8 3.6 %all-to-all-start = ((bf16[4,128,1024]{2,1,0:T(8,128)(2,1)}), bf16[4,128,1024]{2,1,0:T(8,128)(2,1)S(1)}, u32[]{:S(2)}, u32[]{:S(2)}) async-start(bf16[4,128,1024]{2,1,0:T(8,128)(2,1)} %broadcast_in_dim.126), calls=%async_computation | async-start | bytes 2097152 | tf_op jit(solution)/shard_map/all_to_all | solution.py:74
  30.2 2.8 %maximum_bitcast_fusion = bf16[8,2,128,4,128]{2,4,0,3,1:T(8,128)(2,1)} fusion(bf16[1,128,4,8,128]{1,4,3,2,0:T(8,128)(2,1)} %bitcast.118, bf16[1,128,4,8,128]{1,4,3,2,0:T(8,128)(2,1)S(1)} %bitcast.117), kind=kLoop, calls=%fused_computation.14 | loop fusion | flops 1048576 | bytes 4194304 | tf_op jit(solution)/shard_map/transpose | solution.py:62
  34.9 16.6 %all-gather.2.cloned.1.call-done = f32[1024,1024]{1,0:T(8,128)} async-done(((f32[128,1024]{1,0:T(8,128)}), f32[1024,1024]{1,0:T(8,128)}) %all-gather.2.cloned.1.call-update) | async-done | bytes 4194320 | tf_op jit(solution)/shard_map/all_gather | solution.py:65
  51.5 2.5 %multiply_reduce_fusion = f32[1024]{0:T(1024)S(1)} fusion(f32[1024,1024]{1,0:T(8,128)} %all-gather.2.cloned.1.call-done), kind=kLoop, calls=%fused_computation.11 | loop fusion | flops 2096128 | bytes 4198400 | tf_op jit(solution)/shard_map/reduce_sum | solution.py:71
  54.1 3.6 %fusion.24 = (f32[4,128]{1,0:T(4,128)S(1)}, f32[4,128,1024]{2,1,0:T(8,128)S(1)}) fusion(bf16[4,128,1024]{2,1,0:T(8,128)(2,1)S(1)} %all-to-all-done, f32[1024,1024]{1,0:T(8,128)} %all-gather.2.cloned.1.call-done, f32[1024]{0:T(1024)S(1)} %add_rsqrt_fusion, pred[4,1024]{1,0:T(4,128)(4,1)S(1)} %broadcast_in_dim.124), kind=kOutput, calls=%fused_computation.90 | convolution fusion | flops 1077411328 | bytes 7350272 | tf_op jit(solution)/shard_map/gqe,ke->gqk/dot_general | solution.py:91
  63.0 3.0 %collective-permute-done.3 = f32[3,4,128]{2,1,0:T(4,128)S(1)} collective-permute-done((f32[3,4,128]{2,1,0:T(4,128)S(1)}, f32[3,4,128]{2,1,0:T(4,128)S(1)}, u32[]{:S(2)}, u32[]{:S(2)}) %collective-permute-start.3) | collective-permute-done | bytes 6176 | tf_op jit(solution)/shard_map/ppermute | solution.py:30
  68.3 5.2 %fusion.25 = (bf16[4,128,1024]{2,1,0:T(8,128)(2,1)S(1)}, f32[4,128,1024]{2,1,0:T(8,128)}) fusion(bf16[4,128,1024]{2,1,0:T(8,128)(2,1)S(1)} %multiply_convert_fusion.1, f32[1024,1024]{1,0:T(8,128)} %all-gather.2.cloned.1.call-done, f32[1024]{0:T(1024)S(1)} %add_rsqrt_fusion), kind=kOutput, calls=%fused_computation.91 | convolution fusion | flops 1076363264 | bytes 8392704 | tf_op jit(solution)/shard_map/gqk,ke->gqe/dot_general | solution.py:116
  74.0 3.0 %collective-permute-start.8 = (bf16[128,1024]{1,0:T(8,128)(2,1)S(1)}, bf16[128,1024]{1,0:T(8,128)(2,1)S(1)}, u32[]{:S(2)}, u32[]{:S(2)}) collective-permute-start(bf16[128,1024]{1,0:T(8,128)(2,1)S(1)} %get-tuple-element.34), channel_id=1, source_target_pairs={{0,24},{8,0},{16,8},{24,16},{1,25},{9,1},{17,9},{25,17},{2,26},{10... | collective-permute-start | bytes 786440 | tf_op jit(solution)/shard_map/ppermute | solution.py:41
  77.0 2.7 %fusion.10 = f32[1024,1024]{1,0:T(8,128)} fusion(bf16[4,128,1024]{2,1,0:T(8,128)(2,1)S(1)} %all-to-all-done, bf16[4,128,1024]{2,1,0:T(8,128)(2,1)S(1)} %multiply_convert_fusion.1), kind=kOutput, calls=%fused_computation.39 | convolution fusion | flops 268435456 | bytes 4718592 | tf_op jit(solution)/shard_map/dot_general | solution.py:125
  81.5 11.8 %collective-permute-done.7 = bf16[128,1024]{1,0:T(8,128)(2,1)S(1)} collective-permute-done((bf16[128,1024]{1,0:T(8,128)(2,1)S(1)}, bf16[128,1024]{1,0:T(8,128)(2,1)S(1)}, u32[]{:S(2)}, u32[]{:S(2)}) %collective-permute-start.7) | collective-permute-done | bytes 262176 | tf_op jit(solution)/shard_map/ppermute | solution.py:41
  97.9 6.8 %all-to-all-start.1 = ((bf16[8,2,128,4,128]{2,4,3,1,0:T(8,128)(2,1)}), bf16[8,2,128,4,128]{2,4,3,1,0:T(8,128)(2,1)}, u32[]{:S(2)}, u32[]{:S(2)}) async-start(bf16[8,2,128,4,128]{2,4,3,1,0:T(8,128)(2,1)} %copy.25), calls=%async_computation.1 | async-start | bytes 4194304 | tf_op jit(solution)/shard_map/all_to_all | solution.py:119
  107.7 2.4 add_convert_fusion
  113.7 21.7 %all-to-all-done.1 = bf16[8,2,128,4,128]{2,4,3,1,0:T(8,128)(2,1)} async-done(((bf16[8,2,128,4,128]{2,4,3,1,0:T(8,128)(2,1)}), bf16[8,2,128,4,128]{2,4,3,1,0:T(8,128)(2,1)}, u32[]{:S(2)}, u32[]{:S(2)}) %all-to-all-start.1) | async-done | bytes 2097184 | tf_op jit(solution)/shard_map/all_to_all | solution.py:119
  136.9 8.7 %all-to-all-start.2 = ((bf16[8,128,1024]{2,1,0:T(8,128)(2,1)}), bf16[8,128,1024]{2,1,0:T(8,128)(2,1)}, u32[]{:S(2)}, u32[]{:S(2)}) async-start(bf16[8,128,1024]{2,1,0:T(8,128)(2,1)} %broadcast_in_dim.134), calls=%async_computation.2 | async-start | bytes 4194304 | tf_op jit(solution)/shard_map/all_to_all | solution.py:140
  145.6 47.6 %all-reduce.2.cloned.1.call-done = bf16[1024,1024]{1,0:T(8,128)(2,1)} async-done(((bf16[1024,1024]{1,0:T(8,128)(2,1)}), bf16[1024,1024]{1,0:T(8,128)(2,1)}) %all-reduce.2.cloned.1.call-update) | async-done | bytes 2097168 | tf_op jit(solution)/shard_map/psum | solution.py:128
  193.2 3.7 %fusion = f32[1024]{0:T(1024)S(1)} fusion(bf16[1024,1024]{1,0:T(8,128)(2,1)} %all-reduce.2.cloned.1.call-done, f32[1024,1024]{1,0:T(8,128)} %all-gather.2.cloned.1.call-done, f32[1024]{0:T(1024)S(1)} %add_rsqrt_fusion), kind=kLoop, calls=%fused_computation.7 | loop fusion | flops 4193280 | bytes 6299648 | tf_op jit(solution)/shard_map/reduce_sum | solution.py:21
  198.7 2.8 %fusion.23 = (bf16[8,1,128,4,128]{2,4,3,1,0:T(8,128)(2,1)S(1)}, bf16[8,1,128,4,128]{2,4,3,1,0:T(8,128)(2,1)}) fusion(bf16[8,2,128,4,128]{2,4,3,1,0:T(8,128)(2,1)} %all-to-all-done.1), kind=kLoop, calls=%fused_computation.89 | loop fusion | bytes 4194304 | tf_op jit(solution)/shard_map/slice | solution.py:150
  201.5 3.2 %fusion.4 = f32[4,128,1024,1]{2,1,3,0:T(8,128)S(1)} fusion(bf16[8,128,1024]{2,1,0:T(8,128)(2,1)} %all-to-all-done.2, bf16[8,1,128,4,128]{2,4,3,1,0:T(8,128)(2,1)} %get-tuple-element.32), kind=kOutput, calls=%fused_computation.16 | convolution fusion | flops 1073741824 | bytes 5242880 | tf_op jit(solution)/shard_map/mqgr,mqe->gre/dot_general | solution.py:148
  204.7 2.9 %select_convert_fusion = (bf16[4,128,1024]{2,1,0:T(8,128)(2,1)}, f32[4,128,1024]{2,1,0:T(8,128)}) fusion(pred[4]{0:T(512)(128)(4,1)S(1)} %iota_compare_fusion.1, bf16[8,128,1024,1]{2,1,0,3:T(8,128)(2,1)S(1)} %bitcast.116, bf16[8,1,128,4,128]{2,4,3,1,0:T(8,128)(2,1)S(1)} %get-tuple-element.31, f32[4,128,1024,1]{2,1,3,0:T(8,128)S(1)} %fusion.4), kind=kOutput, calls=%fused_computation.18 | convolution fusion | flops 1074790400 | bytes 8388612 | tf_op jit(solution)/shard_map/mqgr,mqe->gre/dot_general | solution.py:150
  207.6 7.2 %convolution_convert_fusion.1 = bf16[128,4096]{1,0:T(8,128)(2,1)} fusion(bf16[128,1024]{1,0:T(8,128)(2,1)S(1)} %multiply_convert_fusion.2, bf16[4096,1024]{1,0:T(8,128)(2,1)} %param.11), kind=kOutput, calls=%fused_computation.6 | convolution fusion | flops 1074266112 | bytes 9699328 | tf_op jit(solution)/shard_map/qe,de->qd/dot_general | solution.py:133
  214.8 7.3 %convolution_convert_fusion = bf16[128,4096]{1,0:T(8,128)(2,1)} fusion(bf16[4096,1024]{1,0:T(8,128)(2,1)} %param.11, bf16[1024,1024]{1,0:T(8,128)(2,1)S(1)} %fusion.2, s32[]{:T(128)S(6)} %select_n.153), kind=kOutput, calls=%fused_computation.5 | convolution fusion | flops 1074266112 | bytes 9699332 | tf_op jit(solution)/shard_map/qe,de->qd/dot_general | solution.py:136
  222.1 13.4 %reduce-scatter.2.cloned.1.call-done = bf16[1,128,1024]{2,1,0:T(8,128)(2,1)} async-done(((bf16[4,128,1024]{2,1,0:T(8,128)(2,1)}), bf16[1,128,1024]{2,1,0:T(8,128)(2,1)}) %reduce-scatter.2.cloned.1.call-update) | async-done | bytes 262160 | tf_op jit(solution)/shard_map/reduce_scatter | solution.py:153
  (99 shorter events, 36.9 us)
Async XLA Ops:
  7.2 6.0 %copy-start.14 = (s32[1,16]{1,0:T(1,128)S(1)}, s32[1,16]{1,0:T(1,128)}, u32[]{:S(2)}) copy-start(s32[1,16]{1,0:T(1,128)} %param.12) | copy-start | bytes 196
  7.2 10.7 %copy-start.9 = (bf16[128,4096]{1,0:T(8,128)(2,1)S(1)}, bf16[128,4096]{1,0:T(8,128)(2,1)}, u32[]{:S(2)}) copy-start(bf16[128,4096]{1,0:T(8,128)(2,1)} %param.9) | copy-start | bytes 3145732
  7.2 44.3 %all-gather.2.cloned.1.call-start = ((), (), s32[]{:S(2)}) async-start(), calls=%async_computation.4 | async-start | bytes 4718592 | tf_op jit(solution)/shard_map/all_gather | solution.py:65
  13.1 20.7 %collective-permute-start = (s32[16]{0:T(128)S(1)}, s32[16]{0:T(128)S(1)}, u32[]{:S(2)}, u32[]{:S(2)}) collective-permute-start(s32[16]{0:T(128)S(1)} %bitcast.128), channel_id=1, source_target_pairs={{0,8},{8,16},{16,24},{24,0},{1,9},{9,17},{17,25},{25,1},{2,10},{10... | collective-permute-start | bytes 200 | tf_op jit(solution)/shard_map/ppermute | solution.py:30
  14.5 19.4 %collective-permute-start.1 = (s32[16]{0:T(128)S(1)}, s32[16]{0:T(128)S(1)}, u32[]{:S(2)}, u32[]{:S(2)}) collective-permute-start(s32[16]{0:T(128)S(1)} %bitcast.129), channel_id=1, source_target_pairs={{0,16},{8,24},{16,0},{24,8},{1,17},{9,25},{17,1},{25,9},{2,18},{10... | collective-permute-start | bytes 200 | tf_op jit(solution)/shard_map/ppermute | solution.py:30
  16.8 17.1 %collective-permute-start.2 = (s32[16]{0:T(128)S(1)}, s32[16]{0:T(128)S(1)}, u32[]{:S(2)}, u32[]{:S(2)}) collective-permute-start(s32[16]{0:T(128)S(1)} %bitcast.130), channel_id=1, source_target_pairs={{0,24},{8,0},{16,8},{24,16},{1,25},{9,1},{17,9},{25,17},{2,26},{10... | collective-permute-start | bytes 200 | tf_op jit(solution)/shard_map/ppermute | solution.py:30
  23.8 5.0 %copy-start.10 = (bf16[128,4096]{1,0:T(8,128)(2,1)S(1)}, bf16[128,4096]{1,0:T(8,128)(2,1)}, u32[]{:S(2)}) copy-start(bf16[128,4096]{1,0:T(8,128)(2,1)} %param.10) | copy-start | bytes 3145732
  23.8 30.2 %all-to-all-start = ((bf16[4,128,1024]{2,1,0:T(8,128)(2,1)}), bf16[4,128,1024]{2,1,0:T(8,128)(2,1)S(1)}, u32[]{:S(2)}, u32[]{:S(2)}) async-start(bf16[4,128,1024]{2,1,0:T(8,128)(2,1)} %broadcast_in_dim.126), calls=%async_computation | async-start | bytes 2097152 | tf_op jit(solution)/shard_map/all_to_all | solution.py:74
  58.4 3.7 %collective-permute-start.4 = (f32[3,4,128]{2,1,0:T(4,128)S(1)}, f32[3,4,128]{2,1,0:T(4,128)S(1)}, u32[]{:S(2)}, u32[]{:S(2)}) collective-permute-start(f32[3,4,128]{2,1,0:T(4,128)S(1)} %get-tuple-element.38), channel_id=1, source_target_pairs={{0,16},{8,24},{16,0},{24,8},{1,17},{9,25},{17,1},{25,9},{2,18},{10... | collective-permute-start | bytes 18440 | tf_op jit(solution)/shard_map/ppermute | solution.py:30
  60.6 2.5 %collective-permute-start.5 = (f32[3,4,128]{2,1,0:T(4,128)S(1)}, f32[3,4,128]{2,1,0:T(4,128)S(1)}, u32[]{:S(2)}, u32[]{:S(2)}) collective-permute-start(f32[3,4,128]{2,1,0:T(4,128)S(1)} %get-tuple-element.38), channel_id=1, source_target_pairs={{0,24},{8,0},{16,8},{24,16},{1,25},{9,1},{17,9},{25,17},{2,26},{10... | collective-permute-start | bytes 18440 | tf_op jit(solution)/shard_map/ppermute | solution.py:30
  61.7 4.3 %collective-permute-start.3 = (f32[3,4,128]{2,1,0:T(4,128)S(1)}, f32[3,4,128]{2,1,0:T(4,128)S(1)}, u32[]{:S(2)}, u32[]{:S(2)}) collective-permute-start(f32[3,4,128]{2,1,0:T(4,128)S(1)} %get-tuple-element.38), channel_id=1, source_target_pairs={{0,8},{8,16},{16,24},{24,0},{1,9},{9,17},{17,25},{25,1},{2,10},{10... | collective-permute-start | bytes 18440 | tf_op jit(solution)/shard_map/ppermute | solution.py:30
  68.3 8.7 %copy-start.2 = (bf16[4,128,1024]{2,1,0:T(8,128)(2,1)}, bf16[4,128,1024]{2,1,0:T(8,128)(2,1)S(1)}, u32[]{:S(2)}) copy-start(bf16[4,128,1024]{2,1,0:T(8,128)(2,1)S(1)} %multiply_convert_fusion.1) | copy-start | bytes 3145732
  73.7 7.9 %collective-permute-start.6 = (bf16[128,1024]{1,0:T(8,128)(2,1)S(1)}, bf16[128,1024]{1,0:T(8,128)(2,1)S(1)}, u32[]{:S(2)}, u32[]{:S(2)}) collective-permute-start(bf16[128,1024]{1,0:T(8,128)(2,1)S(1)} %get-tuple-element.36), channel_id=1, source_target_pairs={{0,8},{8,16},{16,24},{24,0},{1,9},{9,17},{17,25},{25,1},{2,10},{10... | collective-permute-start | bytes 786440 | tf_op jit(solution)/shard_map/ppermute | solution.py:41
  73.7 19.6 %collective-permute-start.7 = (bf16[128,1024]{1,0:T(8,128)(2,1)S(1)}, bf16[128,1024]{1,0:T(8,128)(2,1)S(1)}, u32[]{:S(2)}, u32[]{:S(2)}) collective-permute-start(bf16[128,1024]{1,0:T(8,128)(2,1)S(1)} %get-tuple-element.35), channel_id=1, source_target_pairs={{0,16},{8,24},{16,0},{24,8},{1,17},{9,25},{17,1},{25,9},{2,18},{10... | collective-permute-start | bytes 786440 | tf_op jit(solution)/shard_map/ppermute | solution.py:41
  74.0 19.4 %collective-permute-start.8 = (bf16[128,1024]{1,0:T(8,128)(2,1)S(1)}, bf16[128,1024]{1,0:T(8,128)(2,1)S(1)}, u32[]{:S(2)}, u32[]{:S(2)}) collective-permute-start(bf16[128,1024]{1,0:T(8,128)(2,1)S(1)} %get-tuple-element.34), channel_id=1, source_target_pairs={{0,24},{8,0},{16,8},{24,16},{1,25},{9,1},{17,9},{25,17},{2,26},{10... | collective-permute-start | bytes 786440 | tf_op jit(solution)/shard_map/ppermute | solution.py:41
  94.1 2.3 copy-start.5
  97.9 6.8 %copy-start.3 = (bf16[4,128,1024]{2,1,0:T(8,128)(2,1)S(1)}, bf16[4,128,1024]{2,1,0:T(8,128)(2,1)}, u32[]{:S(2)}) copy-start(bf16[4,128,1024]{2,1,0:T(8,128)(2,1)} %copy-done.2) | copy-start | bytes 3145732
  97.9 37.4 %all-to-all-start.1 = ((bf16[8,2,128,4,128]{2,4,3,1,0:T(8,128)(2,1)}), bf16[8,2,128,4,128]{2,4,3,1,0:T(8,128)(2,1)}, u32[]{:S(2)}, u32[]{:S(2)}) async-start(bf16[8,2,128,4,128]{2,4,3,1,0:T(8,128)(2,1)} %copy.25), calls=%async_computation.1 | async-start | bytes 4194304 | tf_op jit(solution)/shard_map/all_to_all | solution.py:119
  104.7 88.4 %all-reduce.2.cloned.1.call-start = ((), (), s32[]{:S(2)}) async-start(), calls=%async_computation.5 | async-start | bytes 4194304 | tf_op jit(solution)/shard_map/psum | solution.py:128
  105.5 2.2 copy-start.1
  136.9 64.6 %all-to-all-start.2 = ((bf16[8,128,1024]{2,1,0:T(8,128)(2,1)}), bf16[8,128,1024]{2,1,0:T(8,128)(2,1)}, u32[]{:S(2)}, u32[]{:S(2)}) async-start(bf16[8,128,1024]{2,1,0:T(8,128)(2,1)} %broadcast_in_dim.134), calls=%async_computation.2 | async-start | bytes 4194304 | tf_op jit(solution)/shard_map/all_to_all | solution.py:140
  145.6 90.0 %reduce-scatter.2.cloned.1.call-start = ((), (), s32[]{:S(2)}) async-start(), calls=%async_computation.6 | async-start | bytes 1310720 | tf_op jit(solution)/shard_map/reduce_scatter | solution.py:153
  193.2 4.0 %copy-start = (f32[1024,1024]{1,0:T(8,128)S(1)}, f32[1024,1024]{1,0:T(8,128)}, u32[]{:S(2)}) copy-start(f32[1024,1024]{1,0:T(8,128)} %all-gather.2.cloned.1.call-done) | copy-start | bytes 12582916
  193.2 4.7 %copy-start.4 = (bf16[1024,1024]{1,0:T(8,128)(2,1)S(1)}, bf16[1024,1024]{1,0:T(8,128)(2,1)}, u32[]{:S(2)}) copy-start(bf16[1024,1024]{1,0:T(8,128)(2,1)} %all-reduce.2.cloned.1.call-done) | copy-start | bytes 6291460
  (6 other events, 8.3 us)
Sparse Core Ops, SparseCore 0:
  13.2 38.2 all-gather.1
  110.2 82.9 all-reduce.1
  207.7 27.8 reduce-scatter.1

commit v12 on v10

--- a/solution.py
+++ b/solution.py
@@ -114,17 +114,19 @@
         factor[:, :, None] * (jnp.exp(scores - log_total[:, :, None]) - positive)
     ).astype(jnp.bfloat16)
 
-    delta_parts = jnp.einsum("gqk,ke->gqe", grad, group_codes, preferred_element_type=jnp.float32)
-    returned = exchange(delta_parts.astype(jnp.bfloat16), "group").astype(jnp.float32)
-    own_part = jnp.take(delta_parts, group_index, axis=0)
-    query_delta = own_part + jnp.sum(jnp.where(own[:, None, None], 0.0, returned), axis=0)
-
     code_terms = None
     for g in range(groups):
         term = jnp.dot(grad[g].T, q_all[g], preferred_element_type=jnp.float32)
         term = jnp.where(g == group_index, term, term.astype(jnp.bfloat16).astype(jnp.float32))
         code_terms = term if code_terms is None else code_terms + term
-    code_delta = lax.psum(code_terms.astype(jnp.bfloat16), "member").astype(jnp.float32)
+    code_sum = code_terms.astype(jnp.bfloat16)
+    grad_dq, code_sum = lax.optimization_barrier((grad, code_sum))
+    code_delta = lax.psum(code_sum, "member").astype(jnp.float32)
+    delta_parts = jnp.einsum("gqk,ke->gqe", grad_dq, group_codes, preferred_element_type=jnp.float32)
+    returned = exchange(delta_parts.astype(jnp.bfloat16), "group").astype(jnp.float32)
+    own_part = jnp.take(delta_parts, group_index, axis=0)
+    query_delta = own_part + jnp.sum(jnp.where(own[:, None, None], 0.0, returned), axis=0)
+
 
     dz_query = norm_back(query_delta, q_unit, q_inv)
     dz_code_all = norm_back(code_delta, c_unit, c_inv)

time: 208 us -> 205 us (0.986)
    psum x1, waiting for transfers between devices: 41.7 us -> 35.2 us  [body(): code_delta = lax.psum(code_sum, 'member').astype(jnp.float32)]
    ppermute x3, waiting for transfers between devices: 12 us -> 16.4 us  [exchange(): lax.ppermute(sent, axis, [(i, (i + s) % size) for i in range(size)])]
where the time goes in v12:
time: 205 us; the launch traced here: 203 us
  waiting for transfers between devices  85.8 us (42%)
  matrix products  43.4 us (21%)
  starting transfers between devices  26.6 us (13%)
  other arithmetic  17.9 us (9%)
  local copies, waits for them, and re-layouts  15 us (7%)
  between operations  14 us (7%)
    psum x1, waiting for transfers between devices, body(): code_delta = lax.psum(code_sum, 'member').astype(jnp.float32)  35.2 us
    all_gather x1, waiting for transfers between devices, body(): lax.all_gather(jnp.dot(code_feat, projection, preferred_element_type=jnp....  16.5 us
    ppermute x3, waiting for transfers between devices, exchange(): lax.ppermute(sent, axis, [(i, (i + s) % size) for i in range(size)])  16.4 us
    reduce_scatter x1, waiting for transfers between devices, body(): lax.psum_scatter(sent_proj, 'group', scatter_dimension=0, tiled=True)  13.6 us
    ppermute x6, starting transfers between devices, shift_all(): lax.ppermute(x, axis, [(i, (i + s) % size) for i in range(size)])  8.38 us
    dot_general x1, matrix products, body(): jnp.einsum('qe,de->qd', dz_code, projection, preferred_element_type=jnp.f...  7.39 us
    dot_general x1, matrix products, body(): jnp.einsum('qe,de->qd', dz_query, projection, preferred_element_type=jnp....  7.24 us
    all_to_all x1, starting transfers between devices, body(): lax.all_to_all(jnp.broadcast_to(dz_query[None], (members, queries_dev, em...  6.61 us
  transfers between devices with their start and end apart: 15, of which 7 were waited for; matrix products, arithmetic and copies ran while one was open for 30% of the time, Pallas kernels for 0%

profile of v12, /device:TPU:3, one launch (start us, length us, event | category | flops | bytes accessed | tf_op | source)
XLA Modules:
  0.0 202.7 jit_solution(2245639925189366476)
XLA Ops:
  7.2 5.8 %fusion.26 = f32[128,1024]{1,0:T(8,128)} fusion(bf16[128,4096]{1,0:T(8,128)(2,1)} %param.10, bf16[4096,1024]{1,0:T(8,128)(2,1)} %param.11), kind=kOutput, calls=%fused_computation.91 | convolution fusion | flops 1073741824 | bytes 9961472 | tf_op jit(solution)/shard_map/dot_general | solution.py:67
  14.5 2.3 %collective-permute-start.1 = (s32[16]{0:T(128)S(1)}, s32[16]{0:T(128)S(1)}, u32[]{:S(2)}, u32[]{:S(2)}) collective-permute-start(s32[16]{0:T(128)S(1)} %bitcast.129), channel_id=1, source_target_pairs={{0,16},{8,24},{16,0},{24,8},{1,17},{9,25},{17,1},{25,9},{2,18},{10... | collective-permute-start | bytes 200 | tf_op jit(solution)/shard_map/ppermute | solution.py:30
  17.8 4.7 %multiply_reduce_fusion.2 = (f32[128]{0:T(128)S(1)}, f32[128,1024]{1,0:T(8,128)S(1)}) fusion(bf16[128,4096]{1,0:T(8,128)(2,1)S(1)} %copy-done.5, bf16[4096,1024]{1,0:T(8,128)(2,1)} %param.11), kind=kOutput, calls=%fused_computation.31 | convolution fusion | flops 1074003840 | bytes 9961984 | tf_op jit(solution)/shard_map/dot_general | solution.py:14
  23.8 3.6 %all-to-all-start = ((bf16[4,128,1024]{2,1,0:T(8,128)(2,1)}), bf16[4,128,1024]{2,1,0:T(8,128)(2,1)S(1)}, u32[]{:S(2)}, u32[]{:S(2)}) async-start(bf16[4,128,1024]{2,1,0:T(8,128)(2,1)} %broadcast_in_dim.126), calls=%async_computation | async-start | bytes 2097152 | tf_op jit(solution)/shard_map/all_to_all | solution.py:75
  35.0 16.5 %all-gather.2.cloned.1.call-done = f32[1024,1024]{1,0:T(8,128)} async-done(((f32[128,1024]{1,0:T(8,128)}), f32[1024,1024]{1,0:T(8,128)}) %all-gather.2.cloned.1.call-update) | async-done | bytes 4194320 | tf_op jit(solution)/shard_map/all_gather | solution.py:66
  51.5 2.5 %multiply_reduce_fusion = f32[1024]{0:T(1024)S(1)} fusion(f32[1024,1024]{1,0:T(8,128)} %all-gather.2.cloned.1.call-done), kind=kLoop, calls=%fused_computation.11 | loop fusion | flops 2096128 | bytes 4198400 | tf_op jit(solution)/shard_map/reduce_sum | solution.py:72
  54.0 4.7 %all-to-all-start.1 = ((bf16[8,2,128,4,128]{2,4,3,1,0:T(8,128)(2,1)}), bf16[8,2,128,4,128]{2,4,3,1,0:T(8,128)(2,1)}, u32[]{:S(2)}, u32[]{:S(2)}) async-start(bf16[8,2,128,4,128]{2,4,3,1,0:T(8,128)(2,1)} %copy.25), calls=%async_computation.1 | async-start | bytes 4194304 | tf_op jit(solution)/shard_map/all_to_all | solution.py:63
  58.7 3.6 %fusion.24 = (f32[4,128]{1,0:T(4,128)S(1)}, f32[4,128,1024]{2,1,0:T(8,128)S(1)}) fusion(bf16[4,128,1024]{2,1,0:T(8,128)(2,1)S(1)} %all-to-all-done, f32[1024,1024]{1,0:T(8,128)} %all-gather.2.cloned.1.call-done, f32[1024]{0:T(1024)S(1)} %add_rsqrt_fusion, pred[4,1024]{1,0:T(4,128)(4,1)S(1)} %broadcast_in_dim.124), kind=kOutput, calls=%fused_computation.89 | convolution fusion | flops 1077411328 | bytes 7350272 | tf_op jit(solution)/shard_map/gqe,ke->gqk/dot_general | solution.py:92
  68.1 2.6 %collective-permute-done.3 = f32[3,4,128]{2,1,0:T(4,128)S(1)} collective-permute-done((f32[3,4,128]{2,1,0:T(4,128)S(1)}, f32[3,4,128]{2,1,0:T(4,128)S(1)}, u32[]{:S(2)}, u32[]{:S(2)}) %collective-permute-start.3) | collective-permute-done | bytes 6176 | tf_op jit(solution)/shard_map/ppermute | solution.py:30
  75.2 2.4 %add_convert_fusion = bf16[1024,1024]{1,0:T(8,128)(2,1)} fusion(f32[1024,1024]{1,0:T(8,128)S(1)} %fusion.10, f32[1024,1024]{1,0:T(8,128)S(1)} %fusion.11, f32[1024,1024]{1,0:T(8,128)S(1)} %fusion.12, pred[]{:T(512)S(6)} %eq.75, pred[]{:T(512)S(6)} %eq.74, pred[]{:T(512)S(6)} %eq.73, pred[]{:T(512)S(6)} %eq.72, bf16[4,128,1024]{2,1,0:T(8,128)(2,1)S(1)} %all-to-all-done, ...), kind=kOutput, calls=%fused_computation.10 | convolution fusion | flops 285212672 | bytes 15204356 | tf_op jit(solution)/shard_map/dot_general | solution.py:119
  77.6 3.8 %fusion.25 = (bf16[4,128,1024]{2,1,0:T(8,128)(2,1)S(1)}, f32[4,128,1024]{2,1,0:T(8,128)S(1)}) fusion(bf16[4,128,1024]{2,1,0:T(8,128)(2,1)} %copy-done.1, f32[1024,1024]{1,0:T(8,128)} %all-gather.2.cloned.1.call-done, f32[1024]{0:T(1024)S(1)} %add_rsqrt_fusion), kind=kOutput, calls=%fused_computation.90 | convolution fusion | flops 1076363264 | bytes 8392704 | tf_op jit(solution)/shard_map/gqk,ke->gqe/dot_general | solution.py:125
  82.6 3.0 %collective-permute-start.8 = (bf16[128,1024]{1,0:T(8,128)(2,1)}, bf16[128,1024]{1,0:T(8,128)(2,1)S(1)}, u32[]{:S(2)}, u32[]{:S(2)}) collective-permute-start(bf16[128,1024]{1,0:T(8,128)(2,1)} %get-tuple-element.34), channel_id=1, source_target_pairs={{0,24},{8,0},{16,8},{24,16},{1,25},{9,1},{17,9},{25,17},{2,26},{10... | collective-permute-start | bytes 786440 | tf_op jit(solution)/shard_map/ppermute | solution.py:41
  85.6 4.6 %collective-permute-done.6 = bf16[128,1024]{1,0:T(8,128)(2,1)S(1)} collective-permute-done((bf16[128,1024]{1,0:T(8,128)(2,1)}, bf16[128,1024]{1,0:T(8,128)(2,1)S(1)}, u32[]{:S(2)}, u32[]{:S(2)}) %collective-permute-start.6) | collective-permute-done | bytes 262176 | tf_op jit(solution)/shard_map/ppermute | solution.py:41
  90.2 11.8 %collective-permute-done.7 = bf16[128,1024]{1,0:T(8,128)(2,1)S(1)} collective-permute-done((bf16[128,1024]{1,0:T(8,128)(2,1)}, bf16[128,1024]{1,0:T(8,128)(2,1)S(1)}, u32[]{:S(2)}, u32[]{:S(2)}) %collective-permute-start.7) | collective-permute-done | bytes 262176 | tf_op jit(solution)/shard_map/ppermute | solution.py:41
  103.2 2.9 %gather_fusion.2 = bf16[4,128,1024]{2,1,0:T(8,128)(2,1)} fusion(bf16[4,128,1024]{2,1,0:T(8,128)(2,1)} %pad_maximum_fusion, s32[1024]{0:T(1024)S(1)} %pad_clamp_fusion), kind=kCustom, calls=%fused_computation.2 | custom fusion | bytes 2097168 | tf_op jit(solution)/shard_map/jit(_take)/gather | solution.py:43
  109.7 6.6 %all-to-all-start.2 = ((bf16[8,128,1024]{2,1,0:T(8,128)(2,1)}), bf16[8,128,1024]{2,1,0:T(8,128)(2,1)}, u32[]{:S(2)}, u32[]{:S(2)}) async-start(bf16[8,128,1024]{2,1,0:T(8,128)(2,1)} %broadcast_in_dim.134), calls=%async_computation.2 | async-start | bytes 4194304 | tf_op jit(solution)/shard_map/all_to_all | solution.py:141
  116.3 2.8 %fusion.23 = (bf16[8,1,128,4,128]{2,4,3,1,0:T(8,128)(2,1)S(1)}, bf16[8,1,128,4,128]{2,4,3,1,0:T(8,128)(2,1)}) fusion(bf16[8,2,128,4,128]{2,4,3,1,0:T(8,128)(2,1)} %all-to-all-done.1), kind=kLoop, calls=%fused_computation.88 | loop fusion | bytes 4194304 | tf_op jit(solution)/shard_map/slice | solution.py:151
  119.1 35.2 %all-reduce.2.cloned.1.call-done = bf16[1024,1024]{1,0:T(8,128)(2,1)} async-done(((bf16[1024,1024]{1,0:T(8,128)(2,1)}), bf16[1024,1024]{1,0:T(8,128)(2,1)}) %all-reduce.2.cloned.1.call-update) | async-done | bytes 2097168 | tf_op jit(solution)/shard_map/psum | solution.py:124
  154.3 3.7 %fusion = f32[1024]{0:T(1024)S(1)} fusion(bf16[1024,1024]{1,0:T(8,128)(2,1)} %all-reduce.2.cloned.1.call-done, f32[1024,1024]{1,0:T(8,128)} %all-gather.2.cloned.1.call-done, f32[1024]{0:T(1024)S(1)} %add_rsqrt_fusion), kind=kLoop, calls=%fused_computation.7 | loop fusion | flops 4193280 | bytes 6299648 | tf_op jit(solution)/shard_map/reduce_sum | solution.py:21
  159.9 3.2 %fusion.4 = f32[4,128,1024,1]{2,1,3,0:T(8,128)S(1)} fusion(bf16[8,128,1024]{2,1,0:T(8,128)(2,1)} %all-to-all-done.2, bf16[8,1,128,4,128]{2,4,3,1,0:T(8,128)(2,1)} %get-tuple-element.32), kind=kOutput, calls=%fused_computation.16 | convolution fusion | flops 1073741824 | bytes 5242880 | tf_op jit(solution)/shard_map/mqgr,mqe->gre/dot_general | solution.py:149
  163.0 2.9 %select_convert_fusion = (bf16[4,128,1024]{2,1,0:T(8,128)(2,1)}, f32[4,128,1024]{2,1,0:T(8,128)}) fusion(pred[4]{0:T(512)(128)(4,1)S(1)} %iota_compare_fusion.1, bf16[8,128,1024,1]{2,1,0,3:T(8,128)(2,1)S(1)} %bitcast.116, bf16[8,1,128,4,128]{2,4,3,1,0:T(8,128)(2,1)S(1)} %get-tuple-element.31, f32[4,128,1024,1]{2,1,3,0:T(8,128)S(1)} %fusion.4), kind=kOutput, calls=%fused_computation.18 | convolution fusion | flops 1074790400 | bytes 8388612 | tf_op jit(solution)/shard_map/mqgr,mqe->gre/dot_general | solution.py:151
  166.0 7.2 %convolution_convert_fusion.1 = bf16[128,4096]{1,0:T(8,128)(2,1)} fusion(bf16[128,1024]{1,0:T(8,128)(2,1)S(1)} %multiply_convert_fusion.2, bf16[4096,1024]{1,0:T(8,128)(2,1)} %param.11), kind=kOutput, calls=%fused_computation.6 | convolution fusion | flops 1074266112 | bytes 9699328 | tf_op jit(solution)/shard_map/qe,de->qd/dot_general | solution.py:134
  173.2 7.4 %convolution_convert_fusion = bf16[128,4096]{1,0:T(8,128)(2,1)} fusion(bf16[4096,1024]{1,0:T(8,128)(2,1)} %param.11, bf16[1024,1024]{1,0:T(8,128)(2,1)S(1)} %fusion.2, s32[]{:T(128)S(6)} %select_n.153), kind=kOutput, calls=%fused_computation.5 | convolution fusion | flops 1074266112 | bytes 9699332 | tf_op jit(solution)/shard_map/qe,de->qd/dot_general | solution.py:137
  180.6 13.6 %reduce-scatter.2.cloned.1.call-done = bf16[1,128,1024]{2,1,0:T(8,128)(2,1)} async-done(((bf16[4,128,1024]{2,1,0:T(8,128)(2,1)}), bf16[1,128,1024]{2,1,0:T(8,128)(2,1)}) %reduce-scatter.2.cloned.1.call-update) | async-done | bytes 262160 | tf_op jit(solution)/shard_map/reduce_scatter | solution.py:154
  (88 shorter events, 31.1 us)
Async XLA Ops:
  7.2 5.9 %copy-start.9 = (s32[1,16]{1,0:T(1,128)S(1)}, s32[1,16]{1,0:T(1,128)}, u32[]{:S(2)}) copy-start(s32[1,16]{1,0:T(1,128)} %param.12) | copy-start | bytes 196
  7.2 10.7 %copy-start.5 = (bf16[128,4096]{1,0:T(8,128)(2,1)S(1)}, bf16[128,4096]{1,0:T(8,128)(2,1)}, u32[]{:S(2)}) copy-start(bf16[128,4096]{1,0:T(8,128)(2,1)} %param.9) | copy-start | bytes 3145732
  7.2 44.3 %all-gather.2.cloned.1.call-start = ((), (), s32[]{:S(2)}) async-start(), calls=%async_computation.4 | async-start | bytes 4718592 | tf_op jit(solution)/shard_map/all_gather | solution.py:66
  13.1 20.8 %collective-permute-start = (s32[16]{0:T(128)S(1)}, s32[16]{0:T(128)S(1)}, u32[]{:S(2)}, u32[]{:S(2)}) collective-permute-start(s32[16]{0:T(128)S(1)} %bitcast.128), channel_id=1, source_target_pairs={{0,8},{8,16},{16,24},{24,0},{1,9},{9,17},{17,25},{25,1},{2,10},{10... | collective-permute-start | bytes 200 | tf_op jit(solution)/shard_map/ppermute | solution.py:30
  14.5 19.5 %collective-permute-start.1 = (s32[16]{0:T(128)S(1)}, s32[16]{0:T(128)S(1)}, u32[]{:S(2)}, u32[]{:S(2)}) collective-permute-start(s32[16]{0:T(128)S(1)} %bitcast.129), channel_id=1, source_target_pairs={{0,16},{8,24},{16,0},{24,8},{1,17},{9,25},{17,1},{25,9},{2,18},{10... | collective-permute-start | bytes 200 | tf_op jit(solution)/shard_map/ppermute | solution.py:30
  16.8 17.2 %collective-permute-start.2 = (s32[16]{0:T(128)S(1)}, s32[16]{0:T(128)S(1)}, u32[]{:S(2)}, u32[]{:S(2)}) collective-permute-start(s32[16]{0:T(128)S(1)} %bitcast.130), channel_id=1, source_target_pairs={{0,24},{8,0},{16,8},{24,16},{1,25},{9,1},{17,9},{25,17},{2,26},{10... | collective-permute-start | bytes 200 | tf_op jit(solution)/shard_map/ppermute | solution.py:30
  22.6 1.2 copy-start.3
  23.8 5.1 %copy-start.6 = (bf16[128,4096]{1,0:T(8,128)(2,1)S(1)}, bf16[128,4096]{1,0:T(8,128)(2,1)}, u32[]{:S(2)}) copy-start(bf16[128,4096]{1,0:T(8,128)(2,1)} %param.10) | copy-start | bytes 3145732
  23.8 30.2 %all-to-all-start = ((bf16[4,128,1024]{2,1,0:T(8,128)(2,1)}), bf16[4,128,1024]{2,1,0:T(8,128)(2,1)S(1)}, u32[]{:S(2)}, u32[]{:S(2)}) async-start(bf16[4,128,1024]{2,1,0:T(8,128)(2,1)} %broadcast_in_dim.126), calls=%async_computation | async-start | bytes 2097152 | tf_op jit(solution)/shard_map/all_to_all | solution.py:75
  28.9 1.3 copy-start.7
  54.0 54.0 %all-to-all-start.1 = ((bf16[8,2,128,4,128]{2,4,3,1,0:T(8,128)(2,1)}), bf16[8,2,128,4,128]{2,4,3,1,0:T(8,128)(2,1)}, u32[]{:S(2)}, u32[]{:S(2)}) async-start(bf16[8,2,128,4,128]{2,4,3,1,0:T(8,128)(2,1)} %copy.25), calls=%async_computation.1 | async-start | bytes 4194304 | tf_op jit(solution)/shard_map/all_to_all | solution.py:63
  58.7 95.6 %all-reduce.2.cloned.1.call-start = ((), (), s32[]{:S(2)}) async-start(), calls=%async_computation.5 | async-start | bytes 4194304 | tf_op jit(solution)/shard_map/psum | solution.py:124
  63.0 3.7 %collective-permute-start.4 = (f32[3,4,128]{2,1,0:T(4,128)S(1)}, f32[3,4,128]{2,1,0:T(4,128)S(1)}, u32[]{:S(2)}, u32[]{:S(2)}) collective-permute-start(f32[3,4,128]{2,1,0:T(4,128)S(1)} %get-tuple-element.38), channel_id=1, source_target_pairs={{0,16},{8,24},{16,0},{24,8},{1,17},{9,25},{17,1},{25,9},{2,18},{10... | collective-permute-start | bytes 18440 | tf_op jit(solution)/shard_map/ppermute | solution.py:30
  65.2 2.9 %collective-permute-start.5 = (f32[3,4,128]{2,1,0:T(4,128)S(1)}, f32[3,4,128]{2,1,0:T(4,128)S(1)}, u32[]{:S(2)}, u32[]{:S(2)}) collective-permute-start(f32[3,4,128]{2,1,0:T(4,128)S(1)} %get-tuple-element.38), channel_id=1, source_target_pairs={{0,24},{8,0},{16,8},{24,16},{1,25},{9,1},{17,9},{25,17},{2,26},{10... | collective-permute-start | bytes 18440 | tf_op jit(solution)/shard_map/ppermute | solution.py:30
  66.4 4.3 %collective-permute-start.3 = (f32[3,4,128]{2,1,0:T(4,128)S(1)}, f32[3,4,128]{2,1,0:T(4,128)S(1)}, u32[]{:S(2)}, u32[]{:S(2)}) collective-permute-start(f32[3,4,128]{2,1,0:T(4,128)S(1)} %get-tuple-element.38), channel_id=1, source_target_pairs={{0,8},{8,16},{16,24},{24,0},{1,9},{9,17},{17,25},{25,1},{2,10},{10... | collective-permute-start | bytes 18440 | tf_op jit(solution)/shard_map/ppermute | solution.py:30
  72.9 2.2 %copy-start.1 = (bf16[4,128,1024]{2,1,0:T(8,128)(2,1)}, bf16[4,128,1024]{2,1,0:T(8,128)(2,1)S(1)}, u32[]{:S(2)}) copy-start(bf16[4,128,1024]{2,1,0:T(8,128)(2,1)S(1)} %multiply_convert_fusion.1) | copy-start | bytes 3145732
  82.3 7.9 %collective-permute-start.6 = (bf16[128,1024]{1,0:T(8,128)(2,1)}, bf16[128,1024]{1,0:T(8,128)(2,1)S(1)}, u32[]{:S(2)}, u32[]{:S(2)}) collective-permute-start(bf16[128,1024]{1,0:T(8,128)(2,1)} %get-tuple-element.36), channel_id=1, source_target_pairs={{0,8},{8,16},{16,24},{24,0},{1,9},{9,17},{17,25},{25,1},{2,10},{10... | collective-permute-start | bytes 786440 | tf_op jit(solution)/shard_map/ppermute | solution.py:41
  82.3 19.7 %collective-permute-start.7 = (bf16[128,1024]{1,0:T(8,128)(2,1)}, bf16[128,1024]{1,0:T(8,128)(2,1)S(1)}, u32[]{:S(2)}, u32[]{:S(2)}) collective-permute-start(bf16[128,1024]{1,0:T(8,128)(2,1)} %get-tuple-element.35), channel_id=1, source_target_pairs={{0,16},{8,24},{16,0},{24,8},{1,17},{9,25},{17,1},{25,9},{2,18},{10... | collective-permute-start | bytes 786440 | tf_op jit(solution)/shard_map/ppermute | solution.py:41
  82.6 19.4 %collective-permute-start.8 = (bf16[128,1024]{1,0:T(8,128)(2,1)}, bf16[128,1024]{1,0:T(8,128)(2,1)S(1)}, u32[]{:S(2)}, u32[]{:S(2)}) collective-permute-start(bf16[128,1024]{1,0:T(8,128)(2,1)} %get-tuple-element.34), channel_id=1, source_target_pairs={{0,24},{8,0},{16,8},{24,16},{1,25},{9,1},{17,9},{25,17},{2,26},{10... | collective-permute-start | bytes 786440 | tf_op jit(solution)/shard_map/ppermute | solution.py:41
  103.2 4.5 %copy-start.4 = (f32[128,1024]{1,0:T(8,128)S(1)}, f32[128,1024]{1,0:T(8,128)}, u32[]{:S(2)}) copy-start(f32[128,1024]{1,0:T(8,128)} %copy-done.3) | copy-start | bytes 1572868
  109.7 50.2 %all-to-all-start.2 = ((bf16[8,128,1024]{2,1,0:T(8,128)(2,1)}), bf16[8,128,1024]{2,1,0:T(8,128)(2,1)}, u32[]{:S(2)}, u32[]{:S(2)}) async-start(bf16[8,128,1024]{2,1,0:T(8,128)(2,1)} %broadcast_in_dim.134), calls=%async_computation.2 | async-start | bytes 4194304 | tf_op jit(solution)/shard_map/all_to_all | solution.py:141
  116.3 77.9 %reduce-scatter.2.cloned.1.call-start = ((), (), s32[]{:S(2)}) async-start(), calls=%async_computation.6 | async-start | bytes 1310720 | tf_op jit(solution)/shard_map/reduce_scatter | solution.py:154
  154.3 4.0 %copy-start = (f32[1024,1024]{1,0:T(8,128)S(1)}, f32[1024,1024]{1,0:T(8,128)}, u32[]{:S(2)}) copy-start(f32[1024,1024]{1,0:T(8,128)} %all-gather.2.cloned.1.call-done) | copy-start | bytes 12582916
  154.3 4.7 %copy-start.2 = (bf16[1024,1024]{1,0:T(8,128)(2,1)S(1)}, bf16[1024,1024]{1,0:T(8,128)(2,1)}, u32[]{:S(2)}) copy-start(bf16[1024,1024]{1,0:T(8,128)(2,1)} %all-reduce.2.cloned.1.call-done) | copy-start | bytes 6291460
  (1 other events, 0.7 us)
Sparse Core Ops, SparseCore 0:
  13.2 38.2 all-gather.1
  85.7 68.5 all-reduce.1
  166.1 28.0 reduce-scatter.1

commit v13 on v12

--- a/solution.py
+++ b/solution.py
@@ -149,10 +149,8 @@
     proj_parts = jnp.einsum(
         "mqgr,mqe->gre", feat_cols[:, 0], dzq_all, preferred_element_type=jnp.float32
     ) + jnp.einsum("mqgr,mqe->gre", feat_cols[:, 1], dzc_all, preferred_element_type=jnp.float32)
-    own_proj = jnp.take(proj_parts, group_index, axis=0)
-    sent_proj = jnp.where(own[:, None, None], 0.0, proj_parts).astype(jnp.bfloat16)
-    projection_grad = own_proj + lax.psum_scatter(
-        sent_proj, "group", scatter_dimension=0, tiled=True
+    projection_grad = lax.psum_scatter(
+        proj_parts.astype(jnp.bfloat16), "group", scatter_dimension=0, tiled=True
     ).reshape(rows_dev, emb_width).astype(jnp.float32)
     return (query_grad, code_grad, projection_grad)
 

time: 205 us -> 205 us (level)
  no operation moved by 1% of the time
where the time goes in v13:
time: 205 us; the launch traced here: 202 us
  waiting for transfers between devices  85.8 us (42%)
  matrix products  42.7 us (21%)
  starting transfers between devices  26.6 us (13%)
  other arithmetic  17.8 us (9%)
  local copies, waits for them, and re-layouts  15 us (7%)
  between operations  14 us (7%)
    psum x1, waiting for transfers between devices, body(): code_delta = lax.psum(code_sum, 'member').astype(jnp.float32)  35.2 us
    all_gather x1, waiting for transfers between devices, body(): lax.all_gather(jnp.dot(code_feat, projection, preferred_element_type=jnp....  16.5 us
    ppermute x3, waiting for transfers between devices, exchange(): lax.ppermute(sent, axis, [(i, (i + s) % size) for i in range(size)])  16.4 us
    reduce_scatter x1, waiting for transfers between devices, body(): lax.psum_scatter(proj_parts.astype(jnp.bfloat16), 'group', scatter_dimens...  13.6 us
    ppermute x6, starting transfers between devices, shift_all(): lax.ppermute(x, axis, [(i, (i + s) % size) for i in range(size)])  8.38 us
    dot_general x1, matrix products, body(): jnp.einsum('qe,de->qd', dz_code, projection, preferred_element_type=jnp.f...  7.39 us
    dot_general x1, matrix products, body(): jnp.einsum('qe,de->qd', dz_query, projection, preferred_element_type=jnp....  7.24 us
    all_to_all x1, starting transfers between devices, body(): lax.all_to_all(jnp.broadcast_to(dz_query[None], (members, queries_dev, em...  6.61 us
  transfers between devices with their start and end apart: 15, of which 7 were waited for; matrix products, arithmetic and copies ran while one was open for 30% of the time, Pallas kernels for 0%

profile of v13, /device:TPU:3, one launch (start us, length us, event | category | flops | bytes accessed | tf_op | source)
XLA Modules:
  0.0 201.9 jit_solution(10202763439764130706)
XLA Ops:
  7.2 5.8 %fusion.27 = f32[128,1024]{1,0:T(8,128)} fusion(bf16[128,4096]{1,0:T(8,128)(2,1)} %param.8, bf16[4096,1024]{1,0:T(8,128)(2,1)} %param.9), kind=kOutput, calls=%fused_computation.91 | convolution fusion | flops 1073741824 | bytes 9961472 | tf_op jit(solution)/shard_map/dot_general | solution.py:67
  14.5 2.3 %collective-permute-start.1 = (s32[16]{0:T(128)S(1)}, s32[16]{0:T(128)S(1)}, u32[]{:S(2)}, u32[]{:S(2)}) collective-permute-start(s32[16]{0:T(128)S(1)} %bitcast.127), channel_id=1, source_target_pairs={{0,16},{8,24},{16,0},{24,8},{1,17},{9,25},{17,1},{25,9},{2,18},{10... | collective-permute-start | bytes 200 | tf_op jit(solution)/shard_map/ppermute | solution.py:30
  17.8 4.7 %multiply_reduce_fusion.2 = (f32[128]{0:T(128)S(1)}, f32[128,1024]{1,0:T(8,128)S(1)}) fusion(bf16[128,4096]{1,0:T(8,128)(2,1)S(1)} %copy-done.5, bf16[4096,1024]{1,0:T(8,128)(2,1)} %param.9), kind=kOutput, calls=%fused_computation.30 | convolution fusion | flops 1074003840 | bytes 9961984 | tf_op jit(solution)/shard_map/dot_general | solution.py:14
  23.8 3.6 %all-to-all-start = ((bf16[4,128,1024]{2,1,0:T(8,128)(2,1)}), bf16[4,128,1024]{2,1,0:T(8,128)(2,1)S(1)}, u32[]{:S(2)}, u32[]{:S(2)}) async-start(bf16[4,128,1024]{2,1,0:T(8,128)(2,1)} %broadcast_in_dim.126), calls=%async_computation | async-start | bytes 2097152 | tf_op jit(solution)/shard_map/all_to_all | solution.py:75
  34.9 16.5 %all-gather.2.cloned.1.call-done = f32[1024,1024]{1,0:T(8,128)} async-done(((f32[128,1024]{1,0:T(8,128)}), f32[1024,1024]{1,0:T(8,128)}) %all-gather.2.cloned.1.call-update) | async-done | bytes 4194320 | tf_op jit(solution)/shard_map/all_gather | solution.py:66
  51.5 2.5 %multiply_reduce_fusion = f32[1024]{0:T(1024)S(1)} fusion(f32[1024,1024]{1,0:T(8,128)} %all-gather.2.cloned.1.call-done), kind=kLoop, calls=%fused_computation.11 | loop fusion | flops 2096128 | bytes 4198400 | tf_op jit(solution)/shard_map/reduce_sum | solution.py:72
  54.0 4.7 %all-to-all-start.1 = ((bf16[8,2,128,4,128]{2,4,3,1,0:T(8,128)(2,1)}), bf16[8,2,128,4,128]{2,4,3,1,0:T(8,128)(2,1)}, u32[]{:S(2)}, u32[]{:S(2)}) async-start(bf16[8,2,128,4,128]{2,4,3,1,0:T(8,128)(2,1)} %copy.25), calls=%async_computation.1 | async-start | bytes 4194304 | tf_op jit(solution)/shard_map/all_to_all | solution.py:63
  58.7 3.6 %fusion.25 = (f32[4,128]{1,0:T(4,128)S(1)}, f32[4,128,1024]{2,1,0:T(8,128)S(1)}) fusion(bf16[4,128,1024]{2,1,0:T(8,128)(2,1)S(1)} %all-to-all-done, f32[1024,1024]{1,0:T(8,128)} %all-gather.2.cloned.1.call-done, f32[1024]{0:T(1024)S(1)} %add_rsqrt_fusion, pred[4,1024]{1,0:T(4,128)(4,1)S(1)} %broadcast_in_dim.124), kind=kOutput, calls=%fused_computation.89 | convolution fusion | flops 1077411328 | bytes 7350272 | tf_op jit(solution)/shard_map/gqe,ke->gqk/dot_general | solution.py:92
  68.1 2.6 %collective-permute-done.3 = f32[3,4,128]{2,1,0:T(4,128)S(1)} collective-permute-done((f32[3,4,128]{2,1,0:T(4,128)S(1)}, f32[3,4,128]{2,1,0:T(4,128)S(1)}, u32[]{:S(2)}, u32[]{:S(2)}) %collective-permute-start.3) | collective-permute-done | bytes 6176 | tf_op jit(solution)/shard_map/ppermute | solution.py:30
  75.1 2.4 %add_convert_fusion = bf16[1024,1024]{1,0:T(8,128)(2,1)} fusion(f32[1024,1024]{1,0:T(8,128)S(1)} %fusion.11, f32[1024,1024]{1,0:T(8,128)S(1)} %fusion.12, f32[1024,1024]{1,0:T(8,128)S(1)} %fusion.13, pred[]{:T(512)S(6)} %eq.75, pred[]{:T(512)S(6)} %eq.74, pred[]{:T(512)S(6)} %eq.73, pred[]{:T(512)S(6)} %eq.72, bf16[4,128,1024]{2,1,0:T(8,128)(2,1)S(1)} %all-to-all-done, ...), kind=kOutput, calls=%fused_computation.10 | convolution fusion | flops 285212672 | bytes 15204356 | tf_op jit(solution)/shard_map/dot_general | solution.py:119
  77.5 3.8 %fusion.26 = (bf16[4,128,1024]{2,1,0:T(8,128)(2,1)S(1)}, f32[4,128,1024]{2,1,0:T(8,128)S(1)}) fusion(bf16[4,128,1024]{2,1,0:T(8,128)(2,1)} %copy-done.1, f32[1024,1024]{1,0:T(8,128)} %all-gather.2.cloned.1.call-done, f32[1024]{0:T(1024)S(1)} %add_rsqrt_fusion), kind=kOutput, calls=%fused_computation.90 | convolution fusion | flops 1076363264 | bytes 8392704 | tf_op jit(solution)/shard_map/gqk,ke->gqe/dot_general | solution.py:125
  82.6 3.0 %collective-permute-start.8 = (bf16[128,1024]{1,0:T(8,128)(2,1)}, bf16[128,1024]{1,0:T(8,128)(2,1)S(1)}, u32[]{:S(2)}, u32[]{:S(2)}) collective-permute-start(bf16[128,1024]{1,0:T(8,128)(2,1)} %get-tuple-element.33), channel_id=1, source_target_pairs={{0,24},{8,0},{16,8},{24,16},{1,25},{9,1},{17,9},{25,17},{2,26},{10... | collective-permute-start | bytes 786440 | tf_op jit(solution)/shard_map/ppermute | solution.py:41
  85.6 4.6 %collective-permute-done.6 = bf16[128,1024]{1,0:T(8,128)(2,1)S(1)} collective-permute-done((bf16[128,1024]{1,0:T(8,128)(2,1)}, bf16[128,1024]{1,0:T(8,128)(2,1)S(1)}, u32[]{:S(2)}, u32[]{:S(2)}) %collective-permute-start.6) | collective-permute-done | bytes 262176 | tf_op jit(solution)/shard_map/ppermute | solution.py:41
  90.2 11.8 %collective-permute-done.7 = bf16[128,1024]{1,0:T(8,128)(2,1)S(1)} collective-permute-done((bf16[128,1024]{1,0:T(8,128)(2,1)}, bf16[128,1024]{1,0:T(8,128)(2,1)S(1)}, u32[]{:S(2)}, u32[]{:S(2)}) %collective-permute-start.7) | collective-permute-done | bytes 262176 | tf_op jit(solution)/shard_map/ppermute | solution.py:41
  103.2 2.9 %gather_fusion.2 = bf16[4,128,1024]{2,1,0:T(8,128)(2,1)} fusion(bf16[4,128,1024]{2,1,0:T(8,128)(2,1)} %pad_maximum_fusion, s32[1024]{0:T(1024)S(1)} %pad_clamp_fusion), kind=kCustom, calls=%fused_computation.2 | custom fusion | bytes 2097168 | tf_op jit(solution)/shard_map/jit(_take)/gather | solution.py:43
  109.7 6.6 %all-to-all-start.2 = ((bf16[8,128,1024]{2,1,0:T(8,128)(2,1)}), bf16[8,128,1024]{2,1,0:T(8,128)(2,1)}, u32[]{:S(2)}, u32[]{:S(2)}) async-start(bf16[8,128,1024]{2,1,0:T(8,128)(2,1)} %broadcast_in_dim.135), calls=%async_computation.2 | async-start | bytes 4194304 | tf_op jit(solution)/shard_map/all_to_all | solution.py:141
  116.3 2.8 %fusion.24 = (bf16[8,1,128,4,128]{2,4,3,1,0:T(8,128)(2,1)S(1)}, bf16[8,1,128,4,128]{2,4,3,1,0:T(8,128)(2,1)}) fusion(bf16[8,2,128,4,128]{2,4,3,1,0:T(8,128)(2,1)} %all-to-all-done.1), kind=kLoop, calls=%fused_computation.88 | loop fusion | bytes 4194304 | tf_op jit(solution)/shard_map/slice | solution.py:151
  119.1 35.2 %all-reduce.2.cloned.1.call-done = bf16[1024,1024]{1,0:T(8,128)(2,1)} async-done(((bf16[1024,1024]{1,0:T(8,128)(2,1)}), bf16[1024,1024]{1,0:T(8,128)(2,1)}) %all-reduce.2.cloned.1.call-update) | async-done | bytes 2097168 | tf_op jit(solution)/shard_map/psum | solution.py:124
  154.3 3.7 %fusion = f32[1024]{0:T(1024)S(1)} fusion(bf16[1024,1024]{1,0:T(8,128)(2,1)} %all-reduce.2.cloned.1.call-done, f32[1024,1024]{1,0:T(8,128)} %all-gather.2.cloned.1.call-done, f32[1024]{0:T(1024)S(1)} %add_rsqrt_fusion), kind=kLoop, calls=%fused_computation.7 | loop fusion | flops 4193280 | bytes 6299648 | tf_op jit(solution)/shard_map/reduce_sum | solution.py:21
  159.9 3.2 %fusion.5 = f32[4,128,1024,1]{2,1,3,0:T(8,128)S(1)} fusion(bf16[8,128,1024]{2,1,0:T(8,128)(2,1)} %all-to-all-done.2, bf16[8,1,128,4,128]{2,4,3,1,0:T(8,128)(2,1)} %get-tuple-element.31), kind=kOutput, calls=%fused_computation.17 | convolution fusion | flops 1073741824 | bytes 5242880 | tf_op jit(solution)/shard_map/mqgr,mqe->gre/dot_general | solution.py:149
  163.0 2.2 %fusion.4 = bf16[4,128,1024]{2,1,0:T(8,128)(2,1)} fusion(f32[4,128,1024,1]{2,1,3,0:T(8,128)S(1)} %fusion.5, bf16[8,128,1024,1]{2,1,0,3:T(8,128)(2,1)S(1)} %bitcast.116, bf16[8,1,128,4,128]{2,4,3,1,0:T(8,128)(2,1)S(1)} %get-tuple-element.30), kind=kOutput, calls=%fused_computation.16 | convolution fusion | flops 1074790400 | bytes 6291456 | tf_op jit(solution)/shard_map/mqgr,mqe->gre/dot_general | solution.py:151
  165.3 7.2 %convolution_convert_fusion.1 = bf16[128,4096]{1,0:T(8,128)(2,1)} fusion(bf16[128,1024]{1,0:T(8,128)(2,1)S(1)} %multiply_convert_fusion.2, bf16[4096,1024]{1,0:T(8,128)(2,1)} %param.9), kind=kOutput, calls=%fused_computation.6 | convolution fusion | flops 1074266112 | bytes 9699328 | tf_op jit(solution)/shard_map/qe,de->qd/dot_general | solution.py:134
  172.5 7.4 %convolution_convert_fusion = bf16[128,4096]{1,0:T(8,128)(2,1)} fusion(bf16[4096,1024]{1,0:T(8,128)(2,1)} %param.9, bf16[1024,1024]{1,0:T(8,128)(2,1)S(1)} %fusion.2, s32[]{:T(128)S(6)} %select_n.154), kind=kOutput, calls=%fused_computation.5 | convolution fusion | flops 1074266112 | bytes 9699332 | tf_op jit(solution)/shard_map/qe,de->qd/dot_general | solution.py:137
  179.9 13.6 %reduce-scatter.2.cloned.1.call-done = bf16[1,128,1024]{2,1,0:T(8,128)(2,1)} async-done(((bf16[4,128,1024]{2,1,0:T(8,128)(2,1)}), bf16[1,128,1024]{2,1,0:T(8,128)(2,1)}) %reduce-scatter.2.cloned.1.call-update) | async-done | bytes 262160 | tf_op jit(solution)/shard_map/reduce_scatter | solution.py:152
  (87 shorter events, 30.9 us)
Async XLA Ops:
  7.2 5.9 %copy-start.9 = (s32[1,16]{1,0:T(1,128)S(1)}, s32[1,16]{1,0:T(1,128)}, u32[]{:S(2)}) copy-start(s32[1,16]{1,0:T(1,128)} %param.10) | copy-start | bytes 196
  7.2 10.7 %copy-start.5 = (bf16[128,4096]{1,0:T(8,128)(2,1)S(1)}, bf16[128,4096]{1,0:T(8,128)(2,1)}, u32[]{:S(2)}) copy-start(bf16[128,4096]{1,0:T(8,128)(2,1)} %param.7) | copy-start | bytes 3145732
  7.2 44.3 %all-gather.2.cloned.1.call-start = ((), (), s32[]{:S(2)}) async-start(), calls=%async_computation.4 | async-start | bytes 4718592 | tf_op jit(solution)/shard_map/all_gather | solution.py:66
  13.1 20.8 %collective-permute-start = (s32[16]{0:T(128)S(1)}, s32[16]{0:T(128)S(1)}, u32[]{:S(2)}, u32[]{:S(2)}) collective-permute-start(s32[16]{0:T(128)S(1)} %bitcast.126), channel_id=1, source_target_pairs={{0,8},{8,16},{16,24},{24,0},{1,9},{9,17},{17,25},{25,1},{2,10},{10... | collective-permute-start | bytes 200 | tf_op jit(solution)/shard_map/ppermute | solution.py:30
  14.5 19.5 %collective-permute-start.1 = (s32[16]{0:T(128)S(1)}, s32[16]{0:T(128)S(1)}, u32[]{:S(2)}, u32[]{:S(2)}) collective-permute-start(s32[16]{0:T(128)S(1)} %bitcast.127), channel_id=1, source_target_pairs={{0,16},{8,24},{16,0},{24,8},{1,17},{9,25},{17,1},{25,9},{2,18},{10... | collective-permute-start | bytes 200 | tf_op jit(solution)/shard_map/ppermute | solution.py:30
  16.8 17.2 %collective-permute-start.2 = (s32[16]{0:T(128)S(1)}, s32[16]{0:T(128)S(1)}, u32[]{:S(2)}, u32[]{:S(2)}) collective-permute-start(s32[16]{0:T(128)S(1)} %bitcast.128), channel_id=1, source_target_pairs={{0,24},{8,0},{16,8},{24,16},{1,25},{9,1},{17,9},{25,17},{2,26},{10... | collective-permute-start | bytes 200 | tf_op jit(solution)/shard_map/ppermute | solution.py:30
  22.6 1.2 copy-start.3
  23.8 5.1 %copy-start.6 = (bf16[128,4096]{1,0:T(8,128)(2,1)S(1)}, bf16[128,4096]{1,0:T(8,128)(2,1)}, u32[]{:S(2)}) copy-start(bf16[128,4096]{1,0:T(8,128)(2,1)} %param.8) | copy-start | bytes 3145732
  23.8 30.2 %all-to-all-start = ((bf16[4,128,1024]{2,1,0:T(8,128)(2,1)}), bf16[4,128,1024]{2,1,0:T(8,128)(2,1)S(1)}, u32[]{:S(2)}, u32[]{:S(2)}) async-start(bf16[4,128,1024]{2,1,0:T(8,128)(2,1)} %broadcast_in_dim.126), calls=%async_computation | async-start | bytes 2097152 | tf_op jit(solution)/shard_map/all_to_all | solution.py:75
  28.9 1.3 copy-start.7
  54.0 54.0 %all-to-all-start.1 = ((bf16[8,2,128,4,128]{2,4,3,1,0:T(8,128)(2,1)}), bf16[8,2,128,4,128]{2,4,3,1,0:T(8,128)(2,1)}, u32[]{:S(2)}, u32[]{:S(2)}) async-start(bf16[8,2,128,4,128]{2,4,3,1,0:T(8,128)(2,1)} %copy.25), calls=%async_computation.1 | async-start | bytes 4194304 | tf_op jit(solution)/shard_map/all_to_all | solution.py:63
  58.7 95.6 %all-reduce.2.cloned.1.call-start = ((), (), s32[]{:S(2)}) async-start(), calls=%async_computation.5 | async-start | bytes 4194304 | tf_op jit(solution)/shard_map/psum | solution.py:124
  63.0 3.7 %collective-permute-start.4 = (f32[3,4,128]{2,1,0:T(4,128)S(1)}, f32[3,4,128]{2,1,0:T(4,128)S(1)}, u32[]{:S(2)}, u32[]{:S(2)}) collective-permute-start(f32[3,4,128]{2,1,0:T(4,128)S(1)} %get-tuple-element.37), channel_id=1, source_target_pairs={{0,16},{8,24},{16,0},{24,8},{1,17},{9,25},{17,1},{25,9},{2,18},{10... | collective-permute-start | bytes 18440 | tf_op jit(solution)/shard_map/ppermute | solution.py:30
  65.2 2.9 %collective-permute-start.5 = (f32[3,4,128]{2,1,0:T(4,128)S(1)}, f32[3,4,128]{2,1,0:T(4,128)S(1)}, u32[]{:S(2)}, u32[]{:S(2)}) collective-permute-start(f32[3,4,128]{2,1,0:T(4,128)S(1)} %get-tuple-element.37), channel_id=1, source_target_pairs={{0,24},{8,0},{16,8},{24,16},{1,25},{9,1},{17,9},{25,17},{2,26},{10... | collective-permute-start | bytes 18440 | tf_op jit(solution)/shard_map/ppermute | solution.py:30
  66.4 4.3 %collective-permute-start.3 = (f32[3,4,128]{2,1,0:T(4,128)S(1)}, f32[3,4,128]{2,1,0:T(4,128)S(1)}, u32[]{:S(2)}, u32[]{:S(2)}) collective-permute-start(f32[3,4,128]{2,1,0:T(4,128)S(1)} %get-tuple-element.37), channel_id=1, source_target_pairs={{0,8},{8,16},{16,24},{24,0},{1,9},{9,17},{17,25},{25,1},{2,10},{10... | collective-permute-start | bytes 18440 | tf_op jit(solution)/shard_map/ppermute | solution.py:30
  72.9 2.2 %copy-start.1 = (bf16[4,128,1024]{2,1,0:T(8,128)(2,1)}, bf16[4,128,1024]{2,1,0:T(8,128)(2,1)S(1)}, u32[]{:S(2)}) copy-start(bf16[4,128,1024]{2,1,0:T(8,128)(2,1)S(1)} %multiply_convert_fusion.1) | copy-start | bytes 3145732
  82.3 7.9 %collective-permute-start.6 = (bf16[128,1024]{1,0:T(8,128)(2,1)}, bf16[128,1024]{1,0:T(8,128)(2,1)S(1)}, u32[]{:S(2)}, u32[]{:S(2)}) collective-permute-start(bf16[128,1024]{1,0:T(8,128)(2,1)} %get-tuple-element.35), channel_id=1, source_target_pairs={{0,8},{8,16},{16,24},{24,0},{1,9},{9,17},{17,25},{25,1},{2,10},{10... | collective-permute-start | bytes 786440 | tf_op jit(solution)/shard_map/ppermute | solution.py:41
  82.3 19.7 %collective-permute-start.7 = (bf16[128,1024]{1,0:T(8,128)(2,1)}, bf16[128,1024]{1,0:T(8,128)(2,1)S(1)}, u32[]{:S(2)}, u32[]{:S(2)}) collective-permute-start(bf16[128,1024]{1,0:T(8,128)(2,1)} %get-tuple-element.34), channel_id=1, source_target_pairs={{0,16},{8,24},{16,0},{24,8},{1,17},{9,25},{17,1},{25,9},{2,18},{10... | collective-permute-start | bytes 786440 | tf_op jit(solution)/shard_map/ppermute | solution.py:41
  82.6 19.4 %collective-permute-start.8 = (bf16[128,1024]{1,0:T(8,128)(2,1)}, bf16[128,1024]{1,0:T(8,128)(2,1)S(1)}, u32[]{:S(2)}, u32[]{:S(2)}) collective-permute-start(bf16[128,1024]{1,0:T(8,128)(2,1)} %get-tuple-element.33), channel_id=1, source_target_pairs={{0,24},{8,0},{16,8},{24,16},{1,25},{9,1},{17,9},{25,17},{2,26},{10... | collective-permute-start | bytes 786440 | tf_op jit(solution)/shard_map/ppermute | solution.py:41
  103.2 4.5 %copy-start.4 = (f32[128,1024]{1,0:T(8,128)S(1)}, f32[128,1024]{1,0:T(8,128)}, u32[]{:S(2)}) copy-start(f32[128,1024]{1,0:T(8,128)} %copy-done.3) | copy-start | bytes 1572868
  109.7 50.2 %all-to-all-start.2 = ((bf16[8,128,1024]{2,1,0:T(8,128)(2,1)}), bf16[8,128,1024]{2,1,0:T(8,128)(2,1)}, u32[]{:S(2)}, u32[]{:S(2)}) async-start(bf16[8,128,1024]{2,1,0:T(8,128)(2,1)} %broadcast_in_dim.135), calls=%async_computation.2 | async-start | bytes 4194304 | tf_op jit(solution)/shard_map/all_to_all | solution.py:141
  116.3 77.3 %reduce-scatter.2.cloned.1.call-start = ((), (), s32[]{:S(2)}) async-start(), calls=%async_computation.6 | async-start | bytes 1310720 | tf_op jit(solution)/shard_map/reduce_scatter | solution.py:152
  154.3 4.0 %copy-start = (f32[1024,1024]{1,0:T(8,128)S(1)}, f32[1024,1024]{1,0:T(8,128)}, u32[]{:S(2)}) copy-start(f32[1024,1024]{1,0:T(8,128)} %all-gather.2.cloned.1.call-done) | copy-start | bytes 12582916
  154.3 4.7 %copy-start.2 = (bf16[1024,1024]{1,0:T(8,128)(2,1)S(1)}, bf16[1024,1024]{1,0:T(8,128)(2,1)}, u32[]{:S(2)}) copy-start(bf16[1024,1024]{1,0:T(8,128)(2,1)} %all-reduce.2.cloned.1.call-done) | copy-start | bytes 6291460
  (1 other events, 0.7 us)
Sparse Core Ops, SparseCore 0:
  13.2 38.2 all-gather.1
  85.7 68.5 all-reduce.1
  165.4 28.0 reduce-scatter.1
